TPU v7x, 512 devices: a whole 4x4x16 slice. The times are simulated.
512 devices in a mesh: seq: 32 (over y, z_hi, core), chan: 16 (over x, z_lo).
Axes of the slice: x: 4, y: 4, z: 16 (z_hi: 4, z_lo: 4; z = z_hi * 4 + z_lo), core: 2. Of those that a mesh axis runs over, the one named last changes fastest.
Arguments:
- streams: bfloat16 [5, 8192, 8192], P(None, 'seq', 'chan'), may hold values from -6 to 6
- short_filter: bfloat16 [7, 8192], P(None, 'chan'), may hold values from -2 to 2
- long_filter: bfloat16 [128, 8192], P(None, 'chan'), may hold values from -0.5 to 0.5
- edit_table: bfloat16 [64, 8, 8192], P('seq', None, 'chan'), may hold values from -0.25 to 0.25
- edit_bias: float32 [64, 4], replicated, may hold values from -8 to 8
- seq_tiles: int32 [4], replicated, may hold values from 1 to 32, 64 in all
- seq_tenant: int32 [4], replicated, may hold values from 0 to 63
Outputs:
- edited: bfloat16 [8192, 8192], P('seq', 'chan')
Inputs may be any that keep to these rules, and one draw needn't show every extreme that they name: `seq_tiles`: each sequence fills whole tiles; the sequences fill all 64 tiles in order and the longest has 32.
All inputs are finite; a program needn't handle non-finite values.
Results may differ from a plain program's by a relative error of at most 0.013.
Values may be sent and summed in bfloat16 or wider, within the bound.
No kernel may reach another device: no remote copies, remote signals or barrier semaphores. Data moves between devices by JAX's collectives and lax.ppermute only.
A program may use at most 64 MiB of HBM per device.

v0:
```python
import jax
import jax.numpy as jnp
from jax import lax
from jax.sharding import PartitionSpec as P

TILE_ROWS = 128
SEQS = 4


def from_behind(block, axis, distance):
    devices = range(lax.axis_size(axis))
    route = [(i - distance, i) for i in devices if i - distance in devices]
    return lax.ppermute(block, axis, route)


def depth_conv(window, taps_filter):
    width = window.shape[-1]
    kernel = taps_filter[::-1][:, None, :]
    return lax.conv_general_dilated(
        window,
        kernel,
        (1,),
        "VALID",
        dimension_numbers=("NWC", "WIO", "NWC"),
        feature_group_count=width,
        preferred_element_type=jnp.float32,
    )


def tiled_conv(field, border, starts, taps_filter):
    rows_here, width = field.shape
    reach = taps_filter.shape[0]
    tile_count = rows_here // TILE_ROWS
    tiles = field.reshape(tile_count, TILE_ROWS, width)
    trailing = tiles[:, TILE_ROWS - (reach - 1) :, :]
    earlier = jnp.concatenate([border[None], trailing[:-1]], axis=0)
    earlier = jnp.where(starts[:, None, None], jnp.zeros_like(earlier), earlier)
    window = jnp.concatenate([earlier, tiles], axis=1)
    return depth_conv(window, taps_filter).reshape(rows_here, width)


def on_device(streams, short_filter, long_filter, edit_table, edit_bias, seq_tiles, seq_tenant):
    rows_here = streams.shape[1]
    width = streams.shape[2]
    short_reach = short_filter.shape[0]
    long_reach = long_filter.shape[0]
    tile_count = rows_here // TILE_ROWS
    seq_ends = jnp.cumsum(seq_tiles)
    first_tile = lax.axis_index("seq") * tile_count
    tile_ids = first_tile + jnp.arange(tile_count, dtype=jnp.int32)
    seq_of = jnp.sum((seq_ends[None, :] <= tile_ids[:, None]).astype(jnp.int32), axis=1)
    starts = (tile_ids == 0) | jnp.any(seq_ends[None, :] == tile_ids[:, None], axis=1)
    first_gate = streams[0]
    first_key = streams[1]
    second_gate = streams[3]
    second_key = streams[4]
    gated = (first_key.astype(jnp.float32) * streams[2].astype(jnp.float32)).astype(jnp.bfloat16)
    short_border = from_behind(gated[rows_here - (short_reach - 1) :], "seq", 1)
    short_out = tiled_conv(gated, short_border, starts, short_filter)
    mixed = (first_gate.astype(jnp.float32) * short_out).astype(jnp.bfloat16)
    carried = (second_key.astype(jnp.float32) * mixed.astype(jnp.float32)).astype(jnp.bfloat16)
    long_border = from_behind(carried[rows_here - (long_reach - 1) :], "seq", 1)
    long_out = tiled_conv(carried, long_border, starts, long_filter)
    hidden = (second_gate.astype(jnp.float32) * long_out).astype(jnp.bfloat16)
    rows_per = edit_table.shape[1]
    rank = rows_per // 2
    all_rows = lax.all_gather(edit_table, "seq", axis=0, tiled=True)
    tenant_count = all_rows.shape[0]
    picker = (seq_tenant[:, None] == jnp.arange(tenant_count, dtype=jnp.int32)[None, :]).astype(
        jnp.bfloat16
    )
    chosen = jnp.dot(
        picker, all_rows.reshape(tenant_count, rows_per * width), preferred_element_type=jnp.float32
    )
    chosen = chosen.astype(jnp.bfloat16).reshape(SEQS, rows_per, width)
    tok_seq = jnp.repeat(seq_of, TILE_ROWS)
    seq_onehot = (tok_seq[:, None] == jnp.arange(SEQS, dtype=jnp.int32)[None, :]).astype(
        jnp.float32
    )
    projected = jnp.dot(
        hidden, chosen.reshape(SEQS * rows_per, width).T, preferred_element_type=jnp.float32
    )
    projected = projected.reshape(rows_here, SEQS, rows_per)
    selected = jnp.sum(projected * seq_onehot[:, :, None], axis=1)
    summed = lax.psum(selected, "chan")
    tenant_total = edit_bias.shape[0]
    bias_pick = (seq_tenant[:, None] == jnp.arange(tenant_total, dtype=jnp.int32)[None, :]).astype(
        jnp.float32
    )
    bias_seq = jnp.dot(bias_pick, edit_bias, precision=lax.Precision.HIGHEST)
    bias_tok = jnp.dot(seq_onehot, bias_seq, precision=lax.Precision.HIGHEST)
    coefficient = summed[:, rank:] - summed[:, :rank] + bias_tok
    spread = (seq_onehot[:, :, None] * coefficient[:, None, :]).reshape(rows_here, SEQS * rank)
    rows_r = chosen[:, :rank, :].reshape(SEQS * rank, width).astype(jnp.float32)
    change = jnp.dot(spread, rows_r, precision=lax.Precision.HIGHEST)
    return (hidden.astype(jnp.float32) + change).astype(jnp.bfloat16)


def solution(mesh):
    in_specs = (
        P(None, "seq", "chan"),
        P(None, "chan"),
        P(None, "chan"),
        P("seq", None, "chan"),
        P(),
        P(),
        P(),
    )
    out_specs = P("seq", "chan")
    return jax.shard_map(
        on_device, mesh=mesh, in_specs=in_specs, out_specs=out_specs, check_vma=False
    )
```

profile of v0, /device:TPU:8, one launch (start us, length us, event | category | flops | bytes accessed | tf_op | source)
XLA Modules:
  0.0 135.5 jit_solution(4230756904072077659)
XLA Ops:
  0.0 1.1 multiply_convert_fusion.3
  1.1 1.9 %collective-permute-start = (bf16[6,512]{1,0:T(8,128)(2,1)S(1)}, bf16[6,512]{1,0:T(8,128)(2,1)S(1)}, u32[]{:S(2)}, u32[]{:S(2)}) collective-permute-start(bf16[6,512]{1,0:T(8,128)(2,1)S(1)} %slice_bitcast_fusion), channel_id=1, source_target_pairs={{0,16},{16,32},{32,48},{48,64},{64,80},{80,96},{96,112},{112,128},... | collective-permute-start | bytes 18440 | tf_op jit(solution)/shard_map/ppermute | solution.py:13
  3.1 2.2 %slice_convert_fusion.2 = (f32[1,256,512]{2,1,0:T(8,128)S(1)}, f32[256,512]{1,0:T(8,128)S(1)}, f32[256,512]{1,0:T(8,128)}, f32[1,256,512]{2,1,0:T(8,128)S(1)}, f32[1,256,512]{2,1,0:T(8,128)S(1)}) fusion(bf16[5,256,512]{2,1,0:T(8,128)(2,1)} %param.7), kind=kLoop, calls=%fused_computation.30 | loop fusion | flops 393216 | bytes 3407872 | tf_op jit(solution)/shard_map/convert_element_type | solution.py:64
  5.3 0.2 reduce-window.8
  5.5 0.2 compare_reduce_fusion
  5.7 0.2 fusion.22
  6.0 56.8 %all_gather.3 = bf16[64,8,512]{2,1,0:T(8,128)(2,1)S(1)} all-gather(bf16[2,8,512]{2,1,0:T(8,128)(2,1)S(1)} %copy-done.4), channel_id=1, replica_groups=mesh['seq'=32,'chan'=16] {'seq'}, dimensions={0}, use_global_device_ids=true | all-gather | bytes 540672 | tf_op jit(solution)/shard_map/all_gather | solution.py:67
  62.9 0.2 convolution_convert_fusion
  63.3 1.3 rev.7
  64.8 0.2 copy.72
  65.1 0.2 pad.clone
  65.4 0.3 fusion.6
  65.7 0.3 convolution_select_fusion
  66.0 0.3 copy.67
  66.6 0.9 copy-done.1
  67.6 2.3 %collective-permute-start.1 = (bf16[127,512]{1,0:T(8,128)(2,1)S(1)}, bf16[127,512]{1,0:T(8,128)(2,1)S(1)}, u32[]{:S(2)}, u32[]{:S(2)}) collective-permute-start(bf16[127,512]{1,0:T(8,128)(2,1)S(1)} %fusion.9), channel_id=1, source_target_pairs={{0,16},{16,32},{32,48},{48,64},{64,80},{80,96},{96,112},{112,128},... | collective-permute-start | bytes 390152 | tf_op jit(solution)/shard_map/ppermute | solution.py:13
  69.9 0.2 fusion.20
  70.1 10.8 %collective-permute-done.1 = bf16[127,512]{1,0:T(8,128)(2,1)S(1)} collective-permute-done((bf16[127,512]{1,0:T(8,128)(2,1)S(1)}, bf16[127,512]{1,0:T(8,128)(2,1)S(1)}, u32[]{:S(2)}, u32[]{:S(2)}) %collective-permute-start.1) | collective-permute-done | bytes 130080 | tf_op jit(solution)/shard_map/ppermute | solution.py:13
  81.1 6.7 %fusion.4 = f32[2,128,512]{2,0,1:T(2,128)S(1)} fusion(bf16[2,255,512]{2,1,0:T(8,128)(2,1)S(1)} %pad_maximum_fusion, bf16[128,1,512]{2,0,1:T(8,128)(2,1)S(1)} %bitcast.63), kind=kOutput, calls=%fused_computation.16 | convolution fusion | flops 33554432 | bytes 1177600 | tf_op jit(solution)/shard_map/conv_general_dilated | solution.py:19
  88.0 0.2 fusion.2
  88.2 45.0 %psum.7 = f32[256,8]{0,1:T(8,128)S(1)} all-reduce(f32[256,8]{0,1:T(8,128)S(1)} %fusion.2), channel_id=1, replica_groups=mesh['seq'=32,'chan'=16] {'chan'}, use_global_device_ids=true, to_apply=%region_4.5 | all-reduce | flops 2048 | bytes 16384 | tf_op jit(solution)/shard_map/psum | solution.py:85
  133.1 1.0 fusion.3
  134.1 0.2 convolution_add_fusion
  134.3 1.2 fusion.1
  (37 shorter events, 1.4 us)
Async XLA Ops:
  0.0 69.9 %copy-start = (f32[64,4]{0,1:T(4,128)S(1)}, f32[64,4]{0,1:T(4,128)}, u32[]{:S(2)}) copy-start(f32[64,4]{0,1:T(4,128)} %param.11) | copy-start | bytes 3076
  1.1 63.6 %collective-permute-start = (bf16[6,512]{1,0:T(8,128)(2,1)S(1)}, bf16[6,512]{1,0:T(8,128)(2,1)S(1)}, u32[]{:S(2)}, u32[]{:S(2)}) collective-permute-start(bf16[6,512]{1,0:T(8,128)(2,1)S(1)} %slice_bitcast_fusion), channel_id=1, source_target_pairs={{0,16},{16,32},{32,48},{48,64},{64,80},{80,96},{96,112},{112,128},... | collective-permute-start | bytes 18440 | tf_op jit(solution)/shard_map/ppermute | solution.py:13
  3.1 2.3 %copy-start.7 = (s32[4]{0:T(128)S(1)}, s32[4]{0:T(128)}, u32[]{:S(2)}) copy-start(s32[4]{0:T(128)} %param.12) | copy-start | bytes 52
  3.1 2.9 %copy-start.4 = (bf16[2,8,512]{2,1,0:T(8,128)(2,1)S(1)}, bf16[2,8,512]{2,1,0:T(8,128)(2,1)}, u32[]{:S(2)}) copy-start(bf16[2,8,512]{2,1,0:T(8,128)(2,1)} %param.10) | copy-start | bytes 49156
  5.3 57.6 %copy-start.6 = (s32[4]{0:T(128)S(1)}, s32[4]{0:T(128)}, u32[]{:S(2)}) copy-start(s32[4]{0:T(128)} %param.13) | copy-start | bytes 52
  5.3 57.9 %copy-start.5 = (bf16[7,512]{1,0:T(8,128)(2,1)S(1)}, bf16[7,512]{1,0:T(8,128)(2,1)}, u32[]{:S(2)}) copy-start(bf16[7,512]{1,0:T(8,128)(2,1)} %param.8) | copy-start | bytes 21508
  5.3 58.0 %copy-start.2 = (bf16[128,512]{1,0:T(8,128)(2,1)S(1)}, bf16[128,512]{1,0:T(8,128)(2,1)}, u32[]{:S(2)}) copy-start(bf16[128,512]{1,0:T(8,128)(2,1)} %param.9) | copy-start | bytes 393220
  64.7 1.0 copy-start.8
  66.5 1.0 copy-start.1
  67.5 13.6 %copy-start.3 = (bf16[128,512]{1,0:T(8,128)(2,1)S(1)}, bf16[128,512]{1,0:T(8,128)(2,1)}, u32[]{:S(2)}) copy-start(bf16[128,512]{1,0:T(8,128)(2,1)} %rev.7) | copy-start | bytes 393220
  67.6 13.3 %collective-permute-start.1 = (bf16[127,512]{1,0:T(8,128)(2,1)S(1)}, bf16[127,512]{1,0:T(8,128)(2,1)S(1)}, u32[]{:S(2)}, u32[]{:S(2)}) collective-permute-start(bf16[127,512]{1,0:T(8,128)(2,1)S(1)} %fusion.9), channel_id=1, source_target_pairs={{0,16},{16,32},{32,48},{48,64},{64,80},{80,96},{96,112},{112,128},... | collective-permute-start | bytes 390152 | tf_op jit(solution)/shard_map/ppermute | solution.py:13
where the time goes:
time: 136 us
  blocking collectives  102 us (75%)
  waiting for transfers between devices  10.8 us (8%)
  matrix products  9 us (7%)
  other arithmetic  5.95 us (4%)
  starting transfers between devices  4.17 us (3%)
  local copies, waits for them, and re-layouts  3.59 us (3%)
    all_gather x1, blocking collectives, on_device(): all_rows = lax.all_gather(edit_table, 'seq', axis=0, tiled=True)  56.8 us
    psum x1, blocking collectives, on_device(): summed = lax.psum(selected, 'chan')  45 us
    ppermute x2, waiting for transfers between devices, from_behind(): return lax.ppermute(block, axis, route)  10.8 us
    conv_general_dilated x2, matrix products, depth_conv(): lax.conv_general_dilated(window, kernel, (1,), 'VALID', dimension_numbers...  7.03 us
    ppermute x2, starting transfers between devices, from_behind(): return lax.ppermute(block, axis, route)  4.17 us
    convert_element_type x3, other arithmetic, on_device(): hidden = (second_gate.astype(jnp.float32) * long_out).astype(jnp.bfloat16)  3.39 us
  transfers between devices with their start and end apart: 2, of which 1 were waited for; matrix products, arithmetic and copies ran while one was open for 4% of the time, Pallas kernels for 0%

commit v1 on v0

v1 whole, which is shorter than its diff:
```python
import jax
import jax.numpy as jnp
from jax import lax
from jax.sharding import PartitionSpec as P

TILE_ROWS = 128
SEQS = 4


def from_behind(block, axis, distance):
    devices = range(lax.axis_size(axis))
    route = [(i - distance, i) for i in devices if i - distance in devices]
    return lax.ppermute(block, axis, route)


def xor_sum(block, axis):
    size = lax.axis_size(axis)
    step = 1
    while step < size:
        route = [(i, i ^ step) for i in range(size)]
        block = block + lax.ppermute(block, axis, route)
        step *= 2
    return block


def a2a_sum(block, axis):
    size = lax.axis_size(axis)
    copies = jnp.broadcast_to(block[None], (size,) + block.shape)
    return jnp.sum(lax.all_to_all(copies, axis, 0, 0, tiled=False), axis=0)


def depth_conv(window, taps_filter):
    width = window.shape[-1]
    kernel = taps_filter[::-1][:, None, :]
    return lax.conv_general_dilated(
        window,
        kernel,
        (1,),
        "VALID",
        dimension_numbers=("NWC", "WIO", "NWC"),
        feature_group_count=width,
        preferred_element_type=jnp.float32,
    )


def on_device(streams, short_filter, long_filter, edit_table, edit_bias, seq_tiles, seq_tenant):
    rows_here = streams.shape[1]
    width = streams.shape[2]
    short_reach = short_filter.shape[0]
    long_reach = long_filter.shape[0]
    tile_count = rows_here // TILE_ROWS
    me = lax.axis_index("seq")
    seq_ends = jnp.cumsum(seq_tiles)
    tile_ids = me * tile_count + jnp.arange(tile_count, dtype=jnp.int32)
    seq_of = jnp.sum((seq_ends[None, :] <= tile_ids[:, None]).astype(jnp.int32), axis=1)
    starts = (tile_ids == 0) | jnp.any(seq_ends[None, :] == tile_ids[:, None], axis=1)

    held = edit_table.shape[0]
    owner_slot = seq_tenant - me * held
    owned = (owner_slot >= 0) & (owner_slot < held)
    local_rows = jnp.take(edit_table, jnp.clip(owner_slot, 0, held - 1), axis=0)
    local_rows = jnp.where(owned[:, None, None], local_rows, jnp.zeros_like(local_rows))
    chosen = xor_sum(local_rows, "seq")

    first_gate = streams[0].astype(jnp.float32)
    second_gate = streams[3].astype(jnp.float32)
    second_key = streams[4].astype(jnp.float32)
    gated = (streams[1].astype(jnp.float32) * streams[2].astype(jnp.float32)).astype(jnp.bfloat16)
    g_tiles = gated.reshape(tile_count, TILE_ROWS, width)

    def short_window(tile, earlier):
        earlier = jnp.where(starts[tile], jnp.zeros_like(earlier), earlier)
        return jnp.concatenate([earlier, g_tiles[tile]], axis=0)

    def carried_of(tile, short_out):
        rows = slice(tile * TILE_ROWS, (tile + 1) * TILE_ROWS)
        mixed = (first_gate[rows] * short_out).astype(jnp.bfloat16)
        return (second_key[rows] * mixed.astype(jnp.float32)).astype(jnp.bfloat16)

    later = [
        short_window(tile, g_tiles[tile - 1, TILE_ROWS - (short_reach - 1) :])
        for tile in range(1, tile_count)
    ]
    later_out = depth_conv(jnp.stack(later), short_filter)
    carried_later = [carried_of(tile, later_out[tile - 1]) for tile in range(1, tile_count)]

    border = jnp.concatenate(
        [gated[rows_here - (short_reach - 1) :], carried_later[-1][TILE_ROWS - (long_reach - 1) :]],
        axis=0,
    )
    border = from_behind(border, "seq", 1)
    short_border = border[: short_reach - 1]
    long_border = border[short_reach - 1 :]

    first_out = depth_conv(short_window(0, short_border)[None], short_filter)[0]
    carried = [carried_of(0, first_out)] + carried_later

    long_windows = []
    for tile in range(tile_count):
        earlier = long_border if tile == 0 else carried[tile - 1][TILE_ROWS - (long_reach - 1) :]
        earlier = jnp.where(starts[tile], jnp.zeros_like(earlier), earlier)
        long_windows.append(jnp.concatenate([earlier, carried[tile]], axis=0))
    long_out = depth_conv(jnp.stack(long_windows), long_filter)
    hidden = (second_gate.reshape(tile_count, TILE_ROWS, width) * long_out).astype(jnp.bfloat16)

    rows_per = edit_table.shape[1]
    rank = rows_per // 2
    tile_rows = jnp.take(chosen, seq_of, axis=0)
    projected = jnp.einsum(
        "tnc,trc->tnr", hidden, tile_rows, preferred_element_type=jnp.float32
    )
    partial = projected[..., rank:] - projected[..., :rank]
    summed = a2a_sum(partial, "chan")
    bias_tile = jnp.take(jnp.take(edit_bias, seq_tenant, axis=0), seq_of, axis=0)
    coefficient = summed + bias_tile[:, None, :]
    rows_r = tile_rows[:, :rank, :].astype(jnp.float32)
    total = hidden.astype(jnp.float32)
    for r in range(rank):
        total = total + coefficient[:, :, r : r + 1] * rows_r[:, r : r + 1, :]
    return total.astype(jnp.bfloat16).reshape(rows_here, width)


def solution(mesh):
    in_specs = (
        P(None, "seq", "chan"),
        P(None, "chan"),
        P(None, "chan"),
        P("seq", None, "chan"),
        P(),
        P(),
        P(),
    )
    out_specs = P("seq", "chan")
    return jax.shard_map(
        on_device, mesh=mesh, in_specs=in_specs, out_specs=out_specs, check_vma=False
    )
```

time: 136 us -> 83.6 us (0.61)
  the two profiles are of different devices: /device:TPU:8 before, /device:TPU:128 now
where the time goes in v1:
time: 83.6 us; the launch traced here: 83.3 us
  starting transfers between devices  35 us (42%)
  waiting for transfers between devices  26.8 us (32%)
  matrix products  8.02 us (10%)
  other arithmetic  7.35 us (9%)
  local copies, waits for them, and re-layouts  5.57 us (7%)
    ppermute x5, starting transfers between devices, xor_sum(): block = block + lax.ppermute(block, axis, route)  24.8 us
    ppermute x5, waiting for transfers between devices, xor_sum(): block = block + lax.ppermute(block, axis, route)  18.7 us
    all_to_all x1, starting transfers between devices, a2a_sum(): return jnp.sum(lax.all_to_all(copies, axis, 0, 0, tiled=False), axis=0)  8.24 us
    all_to_all x1, waiting for transfers between devices, a2a_sum(): return jnp.sum(lax.all_to_all(copies, axis, 0, 0, tiled=False), axis=0)  8.09 us
    conv_general_dilated x3, matrix products, depth_conv(): lax.conv_general_dilated(window, kernel, (1,), 'VALID', dimension_numbers...  7.82 us
    ppermute x1, starting transfers between devices, from_behind(): return lax.ppermute(block, axis, route)  1.92 us
  transfers between devices with their start and end apart: 7, of which 4 were waited for; matrix products, arithmetic and copies ran while one was open for 16% of the time, Pallas kernels for 0%

profile of v1, /device:TPU:128, one launch (start us, length us, event | category | flops | bytes accessed | tf_op | source)
XLA Modules:
  0.0 83.3 jit_solution(6102812652380284830)
XLA Ops:
  0.0 1.1 %multiply_convert_fusion = bf16[1,256,512]{2,1,0:T(8,128)(2,1)S(1)} fusion(bf16[5,256,512]{2,1,0:T(8,128)(2,1)} %param.7), kind=kLoop, calls=%fused_computation.9 | loop fusion | flops 524288 | bytes 786432 | tf_op jit(solution)/shard_map/convert_element_type | solution.py:68
  1.1 1.2 %slice_convert_fusion = (f32[1,256,512]{2,1,0:T(8,128)S(1)}, bf16[1,256,512]{2,1,0:T(8,128)(2,1)S(1)}, f32[1,256,512]{2,1,0:T(8,128)S(1)}) fusion(bf16[5,256,512]{2,1,0:T(8,128)(2,1)} %param.7), kind=kLoop, calls=%fused_computation.28 | loop fusion | flops 262144 | bytes 2097152 | tf_op jit(solution)/shard_map/convert_element_type | solution.py:65
  2.8 0.7 fusion.43
  3.5 0.6 fusion.29
  5.1 1.9 %collective-permute-start = (bf16[133,512]{1,0:T(8,128)(2,1)S(1)}, bf16[133,512]{1,0:T(8,128)(2,1)S(1)}, u32[]{:S(2)}, u32[]{:S(2)}) collective-permute-start(bf16[133,512]{1,0:T(8,128)(2,1)S(1)} %pad_maximum_fusion), channel_id=1, source_target_pairs={{0,16},{16,32},{32,48},{48,64},{64,80},{80,96},{96,112},{112,128},... | collective-permute-start | bytes 408584 | tf_op jit(solution)/shard_map/ppermute | solution.py:13
  7.1 0.5 gather_fusion
  7.7 9.2 %collective-permute-start.1 = (bf16[4,8,512]{2,1,0:T(8,128)(2,1)S(1)}, bf16[4,8,512]{2,1,0:T(8,128)(2,1)S(1)}, u32[]{:S(2)}, u32[]{:S(2)}) collective-permute-start(bf16[4,8,512]{2,1,0:T(8,128)(2,1)S(1)} %select_select_fusion), channel_id=1, source_target_pairs={{0,16},{16,0},{32,48},{48,32},{64,80},{80,64},{96,112},{112,96},{1... | collective-permute-start | bytes 98312 | tf_op jit(solution)/shard_map/ppermute | solution.py:21
  17.2 0.6 gather_fusion.2
  17.9 1.9 %collective-permute-start.2 = (bf16[4,8,512]{2,1,0:T(8,128)(2,1)S(1)}, bf16[4,8,512]{2,1,0:T(8,128)(2,1)S(1)}, u32[]{:S(2)}, u32[]{:S(2)}) collective-permute-start(bf16[4,8,512]{2,1,0:T(8,128)(2,1)S(1)} %fusion.45), channel_id=1, source_target_pairs={{0,32},{16,48},{32,0},{48,16},{64,96},{80,112},{96,64},{112,80},{1... | collective-permute-start | bytes 98312 | tf_op jit(solution)/shard_map/ppermute | solution.py:21
  19.9 7.8 %collective-permute-done.2 = bf16[4,8,512]{2,1,0:T(8,128)(2,1)S(1)} collective-permute-done((bf16[4,8,512]{2,1,0:T(8,128)(2,1)S(1)}, bf16[4,8,512]{2,1,0:T(8,128)(2,1)S(1)}, u32[]{:S(2)}, u32[]{:S(2)}) %collective-permute-start.2) | collective-permute-done | bytes 32800 | tf_op jit(solution)/shard_map/ppermute | solution.py:21
  27.7 5.1 %collective-permute-start.3 = (bf16[4,8,512]{2,1,0:T(8,128)(2,1)S(1)}, bf16[4,8,512]{2,1,0:T(8,128)(2,1)S(1)}, u32[]{:S(2)}, u32[]{:S(2)}) collective-permute-start(bf16[4,8,512]{2,1,0:T(8,128)(2,1)S(1)} %add.75), channel_id=1, source_target_pairs={{0,64},{16,80},{32,96},{48,112},{64,0},{80,16},{96,32},{112,48},{1... | collective-permute-start | bytes 98312 | tf_op jit(solution)/shard_map/ppermute | solution.py:21
  32.8 0.6 gather_fusion.3
  33.4 8.8 %collective-permute-done.3 = bf16[4,8,512]{2,1,0:T(8,128)(2,1)S(1)} collective-permute-done((bf16[4,8,512]{2,1,0:T(8,128)(2,1)S(1)}, bf16[4,8,512]{2,1,0:T(8,128)(2,1)S(1)}, u32[]{:S(2)}, u32[]{:S(2)}) %collective-permute-start.3) | collective-permute-done | bytes 32800 | tf_op jit(solution)/shard_map/ppermute | solution.py:21
  42.2 3.5 %collective-permute-start.4 = (bf16[4,8,512]{2,1,0:T(8,128)(2,1)S(1)}, bf16[4,8,512]{2,1,0:T(8,128)(2,1)S(1)}, u32[]{:S(2)}, u32[]{:S(2)}) collective-permute-start(bf16[4,8,512]{2,1,0:T(8,128)(2,1)S(1)} %add.76), channel_id=1, source_target_pairs={{0,128},{16,144},{32,160},{48,176},{64,192},{80,208},{96,224},{112... | collective-permute-start | bytes 98312 | tf_op jit(solution)/shard_map/ppermute | solution.py:21
  46.0 2.1 %collective-permute-done.4 = bf16[4,8,512]{2,1,0:T(8,128)(2,1)S(1)} collective-permute-done((bf16[4,8,512]{2,1,0:T(8,128)(2,1)S(1)}, bf16[4,8,512]{2,1,0:T(8,128)(2,1)S(1)}, u32[]{:S(2)}, u32[]{:S(2)}) %collective-permute-start.4) | collective-permute-done | bytes 32800 | tf_op jit(solution)/shard_map/ppermute | solution.py:21
  48.0 5.1 %collective-permute-start.5 = (bf16[4,8,512]{2,1,0:T(8,128)(2,1)S(1)}, bf16[4,8,512]{2,1,0:T(8,128)(2,1)S(1)}, u32[]{:S(2)}, u32[]{:S(2)}) collective-permute-start(bf16[4,8,512]{2,1,0:T(8,128)(2,1)S(1)} %add.77), channel_id=1, source_target_pairs={{0,256},{16,272},{32,288},{48,304},{64,320},{80,336},{96,352},{112... | collective-permute-start | bytes 98312 | tf_op jit(solution)/shard_map/ppermute | solution.py:21
  53.2 0.7 slice_select_fusion.2
  54.5 0.7 fusion.24
  55.2 0.7 slice_select_fusion.1
  56.8 7.5 %fusion.1 = f32[2,128,512]{2,0,1:T(2,128)S(1)} fusion(bf16[1,255,512]{2,0,1:T(2,128)(2,1)S(1)} %copy.112, bf16[1,255,512]{2,0,1:T(2,128)(2,1)S(1)} %copy.111, bf16[128,1,512]{2,0,1:T(8,128)(2,1)S(1)} %bitcast.60), kind=kOutput, calls=%fused_computation.10 | convolution fusion | flops 34598912 | bytes 1177600 | tf_op jit(solution)/shard_map/conv_general_dilated | solution.py:35
  65.2 0.6 broadcast_in_dim.79
  65.8 8.2 %all-to-all-start = ((f32[16,2,128,4]{2,3,1,0:T(4,128)}), f32[16,2,128,4]{2,3,1,0:T(4,128)S(1)}, u32[]{:S(2)}, u32[]{:S(2)}) async-start(f32[16,2,128,4]{2,3,1,0:T(4,128)} %broadcast_in_dim.79), calls=%async_computation | async-start | bytes 131072 | tf_op jit(solution)/shard_map/all_to_all | solution.py:29
  74.1 8.1 %all-to-all-done = f32[16,2,128,4]{2,3,1,0:T(4,128)S(1)} async-done(((f32[16,2,128,4]{2,3,1,0:T(4,128)}), f32[16,2,128,4]{2,3,1,0:T(4,128)S(1)}, u32[]{:S(2)}, u32[]{:S(2)}) %all-to-all-start) | async-done | bytes 65568 | tf_op jit(solution)/shard_map/all_to_all | solution.py:29
  82.3 1.0 %add_convert_fusion = bf16[2,128,512]{2,1,0:T(8,128)(2,1)} fusion(f32[2,512]{1,0:T(2,128)S(1)} %get-tuple-element.26, f32[2,128]{1,0:T(2,128)S(1)} %bitcast.64, f32[2,512]{1,0:T(2,128)S(1)} %get-tuple-element.27, f32[2,128]{1,0:T(2,128)S(1)} %bitcast.65, f32[2,512]{1,0:T(2,128)S(1)} %get-tuple-element.28, f32[2,128]{1,0:T(2,128)S(1)} %bitcast.66, ...), kind=kLoop, calls=%fused_computation.8 | loop fusion | flops 1703936 | bytes 1069056 | tf_op jit(solution)/shard_map/convert_element_type | solution.py:120
  (77 shorter events, 4.6 us)
Async XLA Ops:
  0.0 7.0 %copy-start = (bf16[2,8,512]{2,1,0:T(8,128)(2,1)S(1)}, bf16[2,8,512]{2,1,0:T(8,128)(2,1)}, u32[]{:S(2)}) copy-start(bf16[2,8,512]{2,1,0:T(8,128)(2,1)} %param.10) | copy-start | bytes 49156
  1.1 1.3 %copy-start.5 = (s32[4]{0:T(128)S(1)}, s32[4]{0:T(128)}, u32[]{:S(2)}) copy-start(s32[4]{0:T(128)} %param.12) | copy-start | bytes 52
  2.3 2.0 %copy-start.2 = (bf16[7,512]{1,0:T(8,128)(2,1)S(1)}, bf16[7,512]{1,0:T(8,128)(2,1)}, u32[]{:S(2)}) copy-start(bf16[7,512]{1,0:T(8,128)(2,1)} %param.8) | copy-start | bytes 21508
  2.4 2.1 %copy-start.6 = (pred[8,17]{0,1:T(8,128)(4,1)S(1)}, pred[8,17]{0,1:T(8,128)(4,1)}, u32[]{:S(2)}) copy-start(pred[8,17]{0,1:T(8,128)(4,1)} %constant.95) | copy-start | bytes 412
  4.7 2.4 %copy-start.4 = (s32[4]{0:T(128)S(1)}, s32[4]{0:T(128)}, u32[]{:S(2)}) copy-start(s32[4]{0:T(128)} %param.13) | copy-start | bytes 52
  4.7 12.4 %copy-start.3 = (f32[64,4]{0,1:T(4,128)S(1)}, f32[64,4]{0,1:T(4,128)}, u32[]{:S(2)}) copy-start(f32[64,4]{0,1:T(4,128)} %param.11) | copy-start | bytes 3076
  4.8 40.9 %copy-start.1 = (bf16[128,512]{1,0:T(8,128)(2,1)S(1)}, bf16[128,512]{1,0:T(8,128)(2,1)}, u32[]{:S(2)}) copy-start(bf16[128,512]{1,0:T(8,128)(2,1)} %param.9) | copy-start | bytes 393220
  5.1 48.1 %collective-permute-start = (bf16[133,512]{1,0:T(8,128)(2,1)S(1)}, bf16[133,512]{1,0:T(8,128)(2,1)S(1)}, u32[]{:S(2)}, u32[]{:S(2)}) collective-permute-start(bf16[133,512]{1,0:T(8,128)(2,1)S(1)} %pad_maximum_fusion), channel_id=1, source_target_pairs={{0,16},{16,32},{32,48},{48,64},{64,80},{80,96},{96,112},{112,128},... | collective-permute-start | bytes 408584 | tf_op jit(solution)/shard_map/ppermute | solution.py:13
  7.7 10.1 %collective-permute-start.1 = (bf16[4,8,512]{2,1,0:T(8,128)(2,1)S(1)}, bf16[4,8,512]{2,1,0:T(8,128)(2,1)S(1)}, u32[]{:S(2)}, u32[]{:S(2)}) collective-permute-start(bf16[4,8,512]{2,1,0:T(8,128)(2,1)S(1)} %select_select_fusion), channel_id=1, source_target_pairs={{0,16},{16,0},{32,48},{48,32},{64,80},{80,64},{96,112},{112,96},{1... | collective-permute-start | bytes 98312 | tf_op jit(solution)/shard_map/ppermute | solution.py:21
  17.9 9.7 %collective-permute-start.2 = (bf16[4,8,512]{2,1,0:T(8,128)(2,1)S(1)}, bf16[4,8,512]{2,1,0:T(8,128)(2,1)S(1)}, u32[]{:S(2)}, u32[]{:S(2)}) collective-permute-start(bf16[4,8,512]{2,1,0:T(8,128)(2,1)S(1)} %fusion.45), channel_id=1, source_target_pairs={{0,32},{16,48},{32,0},{48,16},{64,96},{80,112},{96,64},{112,80},{1... | collective-permute-start | bytes 98312 | tf_op jit(solution)/shard_map/ppermute | solution.py:21
  27.7 14.5 %collective-permute-start.3 = (bf16[4,8,512]{2,1,0:T(8,128)(2,1)S(1)}, bf16[4,8,512]{2,1,0:T(8,128)(2,1)S(1)}, u32[]{:S(2)}, u32[]{:S(2)}) collective-permute-start(bf16[4,8,512]{2,1,0:T(8,128)(2,1)S(1)} %add.75), channel_id=1, source_target_pairs={{0,64},{16,80},{32,96},{48,112},{64,0},{80,16},{96,32},{112,48},{1... | collective-permute-start | bytes 98312 | tf_op jit(solution)/shard_map/ppermute | solution.py:21
  42.2 5.8 %collective-permute-start.4 = (bf16[4,8,512]{2,1,0:T(8,128)(2,1)S(1)}, bf16[4,8,512]{2,1,0:T(8,128)(2,1)S(1)}, u32[]{:S(2)}, u32[]{:S(2)}) collective-permute-start(bf16[4,8,512]{2,1,0:T(8,128)(2,1)S(1)} %add.76), channel_id=1, source_target_pairs={{0,128},{16,144},{32,160},{48,176},{64,192},{80,208},{96,224},{112... | collective-permute-start | bytes 98312 | tf_op jit(solution)/shard_map/ppermute | solution.py:21
  48.0 16.2 %collective-permute-start.5 = (bf16[4,8,512]{2,1,0:T(8,128)(2,1)S(1)}, bf16[4,8,512]{2,1,0:T(8,128)(2,1)S(1)}, u32[]{:S(2)}, u32[]{:S(2)}) collective-permute-start(bf16[4,8,512]{2,1,0:T(8,128)(2,1)S(1)} %add.77), channel_id=1, source_target_pairs={{0,256},{16,272},{32,288},{48,304},{64,320},{80,336},{96,352},{112... | collective-permute-start | bytes 98312 | tf_op jit(solution)/shard_map/ppermute | solution.py:21
  65.8 16.4 %all-to-all-start = ((f32[16,2,128,4]{2,3,1,0:T(4,128)}), f32[16,2,128,4]{2,3,1,0:T(4,128)S(1)}, u32[]{:S(2)}, u32[]{:S(2)}) async-start(f32[16,2,128,4]{2,3,1,0:T(4,128)} %broadcast_in_dim.79), calls=%async_computation | async-start | bytes 131072 | tf_op jit(solution)/shard_map/all_to_all | solution.py:29

commit v2 on v1

--- a/solution.py
+++ b/solution.py
@@ -1,26 +1,19 @@
 import jax
 import jax.numpy as jnp
 from jax import lax
-from jax.sharding import PartitionSpec as P
+from jax.sharding import Mesh, PartitionSpec as P
 
 TILE_ROWS = 128
 SEQS = 4
 
 
-def from_behind(block, axis, distance):
-    devices = range(lax.axis_size(axis))
-    route = [(i - distance, i) for i in devices if i - distance in devices]
-    return lax.ppermute(block, axis, route)
+SEQ = ("y", "near")
+GROUP = 8
 
 
-def xor_sum(block, axis):
-    size = lax.axis_size(axis)
-    step = 1
-    while step < size:
-        route = [(i, i ^ step) for i in range(size)]
-        block = block + lax.ppermute(block, axis, route)
-        step *= 2
-    return block
+def shifted(block, distance):
+    size = lax.axis_size(SEQ)
+    return lax.ppermute(block, SEQ, [(i, (i + distance) % size) for i in range(size)])
 
 
 def a2a_sum(block, axis):
@@ -49,7 +42,7 @@
     short_reach = short_filter.shape[0]
     long_reach = long_filter.shape[0]
     tile_count = rows_here // TILE_ROWS
-    me = lax.axis_index("seq")
+    me = lax.axis_index(SEQ)
     seq_ends = jnp.cumsum(seq_tiles)
     tile_ids = me * tile_count + jnp.arange(tile_count, dtype=jnp.int32)
     seq_of = jnp.sum((seq_ends[None, :] <= tile_ids[:, None]).astype(jnp.int32), axis=1)
@@ -60,7 +53,7 @@
     owned = (owner_slot >= 0) & (owner_slot < held)
     local_rows = jnp.take(edit_table, jnp.clip(owner_slot, 0, held - 1), axis=0)
     local_rows = jnp.where(owned[:, None, None], local_rows, jnp.zeros_like(local_rows))
-    chosen = xor_sum(local_rows, "seq")
+    partial_rows = a2a_sum(local_rows, "y")
 
     first_gate = streams[0].astype(jnp.float32)
     second_gate = streams[3].astype(jnp.float32)
@@ -88,9 +81,16 @@
         [gated[rows_here - (short_reach - 1) :], carried_later[-1][TILE_ROWS - (long_reach - 1) :]],
         axis=0,
     )
-    border = from_behind(border, "seq", 1)
-    short_border = border[: short_reach - 1]
-    long_border = border[short_reach - 1 :]
+    row_count = partial_rows.shape[0] * partial_rows.shape[1]
+    sent = jnp.concatenate([border, partial_rows.reshape(row_count, width)], axis=0)
+    sent = shifted(sent, 1)
+    short_border = sent[: short_reach - 1]
+    long_border = sent[short_reach - 1 : border.shape[0]]
+    chosen = partial_rows + sent[border.shape[0] :].reshape(partial_rows.shape)
+    distance = 2
+    while distance < GROUP:
+        chosen = chosen + shifted(chosen, distance)
+        distance *= 2
 
     first_out = depth_conv(short_window(0, short_border)[None], short_filter)[0]
     carried = [carried_of(0, first_out)] + carried_later
@@ -121,16 +121,18 @@
 
 
 def solution(mesh):
+    devices = mesh.devices.reshape(mesh.shape["seq"] // GROUP, GROUP, mesh.shape["chan"])
+    split_mesh = Mesh(devices, ("y", "near", "chan"))
     in_specs = (
-        P(None, "seq", "chan"),
+        P(None, SEQ, "chan"),
         P(None, "chan"),
         P(None, "chan"),
-        P("seq", None, "chan"),
+        P(SEQ, None, "chan"),
         P(),
         P(),
         P(),
     )
-    out_specs = P("seq", "chan")
+    out_specs = P(SEQ, "chan")
     return jax.shard_map(
-        on_device, mesh=mesh, in_specs=in_specs, out_specs=out_specs, check_vma=False
+        on_device, mesh=split_mesh, in_specs=in_specs, out_specs=out_specs, check_vma=False
     )

time: 83.6 us -> 80.7 us (0.965)
  the two profiles are of different devices: /device:TPU:128 before, /device:TPU:2 now
where the time goes in v2:
time: 80.7 us; the launch traced here: 80.2 us
  starting transfers between devices  29.2 us (36%)
  waiting for transfers between devices  28.3 us (35%)
  matrix products  8.02 us (10%)
  local copies, waits for them, and re-layouts  7.2 us (9%)
  other arithmetic  7.01 us (9%)
    ppermute x3, waiting for transfers between devices, shifted(): lax.ppermute(block, SEQ, [(i, (i + distance) % size) for i in range(size)])  21.6 us
    ppermute x3, starting transfers between devices, shifted(): lax.ppermute(block, SEQ, [(i, (i + distance) % size) for i in range(size)])  15.8 us
    all_to_all x2, starting transfers between devices, a2a_sum(): return jnp.sum(lax.all_to_all(copies, axis, 0, 0, tiled=False), axis=0)  13.4 us
    conv_general_dilated x3, matrix products, depth_conv(): lax.conv_general_dilated(window, kernel, (1,), 'VALID', dimension_numbers...  7.82 us
    all_to_all x2, waiting for transfers between devices, a2a_sum(): return jnp.sum(lax.all_to_all(copies, axis, 0, 0, tiled=False), axis=0)  6.76 us
  transfers between devices with their start and end apart: 5, of which 3 were waited for; matrix products, arithmetic and copies ran while one was open for 21% of the time, Pallas kernels for 0%

profile of v2, /device:TPU:2, one launch (start us, length us, event | category | flops | bytes accessed | tf_op | source)
XLA Modules:
  0.0 80.2 jit_solution(2032464629110973199)
XLA Ops:
  0.0 0.8 compare_and_fusion
  0.8 0.5 gather_fusion
  1.4 0.7 broadcast_in_dim.81
  2.1 4.5 %all-to-all-start = ((bf16[4,4,8,512]{3,2,1,0:T(8,128)(2,1)}), bf16[4,4,8,512]{3,2,1,0:T(8,128)(2,1)S(1)}, u32[]{:S(2)}, u32[]{:S(2)}) async-start(bf16[4,4,8,512]{3,2,1,0:T(8,128)(2,1)} %broadcast_in_dim.81), calls=%async_computation | async-start | bytes 262144 | tf_op jit(solution)/shard_map/all_to_all | solution.py:22
  6.6 1.1 %multiply_convert_fusion = bf16[1,256,512]{2,1,0:T(8,128)(2,1)S(1)} fusion(bf16[5,256,512]{2,1,0:T(8,128)(2,1)} %param.7), kind=kLoop, calls=%fused_computation.9 | loop fusion | flops 524288 | bytes 786432 | tf_op jit(solution)/shard_map/convert_element_type | solution.py:61
  8.9 0.6 fusion.45
  9.6 0.6 fusion.30
  11.1 0.5 copy-done.2
  11.9 0.6 gather_fusion.2
  12.6 0.6 gather_fusion.3
  13.2 1.9 %collective-permute-start = (bf16[165,512]{1,0:T(8,128)(2,1)S(1)}, bf16[165,512]{1,0:T(8,128)(2,1)S(1)}, u32[]{:S(2)}, u32[]{:S(2)}) collective-permute-start(bf16[165,512]{1,0:T(8,128)(2,1)S(1)} %pad_maximum_fusion), channel_id=1, source_target_pairs={{0,16},{16,32},{32,48},{48,64},{64,80},{80,96},{96,112},{112,128},... | collective-permute-start | bytes 506888 | tf_op jit(solution)/shard_map/ppermute | solution.py:16
  15.2 15.7 %collective-permute-done = bf16[165,512]{1,0:T(8,128)(2,1)S(1)} collective-permute-done((bf16[165,512]{1,0:T(8,128)(2,1)S(1)}, bf16[165,512]{1,0:T(8,128)(2,1)S(1)}, u32[]{:S(2)}, u32[]{:S(2)}) %collective-permute-start) | collective-permute-done | bytes 168992 | tf_op jit(solution)/shard_map/ppermute | solution.py:16
  30.9 3.9 %collective-permute-start.1 = (bf16[4,8,512]{2,1,0:T(8,128)(2,1)S(1)}, bf16[4,8,512]{2,1,0:T(8,128)(2,1)S(1)}, u32[]{:S(2)}, u32[]{:S(2)}) collective-permute-start(bf16[4,8,512]{2,1,0:T(8,128)(2,1)S(1)} %fusion.27), channel_id=1, source_target_pairs={{0,32},{16,48},{32,64},{48,80},{64,96},{80,112},{96,128},{112,144}... | collective-permute-start | bytes 98312 | tf_op jit(solution)/shard_map/ppermute | solution.py:16
  34.8 0.7 slice_select_fusion.2
  36.2 0.7 fusion.24
  36.9 0.7 slice_select_fusion.1
  38.5 5.9 %collective-permute-done.1 = bf16[4,8,512]{2,1,0:T(8,128)(2,1)S(1)} collective-permute-done((bf16[4,8,512]{2,1,0:T(8,128)(2,1)S(1)}, bf16[4,8,512]{2,1,0:T(8,128)(2,1)S(1)}, u32[]{:S(2)}, u32[]{:S(2)}) %collective-permute-start.1) | collective-permute-done | bytes 32800 | tf_op jit(solution)/shard_map/ppermute | solution.py:16
  44.5 9.9 %collective-permute-start.2 = (bf16[4,8,512]{2,1,0:T(8,128)(2,1)S(1)}, bf16[4,8,512]{2,1,0:T(8,128)(2,1)S(1)}, u32[]{:S(2)}, u32[]{:S(2)}) collective-permute-start(bf16[4,8,512]{2,1,0:T(8,128)(2,1)S(1)} %fusion.47), channel_id=1, source_target_pairs={{0,64},{16,80},{32,96},{48,112},{64,128},{80,144},{96,160},{112,17... | collective-permute-start | bytes 98312 | tf_op jit(solution)/shard_map/ppermute | solution.py:16
  54.4 7.5 %fusion.1 = f32[2,128,512]{2,0,1:T(2,128)S(1)} fusion(bf16[1,255,512]{2,0,1:T(2,128)(2,1)S(1)} %copy.112, bf16[1,255,512]{2,0,1:T(2,128)(2,1)S(1)} %copy.111, bf16[128,1,512]{2,0,1:T(8,128)(2,1)S(1)} %bitcast.68), kind=kOutput, calls=%fused_computation.10 | convolution fusion | flops 34598912 | bytes 1177600 | tf_op jit(solution)/shard_map/conv_general_dilated | solution.py:28
  61.9 0.5 gather_fusion.1
  62.8 0.6 broadcast_in_dim.86
  63.4 8.9 %all-to-all-start.1 = ((f32[16,2,128,4]{2,3,1,0:T(4,128)}), f32[16,2,128,4]{2,3,1,0:T(4,128)S(1)}, u32[]{:S(2)}, u32[]{:S(2)}) async-start(f32[16,2,128,4]{2,3,1,0:T(4,128)} %broadcast_in_dim.86), calls=%async_computation.1 | async-start | bytes 131072 | tf_op jit(solution)/shard_map/all_to_all | solution.py:22
  72.4 6.8 %all-to-all-done.1 = f32[16,2,128,4]{2,3,1,0:T(4,128)S(1)} async-done(((f32[16,2,128,4]{2,3,1,0:T(4,128)}), f32[16,2,128,4]{2,3,1,0:T(4,128)S(1)}, u32[]{:S(2)}, u32[]{:S(2)}) %all-to-all-start.1) | async-done | bytes 65568 | tf_op jit(solution)/shard_map/all_to_all | solution.py:22
  79.3 1.0 %add_convert_fusion = bf16[2,128,512]{2,1,0:T(8,128)(2,1)} fusion(f32[2,512]{1,0:T(2,128)S(1)} %get-tuple-element.26, f32[2,128]{1,0:T(2,128)S(1)} %bitcast.72, f32[2,512]{1,0:T(2,128)S(1)} %get-tuple-element.27, f32[2,128]{1,0:T(2,128)S(1)} %bitcast.73, f32[2,512]{1,0:T(2,128)S(1)} %get-tuple-element.28, f32[2,128]{1,0:T(2,128)S(1)} %bitcast.74, ...), kind=kLoop, calls=%fused_computation.8 | loop fusion | flops 1703936 | bytes 1069056 | tf_op jit(solution)/shard_map/convert_element_type | solution.py:120
  (75 shorter events, 4.5 us)
Async XLA Ops:
  0.0 0.8 copy-start
  0.0 7.7 %copy-start.1 = (bf16[5,256,512]{2,1,0:T(8,128)(2,1)S(1)}, bf16[5,256,512]{2,1,0:T(8,128)(2,1)}, u32[]{:S(2)}) copy-start(bf16[5,256,512]{2,1,0:T(8,128)(2,1)} %param.7) | copy-start | bytes 3932164
  2.1 11.0 %all-to-all-start = ((bf16[4,4,8,512]{3,2,1,0:T(8,128)(2,1)}), bf16[4,4,8,512]{3,2,1,0:T(8,128)(2,1)S(1)}, u32[]{:S(2)}, u32[]{:S(2)}) async-start(bf16[4,4,8,512]{3,2,1,0:T(8,128)(2,1)} %broadcast_in_dim.81), calls=%async_computation | async-start | bytes 262144 | tf_op jit(solution)/shard_map/all_to_all | solution.py:22
  7.7 0.7 copy-start.6
  7.7 1.2 %copy-start.5 = (s32[4]{0:T(128)S(1)}, s32[4]{0:T(128)}, u32[]{:S(2)}) copy-start(s32[4]{0:T(128)} %param.13) | copy-start | bytes 52
  7.8 2.6 %copy-start.3 = (bf16[7,512]{1,0:T(8,128)(2,1)S(1)}, bf16[7,512]{1,0:T(8,128)(2,1)}, u32[]{:S(2)}) copy-start(bf16[7,512]{1,0:T(8,128)(2,1)} %param.8) | copy-start | bytes 21508
  7.8 2.8 %copy-start.7 = (pred[8,17]{0,1:T(8,128)(4,1)S(1)}, pred[8,17]{0,1:T(8,128)(4,1)}, u32[]{:S(2)}) copy-start(pred[8,17]{0,1:T(8,128)(4,1)} %constant.103) | copy-start | bytes 412
  10.8 0.9 %copy-start.2 = (bf16[128,512]{1,0:T(8,128)(2,1)S(1)}, bf16[128,512]{1,0:T(8,128)(2,1)}, u32[]{:S(2)}) copy-start(bf16[128,512]{1,0:T(8,128)(2,1)} %param.9) | copy-start | bytes 393220
  10.8 1.1 %copy-start.4 = (f32[64,4]{0,1:T(4,128)S(1)}, f32[64,4]{0,1:T(4,128)}, u32[]{:S(2)}) copy-start(f32[64,4]{0,1:T(4,128)} %param.11) | copy-start | bytes 3076
  13.2 17.7 %collective-permute-start = (bf16[165,512]{1,0:T(8,128)(2,1)S(1)}, bf16[165,512]{1,0:T(8,128)(2,1)S(1)}, u32[]{:S(2)}, u32[]{:S(2)}) collective-permute-start(bf16[165,512]{1,0:T(8,128)(2,1)S(1)} %pad_maximum_fusion), channel_id=1, source_target_pairs={{0,16},{16,32},{32,48},{48,64},{64,80},{80,96},{96,112},{112,128},... | collective-permute-start | bytes 506888 | tf_op jit(solution)/shard_map/ppermute | solution.py:16
  30.9 13.5 %collective-permute-start.1 = (bf16[4,8,512]{2,1,0:T(8,128)(2,1)S(1)}, bf16[4,8,512]{2,1,0:T(8,128)(2,1)S(1)}, u32[]{:S(2)}, u32[]{:S(2)}) collective-permute-start(bf16[4,8,512]{2,1,0:T(8,128)(2,1)S(1)} %fusion.27), channel_id=1, source_target_pairs={{0,32},{16,48},{32,64},{48,80},{64,96},{80,112},{96,128},{112,144}... | collective-permute-start | bytes 98312 | tf_op jit(solution)/shard_map/ppermute | solution.py:16
  44.5 17.4 %collective-permute-start.2 = (bf16[4,8,512]{2,1,0:T(8,128)(2,1)S(1)}, bf16[4,8,512]{2,1,0:T(8,128)(2,1)S(1)}, u32[]{:S(2)}, u32[]{:S(2)}) collective-permute-start(bf16[4,8,512]{2,1,0:T(8,128)(2,1)S(1)} %fusion.47), channel_id=1, source_target_pairs={{0,64},{16,80},{32,96},{48,112},{64,128},{80,144},{96,160},{112,17... | collective-permute-start | bytes 98312 | tf_op jit(solution)/shard_map/ppermute | solution.py:16
  63.4 15.7 %all-to-all-start.1 = ((f32[16,2,128,4]{2,3,1,0:T(4,128)}), f32[16,2,128,4]{2,3,1,0:T(4,128)S(1)}, u32[]{:S(2)}, u32[]{:S(2)}) async-start(f32[16,2,128,4]{2,3,1,0:T(4,128)} %broadcast_in_dim.86), calls=%async_computation.1 | async-start | bytes 131072 | tf_op jit(solution)/shard_map/all_to_all | solution.py:22

commit v3 on v2

--- a/solution.py
+++ b/solution.py
@@ -7,8 +7,7 @@
 SEQS = 4
 
 
-SEQ = ("y", "near")
-GROUP = 8
+SEQ = ("y", "zh", "core")
 
 
 def shifted(block, distance):
@@ -87,10 +86,7 @@
     short_border = sent[: short_reach - 1]
     long_border = sent[short_reach - 1 : border.shape[0]]
     chosen = partial_rows + sent[border.shape[0] :].reshape(partial_rows.shape)
-    distance = 2
-    while distance < GROUP:
-        chosen = chosen + shifted(chosen, distance)
-        distance *= 2
+    chosen = a2a_sum(chosen, "zh")
 
     first_out = depth_conv(short_window(0, short_border)[None], short_filter)[0]
     carried = [carried_of(0, first_out)] + carried_later
@@ -121,8 +117,8 @@
 
 
 def solution(mesh):
-    devices = mesh.devices.reshape(mesh.shape["seq"] // GROUP, GROUP, mesh.shape["chan"])
-    split_mesh = Mesh(devices, ("y", "near", "chan"))
+    devices = mesh.devices.reshape(mesh.shape["seq"] // 8, 4, 2, mesh.shape["chan"])
+    split_mesh = Mesh(devices, ("y", "zh", "core", "chan"))
     in_specs = (
         P(None, SEQ, "chan"),
         P(None, "chan"),

time: 80.7 us -> 75 us (0.929)
  the two profiles are of different devices: /device:TPU:2 before, /device:TPU:8 now
where the time goes in v3:
time: 75 us; the launch traced here: 74.5 us
  starting transfers between devices  31 us (41%)
  waiting for transfers between devices  20.3 us (27%)
  matrix products  8.02 us (11%)
  local copies, waits for them, and re-layouts  7.89 us (11%)
  other arithmetic  6.89 us (9%)
    all_to_all x3, starting transfers between devices, a2a_sum(): return jnp.sum(lax.all_to_all(copies, axis, 0, 0, tiled=False), axis=0)  29 us
    all_to_all x3, waiting for transfers between devices, a2a_sum(): return jnp.sum(lax.all_to_all(copies, axis, 0, 0, tiled=False), axis=0)  10.5 us
    ppermute x1, waiting for transfers between devices, shifted(): lax.ppermute(block, SEQ, [(i, (i + distance) % size) for i in range(size)])  9.79 us
    conv_general_dilated x3, matrix products, depth_conv(): lax.conv_general_dilated(window, kernel, (1,), 'VALID', dimension_numbers...  7.82 us
    broadcast_in_dim x3, local copies, waits for them, and re-layouts, a2a_sum(): copies = jnp.broadcast_to(block[None], (size,) + block.shape)  1.97 us
    ppermute x1, starting transfers between devices, shifted(): lax.ppermute(block, SEQ, [(i, (i + distance) % size) for i in range(size)])  1.92 us
  transfers between devices with their start and end apart: 4, of which 3 were waited for; matrix products, arithmetic and copies ran while one was open for 22% of the time, Pallas kernels for 0%

profile of v3, /device:TPU:8, one launch (start us, length us, event | category | flops | bytes accessed | tf_op | source)
XLA Modules:
  0.0 74.5 jit_solution(21570529844262036)
XLA Ops:
  0.0 0.8 %compare_and_fusion = (pred[4]{0:T(512)(128)(4,1)S(1)}, pred[4]{0:T(512)(128)(4,1)S(1)}, pred[4]{0:T(512)(128)(4,1)S(1)}, s32[4]{0:T(128)S(1)}) fusion(s32[4]{0:T(128)} %param.13, s32[]{:T(128)S(6)} %mul.103), kind=kLoop, calls=%fused_computation.75 | loop fusion | flops 68 | bytes 48 | tf_op jit(solution)/shard_map/jit(_take)/and | solution.py:110
  0.8 0.5 gather_fusion
  1.4 0.7 broadcast_in_dim.87
  2.1 9.1 %all-to-all-start = ((bf16[4,4,8,512]{3,2,1,0:T(8,128)(2,1)}), bf16[4,4,8,512]{3,2,1,0:T(8,128)(2,1)S(1)}, u32[]{:S(2)}, u32[]{:S(2)}) async-start(bf16[4,4,8,512]{3,2,1,0:T(8,128)(2,1)} %broadcast_in_dim.87), calls=%async_computation | async-start | bytes 262144 | tf_op jit(solution)/shard_map/all_to_all | solution.py:21
  11.2 1.1 %multiply_convert_fusion = bf16[1,256,512]{2,1,0:T(8,128)(2,1)S(1)} fusion(bf16[5,256,512]{2,1,0:T(8,128)(2,1)} %param.7), kind=kLoop, calls=%fused_computation.9 | loop fusion | flops 524288 | bytes 786432 | tf_op jit(solution)/shard_map/convert_element_type | solution.py:60
  13.6 0.7 fusion.45
  14.2 0.7 fusion.30
  15.8 0.5 copy-done.2
  16.7 0.6 gather_fusion.2
  17.3 0.6 gather_fusion.3
  17.9 1.9 %collective-permute-start = (bf16[165,512]{1,0:T(8,128)(2,1)S(1)}, bf16[165,512]{1,0:T(8,128)(2,1)S(1)}, u32[]{:S(2)}, u32[]{:S(2)}) collective-permute-start(bf16[165,512]{1,0:T(8,128)(2,1)S(1)} %pad_maximum_fusion), channel_id=1, source_target_pairs={{0,16},{16,32},{32,48},{48,64},{64,80},{80,96},{96,112},{112,128},... | collective-permute-start | bytes 506888 | tf_op jit(solution)/shard_map/ppermute | solution.py:15
  19.9 9.8 %collective-permute-done = bf16[165,512]{1,0:T(8,128)(2,1)S(1)} collective-permute-done((bf16[165,512]{1,0:T(8,128)(2,1)S(1)}, bf16[165,512]{1,0:T(8,128)(2,1)S(1)}, u32[]{:S(2)}, u32[]{:S(2)}) %collective-permute-start) | collective-permute-done | bytes 168992 | tf_op jit(solution)/shard_map/ppermute | solution.py:15
  29.8 0.7 broadcast_in_dim.91
  30.4 14.7 %all-to-all-start.1 = ((bf16[4,4,8,512]{3,2,1,0:T(8,128)(2,1)}), bf16[4,4,8,512]{3,2,1,0:T(8,128)(2,1)S(1)}, u32[]{:S(2)}, u32[]{:S(2)}) async-start(bf16[4,4,8,512]{3,2,1,0:T(8,128)(2,1)} %broadcast_in_dim.91), calls=%async_computation.1 | async-start | bytes 262144 | tf_op jit(solution)/shard_map/all_to_all | solution.py:21
  45.1 0.6 slice_select_fusion.2
  46.4 0.7 fusion.24
  47.1 0.6 slice_select_fusion.1
  48.6 7.5 %fusion.1 = f32[2,128,512]{2,0,1:T(2,128)S(1)} fusion(bf16[1,255,512]{2,0,1:T(2,128)(2,1)S(1)} %copy.112, bf16[1,255,512]{2,0,1:T(2,128)(2,1)S(1)} %copy.111, bf16[128,1,512]{2,0,1:T(8,128)(2,1)S(1)} %bitcast.66), kind=kOutput, calls=%fused_computation.10 | convolution fusion | flops 34598912 | bytes 1177600 | tf_op jit(solution)/shard_map/conv_general_dilated | solution.py:27
  56.1 2.4 %all-to-all-done.1 = bf16[4,4,8,512]{3,2,1,0:T(8,128)(2,1)S(1)} async-done(((bf16[4,4,8,512]{3,2,1,0:T(8,128)(2,1)}), bf16[4,4,8,512]{3,2,1,0:T(8,128)(2,1)S(1)}, u32[]{:S(2)}, u32[]{:S(2)}) %all-to-all-start.1) | async-done | bytes 131104 | tf_op jit(solution)/shard_map/all_to_all | solution.py:21
  58.5 0.5 gather_fusion.1
  59.4 0.6 broadcast_in_dim.93
  60.0 5.2 %all-to-all-start.2 = ((f32[16,2,128,4]{2,3,1,0:T(4,128)}), f32[16,2,128,4]{2,3,1,0:T(4,128)S(1)}, u32[]{:S(2)}, u32[]{:S(2)}) async-start(f32[16,2,128,4]{2,3,1,0:T(4,128)} %broadcast_in_dim.93), calls=%async_computation.2 | async-start | bytes 131072 | tf_op jit(solution)/shard_map/all_to_all | solution.py:21
  65.3 8.1 %all-to-all-done.2 = f32[16,2,128,4]{2,3,1,0:T(4,128)S(1)} async-done(((f32[16,2,128,4]{2,3,1,0:T(4,128)}), f32[16,2,128,4]{2,3,1,0:T(4,128)S(1)}, u32[]{:S(2)}, u32[]{:S(2)}) %all-to-all-start.2) | async-done | bytes 65568 | tf_op jit(solution)/shard_map/all_to_all | solution.py:21
  73.5 1.0 %add_convert_fusion = bf16[2,128,512]{2,1,0:T(8,128)(2,1)} fusion(f32[2,512]{1,0:T(2,128)S(1)} %get-tuple-element.26, f32[2,128]{1,0:T(2,128)S(1)} %bitcast.70, f32[2,512]{1,0:T(2,128)S(1)} %get-tuple-element.27, f32[2,128]{1,0:T(2,128)S(1)} %bitcast.71, f32[2,512]{1,0:T(2,128)S(1)} %get-tuple-element.28, f32[2,128]{1,0:T(2,128)S(1)} %bitcast.72, ...), kind=kLoop, calls=%fused_computation.8 | loop fusion | flops 1703936 | bytes 1069056 | tf_op jit(solution)/shard_map/convert_element_type | solution.py:116
  (73 shorter events, 4.5 us)
Async XLA Ops:
  0.0 0.8 %copy-start = (bf16[2,8,512]{2,1,0:T(8,128)(2,1)S(1)}, bf16[2,8,512]{2,1,0:T(8,128)(2,1)}, u32[]{:S(2)}) copy-start(bf16[2,8,512]{2,1,0:T(8,128)(2,1)} %param.10) | copy-start | bytes 49156
  0.0 12.3 %copy-start.1 = (bf16[5,256,512]{2,1,0:T(8,128)(2,1)S(1)}, bf16[5,256,512]{2,1,0:T(8,128)(2,1)}, u32[]{:S(2)}) copy-start(bf16[5,256,512]{2,1,0:T(8,128)(2,1)} %param.7) | copy-start | bytes 3932164
  2.1 15.8 %all-to-all-start = ((bf16[4,4,8,512]{3,2,1,0:T(8,128)(2,1)}), bf16[4,4,8,512]{3,2,1,0:T(8,128)(2,1)S(1)}, u32[]{:S(2)}, u32[]{:S(2)}) async-start(bf16[4,4,8,512]{3,2,1,0:T(8,128)(2,1)} %broadcast_in_dim.87), calls=%async_computation | async-start | bytes 262144 | tf_op jit(solution)/shard_map/all_to_all | solution.py:21
  12.3 0.7 copy-start.6
  12.3 1.2 %copy-start.5 = (s32[4]{0:T(128)S(1)}, s32[4]{0:T(128)}, u32[]{:S(2)}) copy-start(s32[4]{0:T(128)} %param.13) | copy-start | bytes 52
  12.4 2.7 %copy-start.3 = (bf16[7,512]{1,0:T(8,128)(2,1)S(1)}, bf16[7,512]{1,0:T(8,128)(2,1)}, u32[]{:S(2)}) copy-start(bf16[7,512]{1,0:T(8,128)(2,1)} %param.8) | copy-start | bytes 21508
  12.4 2.9 %copy-start.7 = (pred[8,17]{0,1:T(8,128)(4,1)S(1)}, pred[8,17]{0,1:T(8,128)(4,1)}, u32[]{:S(2)}) copy-start(pred[8,17]{0,1:T(8,128)(4,1)} %constant.109) | copy-start | bytes 412
  15.5 0.9 %copy-start.2 = (bf16[128,512]{1,0:T(8,128)(2,1)S(1)}, bf16[128,512]{1,0:T(8,128)(2,1)}, u32[]{:S(2)}) copy-start(bf16[128,512]{1,0:T(8,128)(2,1)} %param.9) | copy-start | bytes 393220
  15.5 1.1 %copy-start.4 = (f32[64,4]{0,1:T(4,128)S(1)}, f32[64,4]{0,1:T(4,128)}, u32[]{:S(2)}) copy-start(f32[64,4]{0,1:T(4,128)} %param.11) | copy-start | bytes 3076
  17.9 11.8 %collective-permute-start = (bf16[165,512]{1,0:T(8,128)(2,1)S(1)}, bf16[165,512]{1,0:T(8,128)(2,1)S(1)}, u32[]{:S(2)}, u32[]{:S(2)}) collective-permute-start(bf16[165,512]{1,0:T(8,128)(2,1)S(1)} %pad_maximum_fusion), channel_id=1, source_target_pairs={{0,16},{16,32},{32,48},{48,64},{64,80},{80,96},{96,112},{112,128},... | collective-permute-start | bytes 506888 | tf_op jit(solution)/shard_map/ppermute | solution.py:15
  30.4 28.1 %all-to-all-start.1 = ((bf16[4,4,8,512]{3,2,1,0:T(8,128)(2,1)}), bf16[4,4,8,512]{3,2,1,0:T(8,128)(2,1)S(1)}, u32[]{:S(2)}, u32[]{:S(2)}) async-start(bf16[4,4,8,512]{3,2,1,0:T(8,128)(2,1)} %broadcast_in_dim.91), calls=%async_computation.1 | async-start | bytes 262144 | tf_op jit(solution)/shard_map/all_to_all | solution.py:21
  60.0 13.4 %all-to-all-start.2 = ((f32[16,2,128,4]{2,3,1,0:T(4,128)}), f32[16,2,128,4]{2,3,1,0:T(4,128)S(1)}, u32[]{:S(2)}, u32[]{:S(2)}) async-start(f32[16,2,128,4]{2,3,1,0:T(4,128)} %broadcast_in_dim.93), calls=%async_computation.2 | async-start | bytes 131072 | tf_op jit(solution)/shard_map/all_to_all | solution.py:21

commit v4 on v3

--- a/solution.py
+++ b/solution.py
@@ -49,9 +49,13 @@
 
     held = edit_table.shape[0]
     owner_slot = seq_tenant - me * held
-    owned = (owner_slot >= 0) & (owner_slot < held)
-    local_rows = jnp.take(edit_table, jnp.clip(owner_slot, 0, held - 1), axis=0)
-    local_rows = jnp.where(owned[:, None, None], local_rows, jnp.zeros_like(local_rows))
+    picked = []
+    for s in range(SEQS):
+        rows = jnp.zeros_like(edit_table[0])
+        for slot in range(held):
+            rows = jnp.where(owner_slot[s] == slot, edit_table[slot], rows)
+        picked.append(rows)
+    local_rows = jnp.stack(picked)
     partial_rows = a2a_sum(local_rows, "y")
 
     first_gate = streams[0].astype(jnp.float32)
@@ -86,7 +90,14 @@
     short_border = sent[: short_reach - 1]
     long_border = sent[short_reach - 1 : border.shape[0]]
     chosen = partial_rows + sent[border.shape[0] :].reshape(partial_rows.shape)
-    chosen = a2a_sum(chosen, "zh")
+    zh_size = lax.axis_size("zh")
+    peer = me + (jnp.arange(zh_size, dtype=jnp.int32) - lax.axis_index("zh")) * lax.axis_size("core")
+    peer_tiles = peer[:, None] * tile_count + jnp.arange(tile_count, dtype=jnp.int32)[None, :]
+    peer_seq = jnp.sum((seq_ends[None, None, :] <= peer_tiles[:, :, None]).astype(jnp.int32), axis=2)
+    outgoing = jnp.zeros((zh_size, tile_count) + chosen.shape[1:], chosen.dtype)
+    for s in range(SEQS):
+        outgoing = jnp.where((peer_seq == s)[:, :, None, None], chosen[s], outgoing)
+    tile_rows = jnp.sum(lax.all_to_all(outgoing, "zh", 0, 0, tiled=False), axis=0)
 
     first_out = depth_conv(short_window(0, short_border)[None], short_filter)[0]
     carried = [carried_of(0, first_out)] + carried_later
@@ -101,7 +112,6 @@
 
     rows_per = edit_table.shape[1]
     rank = rows_per // 2
-    tile_rows = jnp.take(chosen, seq_of, axis=0)
     projected = jnp.einsum(
         "tnc,trc->tnr", hidden, tile_rows, preferred_element_type=jnp.float32
     )

time: 75 us -> 80.2 us (1.069)
  between operations: 0.47 us -> 5.41 us
  other arithmetic: 6.89 us -> 8.42 us
  local copies, waits for them, and re-layouts: 7.89 us -> 6.69 us
    all_to_all x3 -> x2, starting transfers between devices: 29 us -> 14.3 us  [a2a_sum(): return jnp.sum(lax.all_to_all(copies, axis, 0, 0, tiled=False), axis=0)]
    all_to_all x0 -> x1, starting transfers between devices: none -> 14.7 us  [on_device(): lax.all_to_all(outgoing, 'zh', 0, 0, tiled=False)]
    all_to_all x3 -> x2, waiting for transfers between devices: 10.5 us -> 8.11 us  [a2a_sum(): return jnp.sum(lax.all_to_all(copies, axis, 0, 0, tiled=False), axis=0)]
    all_to_all x0 -> x1, waiting for transfers between devices: none -> 2.19 us  [on_device(): lax.all_to_all(outgoing, 'zh', 0, 0, tiled=False)]
    select_n x3 -> x2, other arithmetic: 0.16 us -> 1.46 us  [the longest x1 0.74 us: on_device(): outgoing = jnp.where((peer_seq == s)[:, :, None, None], chosen[s], outgoing)]
    gather x2 -> x0, local copies, waits for them, and re-layouts: 1.1 us -> none  [the longest x1 0.55 us: on_device(): local_rows = jnp.take(edit_table, jnp.clip(owner_slot, 0, held - 1), axis=0)]
    broadcast_in_dim x3 -> x2, local copies, waits for them, and re-layouts: 1.97 us -> 1.31 us  [a2a_sum(): copies = jnp.broadcast_to(block[None], (size,) + block.shape)]
  transfers between devices with their start and end apart: 4 -> 4, of which waited for: 3 -> 3; matrix products, arithmetic and copies ran while one was open for 22% -> 21% of each run, Pallas kernels for 0% -> 0%
where the time goes in v4:
time: 80.2 us; the launch traced here: 79.6 us
  starting transfers between devices  30.9 us (39%)
  waiting for transfers between devices  20.1 us (25%)
  other arithmetic  8.42 us (10%)
  matrix products  8.02 us (10%)
  local copies, waits for them, and re-layouts  6.69 us (8%)
  between operations  5.41 us (7%)
    all_to_all x1, starting transfers between devices, on_device(): lax.all_to_all(outgoing, 'zh', 0, 0, tiled=False)  14.7 us
    all_to_all x2, starting transfers between devices, a2a_sum(): return jnp.sum(lax.all_to_all(copies, axis, 0, 0, tiled=False), axis=0)  14.3 us
    ppermute x1, waiting for transfers between devices, shifted(): lax.ppermute(block, SEQ, [(i, (i + distance) % size) for i in range(size)])  9.79 us
    all_to_all x2, waiting for transfers between devices, a2a_sum(): return jnp.sum(lax.all_to_all(copies, axis, 0, 0, tiled=False), axis=0)  8.11 us
    conv_general_dilated x3, matrix products, depth_conv(): lax.conv_general_dilated(window, kernel, (1,), 'VALID', dimension_numbers...  7.81 us
    all_to_all x1, waiting for transfers between devices, on_device(): lax.all_to_all(outgoing, 'zh', 0, 0, tiled=False)  2.19 us
    ppermute x1, starting transfers between devices, shifted(): lax.ppermute(block, SEQ, [(i, (i + distance) % size) for i in range(size)])  1.92 us
  transfers between devices with their start and end apart: 4, of which 3 were waited for; matrix products, arithmetic and copies ran while one was open for 21% of the time, Pallas kernels for 0%

profile of v4, /device:TPU:8, one launch (start us, length us, event | category | flops | bytes accessed | tf_op | source)
XLA Modules:
  0.0 79.6 jit_solution(12447786674933577277)
XLA Ops:
  0.0 0.8 compare_select_fusion.1
  0.8 0.7 fusion.46
  6.4 0.7 select_select_fusion.4
  7.1 0.7 broadcast_in_dim.89
  7.8 9.1 %all-to-all-start = ((bf16[4,4,8,512]{3,2,1,0:T(8,128)(2,1)}), bf16[4,4,8,512]{3,2,1,0:T(8,128)(2,1)S(1)}, u32[]{:S(2)}, u32[]{:S(2)}) async-start(bf16[4,4,8,512]{3,2,1,0:T(8,128)(2,1)} %broadcast_in_dim.89), calls=%async_computation | async-start | bytes 262144 | tf_op jit(solution)/shard_map/all_to_all | solution.py:21
  16.8 1.1 %multiply_convert_fusion = bf16[1,256,512]{2,1,0:T(8,128)(2,1)S(1)} fusion(bf16[5,256,512]{2,1,0:T(8,128)(2,1)} %param.7), kind=kLoop, calls=%fused_computation.7 | loop fusion | flops 524288 | bytes 786432 | tf_op jit(solution)/shard_map/convert_element_type | solution.py:64
  18.2 0.4 copy-done.5
  19.2 0.7 fusion.45
  19.9 0.7 fusion.30
  22.5 0.6 gather_fusion
  23.1 0.6 gather_fusion.1
  23.8 1.9 %collective-permute-start = (bf16[165,512]{1,0:T(8,128)(2,1)S(1)}, bf16[165,512]{1,0:T(8,128)(2,1)S(1)}, u32[]{:S(2)}, u32[]{:S(2)}) collective-permute-start(bf16[165,512]{1,0:T(8,128)(2,1)S(1)} %pad_maximum_fusion), channel_id=1, source_target_pairs={{0,16},{16,32},{32,48},{48,64},{64,80},{80,96},{96,112},{112,128},... | collective-permute-start | bytes 506888 | tf_op jit(solution)/shard_map/ppermute | solution.py:15
  25.8 9.8 %collective-permute-done = bf16[165,512]{1,0:T(8,128)(2,1)S(1)} collective-permute-done((bf16[165,512]{1,0:T(8,128)(2,1)S(1)}, bf16[165,512]{1,0:T(8,128)(2,1)S(1)}, u32[]{:S(2)}, u32[]{:S(2)}) %collective-permute-start) | collective-permute-done | bytes 168992 | tf_op jit(solution)/shard_map/ppermute | solution.py:15
  35.6 0.7 select_select_fusion
  36.3 14.7 %all-to-all-start.1 = ((bf16[4,2,8,512]{3,2,1,0:T(8,128)(2,1)}), bf16[4,2,8,512]{3,2,1,0:T(8,128)(2,1)S(1)}, u32[]{:S(2)}, u32[]{:S(2)}) async-start(bf16[4,2,8,512]{3,2,1,0:T(8,128)(2,1)} %select_select_fusion), calls=%async_computation.1 | async-start | bytes 131072 | tf_op jit(solution)/shard_map/all_to_all | solution.py:100
  51.0 0.6 slice_select_fusion.2
  52.3 0.7 fusion.24
  53.0 0.6 slice_select_fusion.1
  54.5 7.5 %fusion.1 = f32[2,128,512]{2,0,1:T(2,128)S(1)} fusion(bf16[1,255,512]{2,0,1:T(2,128)(2,1)S(1)} %copy.116, bf16[1,255,512]{2,0,1:T(2,128)(2,1)S(1)} %copy.115, bf16[128,1,512]{2,0,1:T(8,128)(2,1)S(1)} %bitcast.82), kind=kOutput, calls=%fused_computation.8 | convolution fusion | flops 34598912 | bytes 1177600 | tf_op jit(solution)/shard_map/conv_general_dilated | solution.py:27
  62.0 2.2 %all-to-all-done.1 = bf16[4,2,8,512]{3,2,1,0:T(8,128)(2,1)S(1)} async-done(((bf16[4,2,8,512]{3,2,1,0:T(8,128)(2,1)}), bf16[4,2,8,512]{3,2,1,0:T(8,128)(2,1)S(1)}, u32[]{:S(2)}, u32[]{:S(2)}) %all-to-all-start.1) | async-done | bytes 65568 | tf_op jit(solution)/shard_map/all_to_all | solution.py:100
  64.5 0.6 broadcast_in_dim.101
  65.1 5.2 %all-to-all-start.2 = ((f32[16,2,128,4]{2,3,1,0:T(4,128)}), f32[16,2,128,4]{2,3,1,0:T(4,128)S(1)}, u32[]{:S(2)}, u32[]{:S(2)}) async-start(f32[16,2,128,4]{2,3,1,0:T(4,128)} %broadcast_in_dim.101), calls=%async_computation.2 | async-start | bytes 131072 | tf_op jit(solution)/shard_map/all_to_all | solution.py:21
  70.4 8.1 %all-to-all-done.2 = f32[16,2,128,4]{2,3,1,0:T(4,128)S(1)} async-done(((f32[16,2,128,4]{2,3,1,0:T(4,128)}), f32[16,2,128,4]{2,3,1,0:T(4,128)S(1)}, u32[]{:S(2)}, u32[]{:S(2)}) %all-to-all-start.2) | async-done | bytes 65568 | tf_op jit(solution)/shard_map/all_to_all | solution.py:21
  78.6 1.0 %add_convert_fusion = bf16[2,128,512]{2,1,0:T(8,128)(2,1)} fusion(f32[2,512]{1,0:T(2,128)S(1)} %get-tuple-element.38, f32[2,128]{1,0:T(2,128)S(1)} %bitcast.86, f32[2,512]{1,0:T(2,128)S(1)} %get-tuple-element.39, f32[2,128]{1,0:T(2,128)S(1)} %bitcast.87, f32[2,512]{1,0:T(2,128)S(1)} %get-tuple-element.40, f32[2,128]{1,0:T(2,128)S(1)} %bitcast.88, ...), kind=kLoop, calls=%fused_computation.6 | loop fusion | flops 1703936 | bytes 1069056 | tf_op jit(solution)/shard_map/convert_element_type | solution.py:126
  (78 shorter events, 4.6 us)
Async XLA Ops:
  0.0 17.9 %copy-start = (bf16[5,256,512]{2,1,0:T(8,128)(2,1)S(1)}, bf16[5,256,512]{2,1,0:T(8,128)(2,1)}, u32[]{:S(2)}) copy-start(bf16[5,256,512]{2,1,0:T(8,128)(2,1)} %param.7) | copy-start | bytes 3932164
  7.8 15.9 %all-to-all-start = ((bf16[4,4,8,512]{3,2,1,0:T(8,128)(2,1)}), bf16[4,4,8,512]{3,2,1,0:T(8,128)(2,1)S(1)}, u32[]{:S(2)}, u32[]{:S(2)}) async-start(bf16[4,4,8,512]{3,2,1,0:T(8,128)(2,1)} %broadcast_in_dim.89), calls=%async_computation | async-start | bytes 262144 | tf_op jit(solution)/shard_map/all_to_all | solution.py:21
  18.0 0.7 copy-start.5
  18.0 1.2 %copy-start.4 = (s32[4]{0:T(128)S(1)}, s32[4]{0:T(128)}, u32[]{:S(2)}) copy-start(s32[4]{0:T(128)} %param.13) | copy-start | bytes 52
  18.1 2.7 %copy-start.2 = (bf16[7,512]{1,0:T(8,128)(2,1)S(1)}, bf16[7,512]{1,0:T(8,128)(2,1)}, u32[]{:S(2)}) copy-start(bf16[7,512]{1,0:T(8,128)(2,1)} %param.8) | copy-start | bytes 21508
  18.1 2.9 %copy-start.6 = (pred[8,17]{0,1:T(8,128)(4,1)S(1)}, pred[8,17]{0,1:T(8,128)(4,1)}, u32[]{:S(2)}) copy-start(pred[8,17]{0,1:T(8,128)(4,1)} %constant.99) | copy-start | bytes 412
  21.1 1.0 %copy-start.1 = (bf16[128,512]{1,0:T(8,128)(2,1)S(1)}, bf16[128,512]{1,0:T(8,128)(2,1)}, u32[]{:S(2)}) copy-start(bf16[128,512]{1,0:T(8,128)(2,1)} %param.9) | copy-start | bytes 393220
  21.1 1.2 %copy-start.3 = (f32[64,4]{0,1:T(4,128)S(1)}, f32[64,4]{0,1:T(4,128)}, u32[]{:S(2)}) copy-start(f32[64,4]{0,1:T(4,128)} %param.11) | copy-start | bytes 3076
  23.8 11.8 %collective-permute-start = (bf16[165,512]{1,0:T(8,128)(2,1)S(1)}, bf16[165,512]{1,0:T(8,128)(2,1)S(1)}, u32[]{:S(2)}, u32[]{:S(2)}) collective-permute-start(bf16[165,512]{1,0:T(8,128)(2,1)S(1)} %pad_maximum_fusion), channel_id=1, source_target_pairs={{0,16},{16,32},{32,48},{48,64},{64,80},{80,96},{96,112},{112,128},... | collective-permute-start | bytes 506888 | tf_op jit(solution)/shard_map/ppermute | solution.py:15
  36.3 27.9 %all-to-all-start.1 = ((bf16[4,2,8,512]{3,2,1,0:T(8,128)(2,1)}), bf16[4,2,8,512]{3,2,1,0:T(8,128)(2,1)S(1)}, u32[]{:S(2)}, u32[]{:S(2)}) async-start(bf16[4,2,8,512]{3,2,1,0:T(8,128)(2,1)} %select_select_fusion), calls=%async_computation.1 | async-start | bytes 131072 | tf_op jit(solution)/shard_map/all_to_all | solution.py:100
  65.1 13.4 %all-to-all-start.2 = ((f32[16,2,128,4]{2,3,1,0:T(4,128)}), f32[16,2,128,4]{2,3,1,0:T(4,128)S(1)}, u32[]{:S(2)}, u32[]{:S(2)}) async-start(f32[16,2,128,4]{2,3,1,0:T(4,128)} %broadcast_in_dim.101), calls=%async_computation.2 | async-start | bytes 131072 | tf_op jit(solution)/shard_map/all_to_all | solution.py:21

commit v5 on v4

--- a/solution.py
+++ b/solution.py
@@ -49,13 +49,9 @@
 
     held = edit_table.shape[0]
     owner_slot = seq_tenant - me * held
-    picked = []
-    for s in range(SEQS):
-        rows = jnp.zeros_like(edit_table[0])
-        for slot in range(held):
-            rows = jnp.where(owner_slot[s] == slot, edit_table[slot], rows)
-        picked.append(rows)
-    local_rows = jnp.stack(picked)
+    owned = (owner_slot >= 0) & (owner_slot < held)
+    local_rows = jnp.take(edit_table, jnp.clip(owner_slot, 0, held - 1), axis=0)
+    local_rows = jnp.where(owned[:, None, None], local_rows, jnp.zeros_like(local_rows))
     partial_rows = a2a_sum(local_rows, "y")
 
     first_gate = streams[0].astype(jnp.float32)

time: 80.2 us -> 74.2 us (0.925)
  between operations: 5.41 us -> 0.5 us
  transfers between devices with their start and end apart: 4 -> 4, of which waited for: 3 -> 3; matrix products, arithmetic and copies ran while one was open for 21% -> 23% of each run, Pallas kernels for 0% -> 0%
where the time goes in v5:
time: 74.2 us; the launch traced here: 73.7 us
  starting transfers between devices  30.9 us (42%)
  waiting for transfers between devices  20.1 us (27%)
  matrix products  8.02 us (11%)
  other arithmetic  7.63 us (10%)
  local copies, waits for them, and re-layouts  6.5 us (9%)
    all_to_all x1, starting transfers between devices, on_device(): lax.all_to_all(outgoing, 'zh', 0, 0, tiled=False)  14.7 us
    all_to_all x2, starting transfers between devices, a2a_sum(): return jnp.sum(lax.all_to_all(copies, axis, 0, 0, tiled=False), axis=0)  14.3 us
    ppermute x1, waiting for transfers between devices, shifted(): lax.ppermute(block, SEQ, [(i, (i + distance) % size) for i in range(size)])  9.79 us
    all_to_all x2, waiting for transfers between devices, a2a_sum(): return jnp.sum(lax.all_to_all(copies, axis, 0, 0, tiled=False), axis=0)  8.11 us
    conv_general_dilated x3, matrix products, depth_conv(): lax.conv_general_dilated(window, kernel, (1,), 'VALID', dimension_numbers...  7.81 us
    all_to_all x1, waiting for transfers between devices, on_device(): lax.all_to_all(outgoing, 'zh', 0, 0, tiled=False)  2.2 us
    ppermute x1, starting transfers between devices, shifted(): lax.ppermute(block, SEQ, [(i, (i + distance) % size) for i in range(size)])  1.92 us
  transfers between devices with their start and end apart: 4, of which 3 were waited for; matrix products, arithmetic and copies ran while one was open for 23% of the time, Pallas kernels for 0%

profile of v5, /device:TPU:8, one launch (start us, length us, event | category | flops | bytes accessed | tf_op | source)
XLA Modules:
  0.0 73.7 jit_solution(16740270814327866082)
XLA Ops:
  0.0 0.8 %compare_and_fusion = (pred[4]{0:T(512)(128)(4,1)S(1)}, pred[4]{0:T(512)(128)(4,1)S(1)}, pred[4]{0:T(512)(128)(4,1)S(1)}, s32[4]{0:T(128)S(1)}) fusion(s32[4]{0:T(128)} %param.13, s32[]{:T(128)S(6)} %mul.118), kind=kLoop, calls=%fused_computation.79 | loop fusion | flops 68 | bytes 48 | tf_op jit(solution)/shard_map/jit(_take)/and | solution.py:116
  0.8 0.5 gather_fusion
  1.4 0.7 broadcast_in_dim.118
  2.1 9.1 %all-to-all-start = ((bf16[4,4,8,512]{3,2,1,0:T(8,128)(2,1)}), bf16[4,4,8,512]{3,2,1,0:T(8,128)(2,1)S(1)}, u32[]{:S(2)}, u32[]{:S(2)}) async-start(bf16[4,4,8,512]{3,2,1,0:T(8,128)(2,1)} %broadcast_in_dim.118), calls=%async_computation | async-start | bytes 262144 | tf_op jit(solution)/shard_map/all_to_all | solution.py:21
  11.2 1.1 %multiply_convert_fusion = bf16[1,256,512]{2,1,0:T(8,128)(2,1)S(1)} fusion(bf16[5,256,512]{2,1,0:T(8,128)(2,1)} %param.7), kind=kLoop, calls=%fused_computation.8 | loop fusion | flops 524288 | bytes 786432 | tf_op jit(solution)/shard_map/convert_element_type | solution.py:60
  12.5 0.4 copy-done.6
  13.6 0.6 fusion.45
  14.1 0.6 fusion.30
  16.6 0.6 gather_fusion.1
  17.2 0.6 gather_fusion.2
  17.9 1.9 %collective-permute-start = (bf16[165,512]{1,0:T(8,128)(2,1)S(1)}, bf16[165,512]{1,0:T(8,128)(2,1)S(1)}, u32[]{:S(2)}, u32[]{:S(2)}) collective-permute-start(bf16[165,512]{1,0:T(8,128)(2,1)S(1)} %pad_maximum_fusion), channel_id=1, source_target_pairs={{0,16},{16,32},{32,48},{48,64},{64,80},{80,96},{96,112},{112,128},... | collective-permute-start | bytes 506888 | tf_op jit(solution)/shard_map/ppermute | solution.py:15
  19.9 9.8 %collective-permute-done = bf16[165,512]{1,0:T(8,128)(2,1)S(1)} collective-permute-done((bf16[165,512]{1,0:T(8,128)(2,1)S(1)}, bf16[165,512]{1,0:T(8,128)(2,1)S(1)}, u32[]{:S(2)}, u32[]{:S(2)}) %collective-permute-start) | collective-permute-done | bytes 168992 | tf_op jit(solution)/shard_map/ppermute | solution.py:15
  29.7 0.7 %select_select_fusion = bf16[4,2,8,512]{3,2,1,0:T(8,128)(2,1)} fusion(pred[4,2]{1,0:T(4,128)(4,1)S(1)} %copy.122, pred[4,2]{1,0:T(4,128)(4,1)S(1)} %copy.121, pred[4,2]{1,0:T(4,128)(4,1)S(1)} %copy.120, pred[4,2]{1,0:T(4,128)(4,1)S(1)} %copy.119, bf16[8,512]{1,0:T(8,128)(2,1)S(1)} %get-tuple-element.13, bf16[8,512]{1,0:T(8,128)(2,1)S(1)} %get-tuple-element.14, ...), kind=kLoop, calls=%fused_computation.50 | loop fusion | flops 131072 | bytes 98336 | tf_op jit(solution)/shard_map/jit(_where)/select_n | solution.py:95
  30.4 14.7 %all-to-all-start.1 = ((bf16[4,2,8,512]{3,2,1,0:T(8,128)(2,1)}), bf16[4,2,8,512]{3,2,1,0:T(8,128)(2,1)S(1)}, u32[]{:S(2)}, u32[]{:S(2)}) async-start(bf16[4,2,8,512]{3,2,1,0:T(8,128)(2,1)} %select_select_fusion), calls=%async_computation.1 | async-start | bytes 131072 | tf_op jit(solution)/shard_map/all_to_all | solution.py:96
  45.2 0.6 slice_select_fusion.2
  46.5 0.6 fusion.24
  47.1 0.7 slice_select_fusion.1
  47.8 0.4 copy.115
  48.7 7.5 %fusion.1 = f32[2,128,512]{2,0,1:T(2,128)S(1)} fusion(bf16[1,255,512]{2,0,1:T(2,128)(2,1)S(1)} %copy.116, bf16[1,255,512]{2,0,1:T(2,128)(2,1)S(1)} %copy.115, bf16[128,1,512]{2,0,1:T(8,128)(2,1)S(1)} %bitcast.74), kind=kOutput, calls=%fused_computation.9 | convolution fusion | flops 34598912 | bytes 1177600 | tf_op jit(solution)/shard_map/conv_general_dilated | solution.py:27
  56.1 2.2 %all-to-all-done.1 = bf16[4,2,8,512]{3,2,1,0:T(8,128)(2,1)S(1)} async-done(((bf16[4,2,8,512]{3,2,1,0:T(8,128)(2,1)}), bf16[4,2,8,512]{3,2,1,0:T(8,128)(2,1)S(1)}, u32[]{:S(2)}, u32[]{:S(2)}) %all-to-all-start.1) | async-done | bytes 65568 | tf_op jit(solution)/shard_map/all_to_all | solution.py:96
  58.6 0.6 broadcast_in_dim.130
  59.3 5.2 %all-to-all-start.2 = ((f32[16,2,128,4]{2,3,1,0:T(4,128)}), f32[16,2,128,4]{2,3,1,0:T(4,128)S(1)}, u32[]{:S(2)}, u32[]{:S(2)}) async-start(f32[16,2,128,4]{2,3,1,0:T(4,128)} %broadcast_in_dim.130), calls=%async_computation.2 | async-start | bytes 131072 | tf_op jit(solution)/shard_map/all_to_all | solution.py:21
  64.5 8.1 %all-to-all-done.2 = f32[16,2,128,4]{2,3,1,0:T(4,128)S(1)} async-done(((f32[16,2,128,4]{2,3,1,0:T(4,128)}), f32[16,2,128,4]{2,3,1,0:T(4,128)S(1)}, u32[]{:S(2)}, u32[]{:S(2)}) %all-to-all-start.2) | async-done | bytes 65568 | tf_op jit(solution)/shard_map/all_to_all | solution.py:21
  72.7 1.0 %add_convert_fusion = bf16[2,128,512]{2,1,0:T(8,128)(2,1)} fusion(f32[2,512]{1,0:T(2,128)S(1)} %get-tuple-element.34, f32[2,128]{1,0:T(2,128)S(1)} %bitcast.78, f32[2,512]{1,0:T(2,128)S(1)} %get-tuple-element.35, f32[2,128]{1,0:T(2,128)S(1)} %bitcast.79, f32[2,512]{1,0:T(2,128)S(1)} %get-tuple-element.36, f32[2,128]{1,0:T(2,128)S(1)} %bitcast.80, ...), kind=kLoop, calls=%fused_computation.7 | loop fusion | flops 1703936 | bytes 1069056 | tf_op jit(solution)/shard_map/convert_element_type | solution.py:122
  (80 shorter events, 4.3 us)
Async XLA Ops:
  0.0 0.8 %copy-start = (bf16[2,8,512]{2,1,0:T(8,128)(2,1)S(1)}, bf16[2,8,512]{2,1,0:T(8,128)(2,1)}, u32[]{:S(2)}) copy-start(bf16[2,8,512]{2,1,0:T(8,128)(2,1)} %param.10) | copy-start | bytes 49156
  0.0 12.3 %copy-start.1 = (bf16[5,256,512]{2,1,0:T(8,128)(2,1)S(1)}, bf16[5,256,512]{2,1,0:T(8,128)(2,1)}, u32[]{:S(2)}) copy-start(bf16[5,256,512]{2,1,0:T(8,128)(2,1)} %param.7) | copy-start | bytes 3932164
  2.1 15.7 %all-to-all-start = ((bf16[4,4,8,512]{3,2,1,0:T(8,128)(2,1)}), bf16[4,4,8,512]{3,2,1,0:T(8,128)(2,1)S(1)}, u32[]{:S(2)}, u32[]{:S(2)}) async-start(bf16[4,4,8,512]{3,2,1,0:T(8,128)(2,1)} %broadcast_in_dim.118), calls=%async_computation | async-start | bytes 262144 | tf_op jit(solution)/shard_map/all_to_all | solution.py:21
  12.3 0.7 copy-start.6
  12.3 1.2 %copy-start.5 = (s32[4]{0:T(128)S(1)}, s32[4]{0:T(128)}, u32[]{:S(2)}) copy-start(s32[4]{0:T(128)} %param.13) | copy-start | bytes 52
  12.4 2.5 %copy-start.3 = (bf16[7,512]{1,0:T(8,128)(2,1)S(1)}, bf16[7,512]{1,0:T(8,128)(2,1)}, u32[]{:S(2)}) copy-start(bf16[7,512]{1,0:T(8,128)(2,1)} %param.8) | copy-start | bytes 21508
  12.4 2.6 %copy-start.7 = (pred[8,17]{0,1:T(8,128)(4,1)S(1)}, pred[8,17]{0,1:T(8,128)(4,1)}, u32[]{:S(2)}) copy-start(pred[8,17]{0,1:T(8,128)(4,1)} %constant.103) | copy-start | bytes 412
  15.3 1.0 %copy-start.2 = (bf16[128,512]{1,0:T(8,128)(2,1)S(1)}, bf16[128,512]{1,0:T(8,128)(2,1)}, u32[]{:S(2)}) copy-start(bf16[128,512]{1,0:T(8,128)(2,1)} %param.9) | copy-start | bytes 393220
  15.3 1.2 %copy-start.4 = (f32[64,4]{0,1:T(4,128)S(1)}, f32[64,4]{0,1:T(4,128)}, u32[]{:S(2)}) copy-start(f32[64,4]{0,1:T(4,128)} %param.11) | copy-start | bytes 3076
  17.9 11.8 %collective-permute-start = (bf16[165,512]{1,0:T(8,128)(2,1)S(1)}, bf16[165,512]{1,0:T(8,128)(2,1)S(1)}, u32[]{:S(2)}, u32[]{:S(2)}) collective-permute-start(bf16[165,512]{1,0:T(8,128)(2,1)S(1)} %pad_maximum_fusion), channel_id=1, source_target_pairs={{0,16},{16,32},{32,48},{48,64},{64,80},{80,96},{96,112},{112,128},... | collective-permute-start | bytes 506888 | tf_op jit(solution)/shard_map/ppermute | solution.py:15
  30.4 27.9 %all-to-all-start.1 = ((bf16[4,2,8,512]{3,2,1,0:T(8,128)(2,1)}), bf16[4,2,8,512]{3,2,1,0:T(8,128)(2,1)S(1)}, u32[]{:S(2)}, u32[]{:S(2)}) async-start(bf16[4,2,8,512]{3,2,1,0:T(8,128)(2,1)} %select_select_fusion), calls=%async_computation.1 | async-start | bytes 131072 | tf_op jit(solution)/shard_map/all_to_all | solution.py:96
  59.3 13.4 %all-to-all-start.2 = ((f32[16,2,128,4]{2,3,1,0:T(4,128)}), f32[16,2,128,4]{2,3,1,0:T(4,128)S(1)}, u32[]{:S(2)}, u32[]{:S(2)}) async-start(f32[16,2,128,4]{2,3,1,0:T(4,128)} %broadcast_in_dim.130), calls=%async_computation.2 | async-start | bytes 131072 | tf_op jit(solution)/shard_map/all_to_all | solution.py:21

commit v6 on v5

--- a/solution.py
+++ b/solution.py
@@ -52,7 +52,7 @@
     owned = (owner_slot >= 0) & (owner_slot < held)
     local_rows = jnp.take(edit_table, jnp.clip(owner_slot, 0, held - 1), axis=0)
     local_rows = jnp.where(owned[:, None, None], local_rows, jnp.zeros_like(local_rows))
-    partial_rows = a2a_sum(local_rows, "y")
+    partial_rows = local_rows
 
     first_gate = streams[0].astype(jnp.float32)
     second_gate = streams[3].astype(jnp.float32)
@@ -85,7 +85,7 @@
     sent = shifted(sent, 1)
     short_border = sent[: short_reach - 1]
     long_border = sent[short_reach - 1 : border.shape[0]]
-    chosen = partial_rows + sent[border.shape[0] :].reshape(partial_rows.shape)
+    chosen = a2a_sum(partial_rows + sent[border.shape[0] :].reshape(partial_rows.shape), "y")
     zh_size = lax.axis_size("zh")
     peer = me + (jnp.arange(zh_size, dtype=jnp.int32) - lax.axis_index("zh")) * lax.axis_size("core")
     peer_tiles = peer[:, None] * tile_count + jnp.arange(tile_count, dtype=jnp.int32)[None, :]

time: 74.2 us -> 76.5 us (1.031)
  the two profiles are of different devices: /device:TPU:8 before, /device:TPU:2 now
where the time goes in v6:
time: 76.5 us; the launch traced here: 76.1 us
  waiting for transfers between devices  28.3 us (37%)
  starting transfers between devices  24.4 us (32%)
  other arithmetic  8.16 us (11%)
  matrix products  8 us (10%)
  local copies, waits for them, and re-layouts  6.67 us (9%)
    all_to_all x1, starting transfers between devices, on_device(): lax.all_to_all(outgoing, 'zh', 0, 0, tiled=False)  14.2 us
    ppermute x1, waiting for transfers between devices, shifted(): lax.ppermute(block, SEQ, [(i, (i + distance) % size) for i in range(size)])  13.6 us
    all_to_all x2, waiting for transfers between devices, a2a_sum(): return jnp.sum(lax.all_to_all(copies, axis, 0, 0, tiled=False), axis=0)  9.16 us
    all_to_all x2, starting transfers between devices, a2a_sum(): return jnp.sum(lax.all_to_all(copies, axis, 0, 0, tiled=False), axis=0)  8.35 us
    conv_general_dilated x3, matrix products, depth_conv(): lax.conv_general_dilated(window, kernel, (1,), 'VALID', dimension_numbers...  7.8 us
    all_to_all x1, waiting for transfers between devices, on_device(): lax.all_to_all(outgoing, 'zh', 0, 0, tiled=False)  5.54 us
    ppermute x1, starting transfers between devices, shifted(): lax.ppermute(block, SEQ, [(i, (i + distance) % size) for i in range(size)])  1.92 us
  transfers between devices with their start and end apart: 4, of which 4 were waited for; matrix products, arithmetic and copies ran while one was open for 17% of the time, Pallas kernels for 0%

profile of v6, /device:TPU:2, one launch (start us, length us, event | category | flops | bytes accessed | tf_op | source)
XLA Modules:
  0.0 76.1 jit_solution(5106097899040202441)
XLA Ops:
  0.0 1.1 %multiply_convert_fusion = bf16[1,256,512]{2,1,0:T(8,128)(2,1)S(1)} fusion(bf16[5,256,512]{2,1,0:T(8,128)(2,1)} %param.7), kind=kLoop, calls=%fused_computation.8 | loop fusion | flops 524288 | bytes 786432 | tf_op jit(solution)/shard_map/convert_element_type | solution.py:60
  1.1 1.2 %fusion.43 = (bf16[1,256,512]{2,1,0:T(8,128)(2,1)S(1)}, f32[1,256,512]{2,1,0:T(8,128)S(1)}, f32[1,256,512]{2,1,0:T(8,128)S(1)}) fusion(bf16[5,256,512]{2,1,0:T(8,128)(2,1)} %param.7), kind=kLoop, calls=%fused_computation.106 | loop fusion | flops 262144 | bytes 2097152 | tf_op jit(solution)/shard_map/slice | solution.py:58
  2.8 0.6 fusion.46
  3.4 0.6 fusion.31
  5.6 0.6 gather_fusion
  6.3 1.9 %collective-permute-start = (bf16[165,512]{1,0:T(8,128)(2,1)S(1)}, bf16[165,512]{1,0:T(8,128)(2,1)S(1)}, u32[]{:S(2)}, u32[]{:S(2)}) collective-permute-start(bf16[165,512]{1,0:T(8,128)(2,1)S(1)} %pad_maximum_fusion), channel_id=1, source_target_pairs={{0,16},{16,32},{32,48},{48,64},{64,80},{80,96},{96,112},{112,128},... | collective-permute-start | bytes 506888 | tf_op jit(solution)/shard_map/ppermute | solution.py:15
  9.4 0.6 gather_fusion.1
  10.1 0.6 gather_fusion.2
  10.7 13.6 %collective-permute-done = bf16[165,512]{1,0:T(8,128)(2,1)S(1)} collective-permute-done((bf16[165,512]{1,0:T(8,128)(2,1)S(1)}, bf16[165,512]{1,0:T(8,128)(2,1)S(1)}, u32[]{:S(2)}, u32[]{:S(2)}) %collective-permute-start) | collective-permute-done | bytes 168992 | tf_op jit(solution)/shard_map/ppermute | solution.py:15
  24.4 0.7 broadcast_in_dim.145
  25.1 3.3 %all-to-all-start = ((bf16[4,4,8,512]{3,2,1,0:T(8,128)(2,1)}), bf16[4,4,8,512]{3,2,1,0:T(8,128)(2,1)S(1)}, u32[]{:S(2)}, u32[]{:S(2)}) async-start(bf16[4,4,8,512]{3,2,1,0:T(8,128)(2,1)} %broadcast_in_dim.145), calls=%async_computation | async-start | bytes 262144 | tf_op jit(solution)/shard_map/all_to_all | solution.py:21
  28.4 0.6 slice_select_fusion.2
  29.7 0.7 fusion.24
  30.4 0.6 slice_select_fusion.1
  31.1 0.4 copy.115
  31.9 2.4 %all-to-all-done = bf16[4,4,8,512]{3,2,1,0:T(8,128)(2,1)S(1)} async-done(((bf16[4,4,8,512]{3,2,1,0:T(8,128)(2,1)}), bf16[4,4,8,512]{3,2,1,0:T(8,128)(2,1)S(1)}, u32[]{:S(2)}, u32[]{:S(2)}) %all-to-all-start) | async-done | bytes 131104 | tf_op jit(solution)/shard_map/all_to_all | solution.py:21
  34.4 0.7 select_select_fusion
  35.1 14.2 %all-to-all-start.1 = ((bf16[4,2,8,512]{3,2,1,0:T(8,128)(2,1)}), bf16[4,2,8,512]{3,2,1,0:T(8,128)(2,1)S(1)}, u32[]{:S(2)}, u32[]{:S(2)}) async-start(bf16[4,2,8,512]{3,2,1,0:T(8,128)(2,1)} %select_select_fusion), calls=%async_computation.1 | async-start | bytes 131072 | tf_op jit(solution)/shard_map/all_to_all | solution.py:96
  49.3 7.5 %fusion.1 = f32[2,128,512]{2,0,1:T(2,128)S(1)} fusion(bf16[1,255,512]{2,0,1:T(2,128)(2,1)S(1)} %copy.116, bf16[1,255,512]{2,0,1:T(2,128)(2,1)S(1)} %copy.115, bf16[128,1,512]{2,0,1:T(8,128)(2,1)S(1)} %bitcast.76), kind=kOutput, calls=%fused_computation.9 | convolution fusion | flops 34598912 | bytes 1177600 | tf_op jit(solution)/shard_map/conv_general_dilated | solution.py:27
  56.8 5.5 %all-to-all-done.1 = bf16[4,2,8,512]{3,2,1,0:T(8,128)(2,1)S(1)} async-done(((bf16[4,2,8,512]{3,2,1,0:T(8,128)(2,1)}), bf16[4,2,8,512]{3,2,1,0:T(8,128)(2,1)S(1)}, u32[]{:S(2)}, u32[]{:S(2)}) %all-to-all-start.1) | async-done | bytes 65568 | tf_op jit(solution)/shard_map/all_to_all | solution.py:96
  62.6 0.6 broadcast_in_dim.154
  63.2 5.0 %all-to-all-start.2 = ((f32[16,2,128,4]{2,3,1,0:T(4,128)}), f32[16,2,128,4]{2,3,1,0:T(4,128)S(1)}, u32[]{:S(2)}, u32[]{:S(2)}) async-start(f32[16,2,128,4]{2,3,1,0:T(4,128)} %broadcast_in_dim.154), calls=%async_computation.2 | async-start | bytes 131072 | tf_op jit(solution)/shard_map/all_to_all | solution.py:21
  68.2 6.8 %all-to-all-done.2 = f32[16,2,128,4]{2,3,1,0:T(4,128)S(1)} async-done(((f32[16,2,128,4]{2,3,1,0:T(4,128)}), f32[16,2,128,4]{2,3,1,0:T(4,128)S(1)}, u32[]{:S(2)}, u32[]{:S(2)}) %all-to-all-start.2) | async-done | bytes 65568 | tf_op jit(solution)/shard_map/all_to_all | solution.py:21
  75.1 1.0 %add_convert_fusion = bf16[2,128,512]{2,1,0:T(8,128)(2,1)} fusion(f32[2,512]{1,0:T(2,128)S(1)} %get-tuple-element.34, f32[2,128]{1,0:T(2,128)S(1)} %bitcast.80, f32[2,512]{1,0:T(2,128)S(1)} %get-tuple-element.35, f32[2,128]{1,0:T(2,128)S(1)} %bitcast.81, f32[2,512]{1,0:T(2,128)S(1)} %get-tuple-element.36, f32[2,128]{1,0:T(2,128)S(1)} %bitcast.82, ...), kind=kLoop, calls=%fused_computation.7 | loop fusion | flops 1703936 | bytes 1069056 | tf_op jit(solution)/shard_map/convert_element_type | solution.py:122
  (82 shorter events, 4.8 us)
Async XLA Ops:
  0.0 5.6 %copy-start = (bf16[2,8,512]{2,1,0:T(8,128)(2,1)S(1)}, bf16[2,8,512]{2,1,0:T(8,128)(2,1)}, u32[]{:S(2)}) copy-start(bf16[2,8,512]{2,1,0:T(8,128)(2,1)} %param.10) | copy-start | bytes 49156
  1.1 1.3 %copy-start.5 = (s32[4]{0:T(128)S(1)}, s32[4]{0:T(128)}, u32[]{:S(2)}) copy-start(s32[4]{0:T(128)} %param.12) | copy-start | bytes 52
  2.3 1.9 %copy-start.2 = (bf16[7,512]{1,0:T(8,128)(2,1)S(1)}, bf16[7,512]{1,0:T(8,128)(2,1)}, u32[]{:S(2)}) copy-start(bf16[7,512]{1,0:T(8,128)(2,1)} %param.8) | copy-start | bytes 21508
  2.4 2.1 %copy-start.6 = (pred[8,17]{0,1:T(8,128)(4,1)S(1)}, pred[8,17]{0,1:T(8,128)(4,1)}, u32[]{:S(2)}) copy-start(pred[8,17]{0,1:T(8,128)(4,1)} %constant.103) | copy-start | bytes 412
  4.6 0.7 copy-start.4
  4.8 4.3 %copy-start.1 = (bf16[128,512]{1,0:T(8,128)(2,1)S(1)}, bf16[128,512]{1,0:T(8,128)(2,1)}, u32[]{:S(2)}) copy-start(bf16[128,512]{1,0:T(8,128)(2,1)} %param.9) | copy-start | bytes 393220
  4.8 4.5 %copy-start.3 = (f32[64,4]{0,1:T(4,128)S(1)}, f32[64,4]{0,1:T(4,128)}, u32[]{:S(2)}) copy-start(f32[64,4]{0,1:T(4,128)} %param.11) | copy-start | bytes 3076
  6.3 18.0 %collective-permute-start = (bf16[165,512]{1,0:T(8,128)(2,1)S(1)}, bf16[165,512]{1,0:T(8,128)(2,1)S(1)}, u32[]{:S(2)}, u32[]{:S(2)}) collective-permute-start(bf16[165,512]{1,0:T(8,128)(2,1)S(1)} %pad_maximum_fusion), channel_id=1, source_target_pairs={{0,16},{16,32},{32,48},{48,64},{64,80},{80,96},{96,112},{112,128},... | collective-permute-start | bytes 506888 | tf_op jit(solution)/shard_map/ppermute | solution.py:15
  25.1 9.3 %all-to-all-start = ((bf16[4,4,8,512]{3,2,1,0:T(8,128)(2,1)}), bf16[4,4,8,512]{3,2,1,0:T(8,128)(2,1)S(1)}, u32[]{:S(2)}, u32[]{:S(2)}) async-start(bf16[4,4,8,512]{3,2,1,0:T(8,128)(2,1)} %broadcast_in_dim.145), calls=%async_computation | async-start | bytes 262144 | tf_op jit(solution)/shard_map/all_to_all | solution.py:21
  35.1 27.2 %all-to-all-start.1 = ((bf16[4,2,8,512]{3,2,1,0:T(8,128)(2,1)}), bf16[4,2,8,512]{3,2,1,0:T(8,128)(2,1)S(1)}, u32[]{:S(2)}, u32[]{:S(2)}) async-start(bf16[4,2,8,512]{3,2,1,0:T(8,128)(2,1)} %select_select_fusion), calls=%async_computation.1 | async-start | bytes 131072 | tf_op jit(solution)/shard_map/all_to_all | solution.py:96
  63.2 11.8 %all-to-all-start.2 = ((f32[16,2,128,4]{2,3,1,0:T(4,128)}), f32[16,2,128,4]{2,3,1,0:T(4,128)S(1)}, u32[]{:S(2)}, u32[]{:S(2)}) async-start(f32[16,2,128,4]{2,3,1,0:T(4,128)} %broadcast_in_dim.154), calls=%async_computation.2 | async-start | bytes 131072 | tf_op jit(solution)/shard_map/all_to_all | solution.py:21

commit v7 on v6

--- a/solution.py
+++ b/solution.py
@@ -85,15 +85,15 @@
     sent = shifted(sent, 1)
     short_border = sent[: short_reach - 1]
     long_border = sent[short_reach - 1 : border.shape[0]]
-    chosen = a2a_sum(partial_rows + sent[border.shape[0] :].reshape(partial_rows.shape), "y")
-    zh_size = lax.axis_size("zh")
-    peer = me + (jnp.arange(zh_size, dtype=jnp.int32) - lax.axis_index("zh")) * lax.axis_size("core")
+    chosen = partial_rows + sent[border.shape[0] :].reshape(partial_rows.shape)
+    zh_size = lax.axis_size(SEQ[:2])
+    peer = jnp.arange(zh_size, dtype=jnp.int32) * lax.axis_size("core") + lax.axis_index("core")
     peer_tiles = peer[:, None] * tile_count + jnp.arange(tile_count, dtype=jnp.int32)[None, :]
     peer_seq = jnp.sum((seq_ends[None, None, :] <= peer_tiles[:, :, None]).astype(jnp.int32), axis=2)
     outgoing = jnp.zeros((zh_size, tile_count) + chosen.shape[1:], chosen.dtype)
     for s in range(SEQS):
         outgoing = jnp.where((peer_seq == s)[:, :, None, None], chosen[s], outgoing)
-    tile_rows = jnp.sum(lax.all_to_all(outgoing, "zh", 0, 0, tiled=False), axis=0)
+    tile_rows = jnp.sum(lax.all_to_all(outgoing, SEQ[:2], 0, 0, tiled=False), axis=0)
 
     first_out = depth_conv(short_window(0, short_border)[None], short_filter)[0]
     carried = [carried_of(0, first_out)] + carried_later

time: 76.5 us -> 74.3 us (0.971)
  the two profiles are of different devices: /device:TPU:2 before, /device:TPU:8 now
where the time goes in v7:
time: 74.3 us; the launch traced here: 73.9 us
  starting transfers between devices  26.8 us (36%)
  waiting for transfers between devices  24.5 us (33%)
  other arithmetic  8.12 us (11%)
  matrix products  8.02 us (11%)
  local copies, waits for them, and re-layouts  5.95 us (8%)
    all_to_all x1, starting transfers between devices, on_device(): lax.all_to_all(outgoing, SEQ[:2], 0, 0, tiled=False)  18.7 us
    ppermute x1, waiting for transfers between devices, shifted(): lax.ppermute(block, SEQ, [(i, (i + distance) % size) for i in range(size)])  11.2 us
    all_to_all x1, waiting for transfers between devices, a2a_sum(): return jnp.sum(lax.all_to_all(copies, axis, 0, 0, tiled=False), axis=0)  8.11 us
    conv_general_dilated x3, matrix products, depth_conv(): lax.conv_general_dilated(window, kernel, (1,), 'VALID', dimension_numbers...  7.81 us
    all_to_all x1, starting transfers between devices, a2a_sum(): return jnp.sum(lax.all_to_all(copies, axis, 0, 0, tiled=False), axis=0)  6.22 us
    all_to_all x1, waiting for transfers between devices, on_device(): lax.all_to_all(outgoing, SEQ[:2], 0, 0, tiled=False)  5.21 us
    ppermute x1, starting transfers between devices, shifted(): lax.ppermute(block, SEQ, [(i, (i + distance) % size) for i in range(size)])  1.92 us
  transfers between devices with their start and end apart: 3, of which 3 were waited for; matrix products, arithmetic and copies ran while one was open for 18% of the time, Pallas kernels for 0%

profile of v7, /device:TPU:8, one launch (start us, length us, event | category | flops | bytes accessed | tf_op | source)
XLA Modules:
  0.0 73.9 jit_solution(9433504908047304377)
XLA Ops:
  0.0 1.1 %multiply_convert_fusion = bf16[1,256,512]{2,1,0:T(8,128)(2,1)S(1)} fusion(bf16[5,256,512]{2,1,0:T(8,128)(2,1)} %param.7), kind=kLoop, calls=%fused_computation.8 | loop fusion | flops 524288 | bytes 786432 | tf_op jit(solution)/shard_map/convert_element_type | solution.py:60
  1.1 1.2 %fusion.43 = (bf16[1,256,512]{2,1,0:T(8,128)(2,1)S(1)}, f32[1,256,512]{2,1,0:T(8,128)S(1)}, f32[1,256,512]{2,1,0:T(8,128)S(1)}) fusion(bf16[5,256,512]{2,1,0:T(8,128)(2,1)} %param.7), kind=kLoop, calls=%fused_computation.106 | loop fusion | flops 262144 | bytes 2097152 | tf_op jit(solution)/shard_map/slice | solution.py:58
  2.8 0.6 fusion.46
  3.4 0.6 fusion.31
  4.9 0.3 copy-done.4
  5.5 0.6 gather_fusion
  6.2 1.9 %collective-permute-start = (bf16[165,512]{1,0:T(8,128)(2,1)S(1)}, bf16[165,512]{1,0:T(8,128)(2,1)S(1)}, u32[]{:S(2)}, u32[]{:S(2)}) collective-permute-start(bf16[165,512]{1,0:T(8,128)(2,1)S(1)} %pad_maximum_fusion), channel_id=1, source_target_pairs={{0,16},{16,32},{32,48},{48,64},{64,80},{80,96},{96,112},{112,128},... | collective-permute-start | bytes 506888 | tf_op jit(solution)/shard_map/ppermute | solution.py:15
  9.2 0.6 gather_fusion.1
  9.8 0.6 gather_fusion.2
  10.5 11.2 %collective-permute-done = bf16[165,512]{1,0:T(8,128)(2,1)S(1)} collective-permute-done((bf16[165,512]{1,0:T(8,128)(2,1)S(1)}, bf16[165,512]{1,0:T(8,128)(2,1)S(1)}, u32[]{:S(2)}, u32[]{:S(2)}) %collective-permute-start) | collective-permute-done | bytes 168992 | tf_op jit(solution)/shard_map/ppermute | solution.py:15
  21.8 0.9 %select_select_fusion = bf16[16,2,8,512]{3,2,1,0:T(8,128)(2,1)} fusion(pred[16,2]{1,0:T(8,128)(4,1)S(1)} %copy.122, pred[16,2]{1,0:T(8,128)(4,1)S(1)} %copy.121, pred[16,2]{1,0:T(8,128)(4,1)S(1)} %copy.120, pred[16,2]{1,0:T(8,128)(4,1)S(1)} %copy.119, bf16[8,512]{1,0:T(8,128)(2,1)S(1)} %get-tuple-element.13, bf16[8,512]{1,0:T(8,128)(2,1)S(1)} %get-tuple-element.14, ...), kind=kLoop, calls=%fused_computation.27 | loop fusion | flops 524288 | bytes 295040 | tf_op jit(solution)/shard_map/jit(_where)/select_n | solution.py:95
  22.7 18.7 %all-to-all-start = ((bf16[16,2,8,512]{3,2,1,0:T(8,128)(2,1)}), bf16[16,2,8,512]{3,2,1,0:T(8,128)(2,1)S(1)}, u32[]{:S(2)}, u32[]{:S(2)}) async-start(bf16[16,2,8,512]{3,2,1,0:T(8,128)(2,1)} %select_select_fusion), calls=%async_computation | async-start | bytes 524288 | tf_op jit(solution)/shard_map/all_to_all | solution.py:96
  41.3 0.6 slice_select_fusion.2
  42.7 0.6 fusion.24
  43.3 0.7 slice_select_fusion.1
  44.0 0.4 copy.115
  44.4 0.4 copy.116
  44.8 7.5 %fusion.1 = f32[2,128,512]{2,0,1:T(2,128)S(1)} fusion(bf16[1,255,512]{2,0,1:T(2,128)(2,1)S(1)} %copy.116, bf16[1,255,512]{2,0,1:T(2,128)(2,1)S(1)} %copy.115, bf16[128,1,512]{2,0,1:T(8,128)(2,1)S(1)} %bitcast.76), kind=kOutput, calls=%fused_computation.9 | convolution fusion | flops 34598912 | bytes 1177600 | tf_op jit(solution)/shard_map/conv_general_dilated | solution.py:27
  52.3 5.2 %all-to-all-done = bf16[16,2,8,512]{3,2,1,0:T(8,128)(2,1)S(1)} async-done(((bf16[16,2,8,512]{3,2,1,0:T(8,128)(2,1)}), bf16[16,2,8,512]{3,2,1,0:T(8,128)(2,1)S(1)}, u32[]{:S(2)}, u32[]{:S(2)}) %all-to-all-start) | async-done | bytes 262176 | tf_op jit(solution)/shard_map/all_to_all | solution.py:96
  57.6 0.2 fusion.41
  57.8 0.6 broadcast_in_dim.147
  58.5 6.2 %all-to-all-start.1 = ((f32[16,2,128,4]{2,3,1,0:T(4,128)}), f32[16,2,128,4]{2,3,1,0:T(4,128)S(1)}, u32[]{:S(2)}, u32[]{:S(2)}) async-start(f32[16,2,128,4]{2,3,1,0:T(4,128)} %broadcast_in_dim.147), calls=%async_computation.1 | async-start | bytes 131072 | tf_op jit(solution)/shard_map/all_to_all | solution.py:21
  64.7 8.1 %all-to-all-done.1 = f32[16,2,128,4]{2,3,1,0:T(4,128)S(1)} async-done(((f32[16,2,128,4]{2,3,1,0:T(4,128)}), f32[16,2,128,4]{2,3,1,0:T(4,128)S(1)}, u32[]{:S(2)}, u32[]{:S(2)}) %all-to-all-start.1) | async-done | bytes 65568 | tf_op jit(solution)/shard_map/all_to_all | solution.py:21
  73.0 1.0 %add_convert_fusion = bf16[2,128,512]{2,1,0:T(8,128)(2,1)} fusion(f32[2,512]{1,0:T(2,128)S(1)} %get-tuple-element.34, f32[2,128]{1,0:T(2,128)S(1)} %bitcast.80, f32[2,512]{1,0:T(2,128)S(1)} %get-tuple-element.35, f32[2,128]{1,0:T(2,128)S(1)} %bitcast.81, f32[2,512]{1,0:T(2,128)S(1)} %get-tuple-element.36, f32[2,128]{1,0:T(2,128)S(1)} %bitcast.82, ...), kind=kLoop, calls=%fused_computation.7 | loop fusion | flops 1703936 | bytes 1069056 | tf_op jit(solution)/shard_map/convert_element_type | solution.py:122
  (78 shorter events, 3.8 us)
Async XLA Ops:
  0.0 5.5 %copy-start = (bf16[2,8,512]{2,1,0:T(8,128)(2,1)S(1)}, bf16[2,8,512]{2,1,0:T(8,128)(2,1)}, u32[]{:S(2)}) copy-start(bf16[2,8,512]{2,1,0:T(8,128)(2,1)} %param.10) | copy-start | bytes 49156
  1.1 1.3 %copy-start.5 = (s32[4]{0:T(128)S(1)}, s32[4]{0:T(128)}, u32[]{:S(2)}) copy-start(s32[4]{0:T(128)} %param.12) | copy-start | bytes 52
  2.3 1.8 %copy-start.2 = (bf16[7,512]{1,0:T(8,128)(2,1)S(1)}, bf16[7,512]{1,0:T(8,128)(2,1)}, u32[]{:S(2)}) copy-start(bf16[7,512]{1,0:T(8,128)(2,1)} %param.8) | copy-start | bytes 21508
  2.4 2.0 %copy-start.6 = (pred[8,17]{0,1:T(8,128)(4,1)S(1)}, pred[8,17]{0,1:T(8,128)(4,1)}, u32[]{:S(2)}) copy-start(pred[8,17]{0,1:T(8,128)(4,1)} %constant.103) | copy-start | bytes 412
  4.5 0.7 copy-start.4
  4.7 4.2 %copy-start.1 = (bf16[128,512]{1,0:T(8,128)(2,1)S(1)}, bf16[128,512]{1,0:T(8,128)(2,1)}, u32[]{:S(2)}) copy-start(bf16[128,512]{1,0:T(8,128)(2,1)} %param.9) | copy-start | bytes 393220
  4.7 4.4 %copy-start.3 = (f32[64,4]{0,1:T(4,128)S(1)}, f32[64,4]{0,1:T(4,128)}, u32[]{:S(2)}) copy-start(f32[64,4]{0,1:T(4,128)} %param.11) | copy-start | bytes 3076
  6.2 15.4 %collective-permute-start = (bf16[165,512]{1,0:T(8,128)(2,1)S(1)}, bf16[165,512]{1,0:T(8,128)(2,1)S(1)}, u32[]{:S(2)}, u32[]{:S(2)}) collective-permute-start(bf16[165,512]{1,0:T(8,128)(2,1)S(1)} %pad_maximum_fusion), channel_id=1, source_target_pairs={{0,16},{16,32},{32,48},{48,64},{64,80},{80,96},{96,112},{112,128},... | collective-permute-start | bytes 506888 | tf_op jit(solution)/shard_map/ppermute | solution.py:15
  22.7 34.9 %all-to-all-start = ((bf16[16,2,8,512]{3,2,1,0:T(8,128)(2,1)}), bf16[16,2,8,512]{3,2,1,0:T(8,128)(2,1)S(1)}, u32[]{:S(2)}, u32[]{:S(2)}) async-start(bf16[16,2,8,512]{3,2,1,0:T(8,128)(2,1)} %select_select_fusion), calls=%async_computation | async-start | bytes 524288 | tf_op jit(solution)/shard_map/all_to_all | solution.py:96
  58.5 14.4 %all-to-all-start.1 = ((f32[16,2,128,4]{2,3,1,0:T(4,128)}), f32[16,2,128,4]{2,3,1,0:T(4,128)S(1)}, u32[]{:S(2)}, u32[]{:S(2)}) async-start(f32[16,2,128,4]{2,3,1,0:T(4,128)} %broadcast_in_dim.147), calls=%async_computation.1 | async-start | bytes 131072 | tf_op jit(solution)/shard_map/all_to_all | solution.py:21

commit v8 on v7

--- a/solution.py
+++ b/solution.py
@@ -54,31 +54,27 @@
     local_rows = jnp.where(owned[:, None, None], local_rows, jnp.zeros_like(local_rows))
     partial_rows = local_rows
 
-    first_gate = streams[0].astype(jnp.float32)
-    second_gate = streams[3].astype(jnp.float32)
-    second_key = streams[4].astype(jnp.float32)
-    gated = (streams[1].astype(jnp.float32) * streams[2].astype(jnp.float32)).astype(jnp.bfloat16)
-    g_tiles = gated.reshape(tile_count, TILE_ROWS, width)
+    def gated_rows(begin, stop):
+        key = streams[1, begin:stop].astype(jnp.float32)
+        return (key * streams[2, begin:stop].astype(jnp.float32)).astype(jnp.bfloat16)
 
-    def short_window(tile, earlier):
+    def short_window(tile, earlier, own):
         earlier = jnp.where(starts[tile], jnp.zeros_like(earlier), earlier)
-        return jnp.concatenate([earlier, g_tiles[tile]], axis=0)
+        return jnp.concatenate([earlier, own], axis=0)
 
-    def carried_of(tile, short_out):
+    def carried_of(tile, window):
+        short_out = depth_conv(window[None], short_filter)[0]
         rows = slice(tile * TILE_ROWS, (tile + 1) * TILE_ROWS)
-        mixed = (first_gate[rows] * short_out).astype(jnp.bfloat16)
-        return (second_key[rows] * mixed.astype(jnp.float32)).astype(jnp.bfloat16)
+        mixed = (streams[0, rows].astype(jnp.float32) * short_out).astype(jnp.bfloat16)
+        return (streams[4, rows].astype(jnp.float32) * mixed.astype(jnp.float32)).astype(jnp.bfloat16)
 
-    later = [
-        short_window(tile, g_tiles[tile - 1, TILE_ROWS - (short_reach - 1) :])
-        for tile in range(1, tile_count)
-    ]
-    later_out = depth_conv(jnp.stack(later), short_filter)
-    carried_later = [carried_of(tile, later_out[tile - 1]) for tile in range(1, tile_count)]
-
+    last = tile_count - 1
+    last_window = gated_rows(last * TILE_ROWS - (short_reach - 1), rows_here)
+    carried_last = carried_of(
+        last, short_window(last, last_window[: short_reach - 1], last_window[short_reach - 1 :])
+    )
     border = jnp.concatenate(
-        [gated[rows_here - (short_reach - 1) :], carried_later[-1][TILE_ROWS - (long_reach - 1) :]],
-        axis=0,
+        [last_window[TILE_ROWS:], carried_last[TILE_ROWS - (long_reach - 1) :]], axis=0
     )
     row_count = partial_rows.shape[0] * partial_rows.shape[1]
     sent = jnp.concatenate([border, partial_rows.reshape(row_count, width)], axis=0)
@@ -95,8 +91,16 @@
         outgoing = jnp.where((peer_seq == s)[:, :, None, None], chosen[s], outgoing)
     tile_rows = jnp.sum(lax.all_to_all(outgoing, SEQ[:2], 0, 0, tiled=False), axis=0)
 
-    first_out = depth_conv(short_window(0, short_border)[None], short_filter)[0]
-    carried = [carried_of(0, first_out)] + carried_later
+    gated_first = gated_rows(0, last * TILE_ROWS)
+    carried = []
+    for tile in range(last):
+        own = gated_first[tile * TILE_ROWS : (tile + 1) * TILE_ROWS]
+        if tile == 0:
+            earlier = short_border
+        else:
+            earlier = gated_first[tile * TILE_ROWS - (short_reach - 1) : tile * TILE_ROWS]
+        carried.append(carried_of(tile, short_window(tile, earlier, own)))
+    carried.append(carried_last)
 
     long_windows = []
     for tile in range(tile_count):
@@ -104,7 +108,8 @@
         earlier = jnp.where(starts[tile], jnp.zeros_like(earlier), earlier)
         long_windows.append(jnp.concatenate([earlier, carried[tile]], axis=0))
     long_out = depth_conv(jnp.stack(long_windows), long_filter)
-    hidden = (second_gate.reshape(tile_count, TILE_ROWS, width) * long_out).astype(jnp.bfloat16)
+    second_gate = streams[3].astype(jnp.float32).reshape(tile_count, TILE_ROWS, width)
+    hidden = (second_gate * long_out).astype(jnp.bfloat16)
 
     rows_per = edit_table.shape[1]
     rank = rows_per // 2

time: 74.3 us -> 78.3 us (1.054)
  local copies, waits for them, and re-layouts: 5.95 us -> 7.89 us
  waiting for transfers between devices: 24.5 us -> 26.4 us
    all_to_all x1, waiting for transfers between devices: 5.21 us -> 7.13 us  [on_device(): lax.all_to_all(outgoing, SEQ[:2], 0, 0, tiled=False)]
    rev x2, local copies, waits for them, and re-layouts: 0.3 us -> 1.61 us  [depth_conv(): kernel = taps_filter[::-1][:, None, :]]
  transfers between devices with their start and end apart: 3 -> 3, of which waited for: 3 -> 3; matrix products, arithmetic and copies ran while one was open for 18% -> 14% of each run, Pallas kernels for 0% -> 0%
where the time goes in v8:
time: 78.3 us; the launch traced here: 77.9 us
  starting transfers between devices  26.8 us (34%)
  waiting for transfers between devices  26.4 us (34%)
  other arithmetic  8.33 us (11%)
  matrix products  8.02 us (10%)
  local copies, waits for them, and re-layouts  7.89 us (10%)
    all_to_all x1, starting transfers between devices, on_device(): lax.all_to_all(outgoing, SEQ[:2], 0, 0, tiled=False)  18.7 us
    ppermute x1, waiting for transfers between devices, shifted(): lax.ppermute(block, SEQ, [(i, (i + distance) % size) for i in range(size)])  11.2 us
    all_to_all x1, waiting for transfers between devices, a2a_sum(): return jnp.sum(lax.all_to_all(copies, axis, 0, 0, tiled=False), axis=0)  8.11 us
    conv_general_dilated x3, matrix products, depth_conv(): lax.conv_general_dilated(window, kernel, (1,), 'VALID', dimension_numbers...  7.81 us
    all_to_all x1, waiting for transfers between devices, on_device(): lax.all_to_all(outgoing, SEQ[:2], 0, 0, tiled=False)  7.13 us
    all_to_all x1, starting transfers between devices, a2a_sum(): return jnp.sum(lax.all_to_all(copies, axis, 0, 0, tiled=False), axis=0)  6.22 us
    ppermute x1, starting transfers between devices, shifted(): lax.ppermute(block, SEQ, [(i, (i + distance) % size) for i in range(size)])  1.92 us
    rev x2, local copies, waits for them, and re-layouts, depth_conv(): kernel = taps_filter[::-1][:, None, :]  1.61 us
  transfers between devices with their start and end apart: 3, of which 3 were waited for; matrix products, arithmetic and copies ran while one was open for 14% of the time, Pallas kernels for 0%

profile of v8, /device:TPU:8, one launch (start us, length us, event | category | flops | bytes accessed | tf_op | source)
XLA Modules:
  0.0 77.9 jit_solution(17420562682081363241)
XLA Ops:
  0.0 0.8 %reduce-window.8 = s32[4,1]{0,1:T(1,128)S(1)} reduce-window(s32[4,1]{0,1:T(1,128)} %bitcast.84, s32[]{:T(128)} %constant.53.clone.1), window={size=4x1 pad=3_0x0_0}, to_apply=%region_0.0 | reduce-window | flops 12 | bytes 36 | tf_op jit(solution)/shard_map/reduce-window.3
  1.1 0.6 fusion.44
  1.6 0.7 compare_and_fusion
  2.6 1.4 %rev.7 = bf16[7,512]{1,0:T(8,128)(2,1)S(1)} reverse(bf16[7,512]{1,0:T(8,128)(2,1)} %param.8), dimensions={0} | reverse | bytes 14336 | tf_op jit(solution)/shard_map/rev | solution.py:26
  4.1 1.0 %multiply_convert_fusion = bf16[1,134,512]{2,1,0:T(8,128)(2,1)S(1)} fusion(bf16[5,256,512]{2,1,0:T(8,128)(2,1)} %param.7), kind=kLoop, calls=%fused_computation.15 | loop fusion | flops 274432 | bytes 411648 | tf_op jit(solution)/shard_map/convert_element_type | solution.py:59
  5.2 0.7 slice_bitcast_fusion.7
  6.5 0.9 %copy-done.1 = bf16[5,256,512]{2,1,0:T(8,128)(2,1)S(1)} copy-done((bf16[5,256,512]{2,1,0:T(8,128)(2,1)S(1)}, bf16[5,256,512]{2,1,0:T(8,128)(2,1)}, u32[]{:S(2)}) %copy-start.1) | copy-done | bytes 1310744
  7.5 0.5 gather_fusion
  8.2 1.9 %collective-permute-start = (bf16[165,512]{1,0:T(8,128)(2,1)S(1)}, bf16[165,512]{1,0:T(8,128)(2,1)S(1)}, u32[]{:S(2)}, u32[]{:S(2)}) collective-permute-start(bf16[165,512]{1,0:T(8,128)(2,1)S(1)} %pad_maximum_fusion), channel_id=1, source_target_pairs={{0,16},{16,32},{32,48},{48,64},{64,80},{80,96},{96,112},{112,128},... | collective-permute-start | bytes 506888 | tf_op jit(solution)/shard_map/ppermute | solution.py:15
  11.2 0.6 gather_fusion.1
  11.8 0.6 gather_fusion.2
  12.5 11.2 %collective-permute-done = bf16[165,512]{1,0:T(8,128)(2,1)S(1)} collective-permute-done((bf16[165,512]{1,0:T(8,128)(2,1)S(1)}, bf16[165,512]{1,0:T(8,128)(2,1)S(1)}, u32[]{:S(2)}, u32[]{:S(2)}) %collective-permute-start) | collective-permute-done | bytes 168992 | tf_op jit(solution)/shard_map/ppermute | solution.py:15
  23.8 0.6 slice_select_fusion.2
  25.0 0.7 fusion.23
  25.7 0.9 %select_select_fusion = bf16[16,2,8,512]{3,2,1,0:T(8,128)(2,1)} fusion(pred[16,2]{1,0:T(8,128)(4,1)S(1)} %copy.122, pred[16,2]{1,0:T(8,128)(4,1)S(1)} %copy.121, pred[16,2]{1,0:T(8,128)(4,1)S(1)} %copy.120, pred[16,2]{1,0:T(8,128)(4,1)S(1)} %copy.119, bf16[8,512]{1,0:T(8,128)(2,1)S(1)} %get-tuple-element.12, bf16[8,512]{1,0:T(8,128)(2,1)S(1)} %get-tuple-element.13, ...), kind=kLoop, calls=%fused_computation.25 | loop fusion | flops 524288 | bytes 295040 | tf_op jit(solution)/shard_map/jit(_where)/select_n | solution.py:91
  26.6 18.7 %all-to-all-start = ((bf16[16,2,8,512]{3,2,1,0:T(8,128)(2,1)}), bf16[16,2,8,512]{3,2,1,0:T(8,128)(2,1)S(1)}, u32[]{:S(2)}, u32[]{:S(2)}) async-start(bf16[16,2,8,512]{3,2,1,0:T(8,128)(2,1)} %select_select_fusion), calls=%async_computation | async-start | bytes 524288 | tf_op jit(solution)/shard_map/all_to_all | solution.py:92
  45.3 0.6 slice_select_fusion.1
  46.0 0.4 copy.115
  46.9 7.5 %fusion.1 = f32[2,128,512]{2,0,1:T(2,128)S(1)} fusion(bf16[1,255,512]{2,0,1:T(2,128)(2,1)S(1)} %copy.116, bf16[1,255,512]{2,0,1:T(2,128)(2,1)S(1)} %copy.115, bf16[128,1,512]{2,0,1:T(8,128)(2,1)S(1)} %bitcast.74), kind=kOutput, calls=%fused_computation.8 | convolution fusion | flops 34598912 | bytes 1177600 | tf_op jit(solution)/shard_map/conv_general_dilated | solution.py:27
  54.4 7.1 %all-to-all-done = bf16[16,2,8,512]{3,2,1,0:T(8,128)(2,1)S(1)} async-done(((bf16[16,2,8,512]{3,2,1,0:T(8,128)(2,1)}), bf16[16,2,8,512]{3,2,1,0:T(8,128)(2,1)S(1)}, u32[]{:S(2)}, u32[]{:S(2)}) %all-to-all-start) | async-done | bytes 262176 | tf_op jit(solution)/shard_map/all_to_all | solution.py:92
  61.8 0.6 broadcast_in_dim.151
  62.4 6.2 %all-to-all-start.1 = ((f32[16,2,128,4]{2,3,1,0:T(4,128)}), f32[16,2,128,4]{2,3,1,0:T(4,128)S(1)}, u32[]{:S(2)}, u32[]{:S(2)}) async-start(f32[16,2,128,4]{2,3,1,0:T(4,128)} %broadcast_in_dim.151), calls=%async_computation.1 | async-start | bytes 131072 | tf_op jit(solution)/shard_map/all_to_all | solution.py:21
  68.7 8.1 %all-to-all-done.1 = f32[16,2,128,4]{2,3,1,0:T(4,128)S(1)} async-done(((f32[16,2,128,4]{2,3,1,0:T(4,128)}), f32[16,2,128,4]{2,3,1,0:T(4,128)S(1)}, u32[]{:S(2)}, u32[]{:S(2)}) %all-to-all-start.1) | async-done | bytes 65568 | tf_op jit(solution)/shard_map/all_to_all | solution.py:21
  76.9 1.0 %add_convert_fusion = bf16[2,128,512]{2,1,0:T(8,128)(2,1)} fusion(f32[2,512]{1,0:T(2,128)S(1)} %get-tuple-element.33, f32[2,128]{1,0:T(2,128)S(1)} %bitcast.78, f32[2,512]{1,0:T(2,128)S(1)} %get-tuple-element.34, f32[2,128]{1,0:T(2,128)S(1)} %bitcast.79, f32[2,512]{1,0:T(2,128)S(1)} %get-tuple-element.35, f32[2,128]{1,0:T(2,128)S(1)} %bitcast.80, ...), kind=kLoop, calls=%fused_computation.7 | loop fusion | flops 1703936 | bytes 1069056 | tf_op jit(solution)/shard_map/convert_element_type | solution.py:127
  (75 shorter events, 4.1 us)
Async XLA Ops:
  0.0 7.5 %copy-start = (bf16[2,8,512]{2,1,0:T(8,128)(2,1)S(1)}, bf16[2,8,512]{2,1,0:T(8,128)(2,1)}, u32[]{:S(2)}) copy-start(bf16[2,8,512]{2,1,0:T(8,128)(2,1)} %param.10) | copy-start | bytes 49156
  0.0 6.0 %copy-start.5 = (pred[8,17]{0,1:T(8,128)(4,1)S(1)}, pred[8,17]{0,1:T(8,128)(4,1)}, u32[]{:S(2)}) copy-start(pred[8,17]{0,1:T(8,128)(4,1)} %constant.103) | copy-start | bytes 412
  6.1 1.3 %copy-start.1 = (bf16[5,256,512]{2,1,0:T(8,128)(2,1)S(1)}, bf16[5,256,512]{2,1,0:T(8,128)(2,1)}, u32[]{:S(2)}) copy-start(bf16[5,256,512]{2,1,0:T(8,128)(2,1)} %param.7) | copy-start | bytes 3932164
  6.4 3.9 %copy-start.4 = (s32[4]{0:T(128)S(1)}, s32[4]{0:T(128)}, u32[]{:S(2)}) copy-start(s32[4]{0:T(128)} %param.13) | copy-start | bytes 52
  7.4 3.5 %copy-start.3 = (f32[64,4]{0,1:T(4,128)S(1)}, f32[64,4]{0,1:T(4,128)}, u32[]{:S(2)}) copy-start(f32[64,4]{0,1:T(4,128)} %param.11) | copy-start | bytes 3076
  7.4 3.7 %copy-start.2 = (bf16[128,512]{1,0:T(8,128)(2,1)S(1)}, bf16[128,512]{1,0:T(8,128)(2,1)}, u32[]{:S(2)}) copy-start(bf16[128,512]{1,0:T(8,128)(2,1)} %param.9) | copy-start | bytes 393220
  8.2 15.4 %collective-permute-start = (bf16[165,512]{1,0:T(8,128)(2,1)S(1)}, bf16[165,512]{1,0:T(8,128)(2,1)S(1)}, u32[]{:S(2)}, u32[]{:S(2)}) collective-permute-start(bf16[165,512]{1,0:T(8,128)(2,1)S(1)} %pad_maximum_fusion), channel_id=1, source_target_pairs={{0,16},{16,32},{32,48},{48,64},{64,80},{80,96},{96,112},{112,128},... | collective-permute-start | bytes 506888 | tf_op jit(solution)/shard_map/ppermute | solution.py:15
  26.6 34.9 %all-to-all-start = ((bf16[16,2,8,512]{3,2,1,0:T(8,128)(2,1)}), bf16[16,2,8,512]{3,2,1,0:T(8,128)(2,1)S(1)}, u32[]{:S(2)}, u32[]{:S(2)}) async-start(bf16[16,2,8,512]{3,2,1,0:T(8,128)(2,1)} %select_select_fusion), calls=%async_computation | async-start | bytes 524288 | tf_op jit(solution)/shard_map/all_to_all | solution.py:92
  62.4 14.4 %all-to-all-start.1 = ((f32[16,2,128,4]{2,3,1,0:T(4,128)}), f32[16,2,128,4]{2,3,1,0:T(4,128)S(1)}, u32[]{:S(2)}, u32[]{:S(2)}) async-start(f32[16,2,128,4]{2,3,1,0:T(4,128)} %broadcast_in_dim.151), calls=%async_computation.1 | async-start | bytes 131072 | tf_op jit(solution)/shard_map/all_to_all | solution.py:21

commit v9 on v7

--- a/solution.py
+++ b/solution.py
@@ -52,7 +52,7 @@
     owned = (owner_slot >= 0) & (owner_slot < held)
     local_rows = jnp.take(edit_table, jnp.clip(owner_slot, 0, held - 1), axis=0)
     local_rows = jnp.where(owned[:, None, None], local_rows, jnp.zeros_like(local_rows))
-    partial_rows = local_rows
+    partial_rows = a2a_sum(local_rows, "zh")
 
     first_gate = streams[0].astype(jnp.float32)
     second_gate = streams[3].astype(jnp.float32)
@@ -86,14 +86,15 @@
     short_border = sent[: short_reach - 1]
     long_border = sent[short_reach - 1 : border.shape[0]]
     chosen = partial_rows + sent[border.shape[0] :].reshape(partial_rows.shape)
-    zh_size = lax.axis_size(SEQ[:2])
-    peer = jnp.arange(zh_size, dtype=jnp.int32) * lax.axis_size("core") + lax.axis_index("core")
+    zh_size = lax.axis_size("y")
+    stride = lax.axis_size("zh") * lax.axis_size("core")
+    peer = me + (jnp.arange(zh_size, dtype=jnp.int32) - lax.axis_index("y")) * stride
     peer_tiles = peer[:, None] * tile_count + jnp.arange(tile_count, dtype=jnp.int32)[None, :]
     peer_seq = jnp.sum((seq_ends[None, None, :] <= peer_tiles[:, :, None]).astype(jnp.int32), axis=2)
     outgoing = jnp.zeros((zh_size, tile_count) + chosen.shape[1:], chosen.dtype)
     for s in range(SEQS):
         outgoing = jnp.where((peer_seq == s)[:, :, None, None], chosen[s], outgoing)
-    tile_rows = jnp.sum(lax.all_to_all(outgoing, SEQ[:2], 0, 0, tiled=False), axis=0)
+    tile_rows = jnp.sum(lax.all_to_all(outgoing, "y", 0, 0, tiled=False), axis=0)
 
     first_out = depth_conv(short_window(0, short_border)[None], short_filter)[0]
     carried = [carried_of(0, first_out)] + carried_later

time: 74.3 us -> 81.5 us (1.097)
  waiting for transfers between devices: 24.5 us -> 31 us
    all_to_all x1 -> x2, starting transfers between devices: 6.22 us -> 20.6 us  [a2a_sum(): return jnp.sum(lax.all_to_all(copies, axis, 0, 0, tiled=False), axis=0)]
    all_to_all x1, starting transfers between devices: 18.7 us -> 4.91 us  [on_device(): lax.all_to_all(outgoing, 'y', 0, 0, tiled=False)]
    all_to_all x1 -> x2, waiting for transfers between devices: 8.11 us -> 15.9 us  [a2a_sum(): return jnp.sum(lax.all_to_all(copies, axis, 0, 0, tiled=False), axis=0)]
    all_to_all x1, waiting for transfers between devices: 5.21 us -> 0.01 us  [on_device(): lax.all_to_all(outgoing, 'y', 0, 0, tiled=False)]
    ppermute x1, waiting for transfers between devices: 11.2 us -> 15 us  [shifted(): lax.ppermute(block, SEQ, [(i, (i + distance) % size) for i in range(size)])]
    slice x1, other arithmetic: 1.22 us -> 0.1 us  [on_device(): second_gate = streams[3].astype(jnp.float32)]
  transfers between devices with their start and end apart: 3 -> 4, of which waited for: 3 -> 3; matrix products, arithmetic and copies ran while one was open for 18% -> 21% of each run, Pallas kernels for 0% -> 0%
where the time goes in v9:
time: 81.5 us; the launch traced here: 81 us
  waiting for transfers between devices  31 us (38%)
  starting transfers between devices  27.4 us (34%)
  matrix products  8.02 us (10%)
  other arithmetic  7.63 us (9%)
  local copies, waits for them, and re-layouts  6.5 us (8%)
    all_to_all x2, starting transfers between devices, a2a_sum(): return jnp.sum(lax.all_to_all(copies, axis, 0, 0, tiled=False), axis=0)  20.6 us
    all_to_all x2, waiting for transfers between devices, a2a_sum(): return jnp.sum(lax.all_to_all(copies, axis, 0, 0, tiled=False), axis=0)  15.9 us
    ppermute x1, waiting for transfers between devices, shifted(): lax.ppermute(block, SEQ, [(i, (i + distance) % size) for i in range(size)])  15 us
    conv_general_dilated x3, matrix products, depth_conv(): lax.conv_general_dilated(window, kernel, (1,), 'VALID', dimension_numbers...  7.81 us
    all_to_all x1, starting transfers between devices, on_device(): lax.all_to_all(outgoing, 'y', 0, 0, tiled=False)  4.91 us
    ppermute x1, starting transfers between devices, shifted(): lax.ppermute(block, SEQ, [(i, (i + distance) % size) for i in range(size)])  1.92 us
  transfers between devices with their start and end apart: 4, of which 3 were waited for; matrix products, arithmetic and copies ran while one was open for 21% of the time, Pallas kernels for 0%

profile of v9, /device:TPU:8, one launch (start us, length us, event | category | flops | bytes accessed | tf_op | source)
XLA Modules:
  0.0 81.0 jit_solution(11957303796251319890)
XLA Ops:
  0.0 0.8 compare_and_fusion
  0.8 0.5 gather_fusion
  1.4 0.7 broadcast_in_dim.118
  2.1 15.1 %all-to-all-start = ((bf16[4,4,8,512]{3,2,1,0:T(8,128)(2,1)}), bf16[4,4,8,512]{3,2,1,0:T(8,128)(2,1)S(1)}, u32[]{:S(2)}, u32[]{:S(2)}) async-start(bf16[4,4,8,512]{3,2,1,0:T(8,128)(2,1)} %broadcast_in_dim.118), calls=%async_computation | async-start | bytes 262144 | tf_op jit(solution)/shard_map/all_to_all | solution.py:21
  17.2 1.1 %multiply_convert_fusion = bf16[1,256,512]{2,1,0:T(8,128)(2,1)S(1)} fusion(bf16[5,256,512]{2,1,0:T(8,128)(2,1)} %param.7), kind=kLoop, calls=%fused_computation.8 | loop fusion | flops 524288 | bytes 786432 | tf_op jit(solution)/shard_map/convert_element_type | solution.py:60
  18.5 0.4 copy-done.6
  19.5 0.6 fusion.45
  20.1 0.6 fusion.30
  22.5 0.6 gather_fusion.1
  23.1 0.6 gather_fusion.2
  23.8 7.8 %all-to-all-done = bf16[4,4,8,512]{3,2,1,0:T(8,128)(2,1)S(1)} async-done(((bf16[4,4,8,512]{3,2,1,0:T(8,128)(2,1)}), bf16[4,4,8,512]{3,2,1,0:T(8,128)(2,1)S(1)}, u32[]{:S(2)}, u32[]{:S(2)}) %all-to-all-start) | async-done | bytes 131104 | tf_op jit(solution)/shard_map/all_to_all | solution.py:21
  31.7 1.9 %collective-permute-start = (bf16[165,512]{1,0:T(8,128)(2,1)S(1)}, bf16[165,512]{1,0:T(8,128)(2,1)S(1)}, u32[]{:S(2)}, u32[]{:S(2)}) collective-permute-start(bf16[165,512]{1,0:T(8,128)(2,1)S(1)} %pad_maximum_fusion), channel_id=1, source_target_pairs={{0,16},{16,32},{32,48},{48,64},{64,80},{80,96},{96,112},{112,128},... | collective-permute-start | bytes 506888 | tf_op jit(solution)/shard_map/ppermute | solution.py:15
  33.7 15.0 %collective-permute-done = bf16[165,512]{1,0:T(8,128)(2,1)S(1)} collective-permute-done((bf16[165,512]{1,0:T(8,128)(2,1)S(1)}, bf16[165,512]{1,0:T(8,128)(2,1)S(1)}, u32[]{:S(2)}, u32[]{:S(2)}) %collective-permute-start) | collective-permute-done | bytes 168992 | tf_op jit(solution)/shard_map/ppermute | solution.py:15
  48.7 0.7 select_select_fusion
  49.5 4.9 %all-to-all-start.1 = ((bf16[4,2,8,512]{3,2,1,0:T(8,128)(2,1)}), bf16[4,2,8,512]{3,2,1,0:T(8,128)(2,1)S(1)}, u32[]{:S(2)}, u32[]{:S(2)}) async-start(bf16[4,2,8,512]{3,2,1,0:T(8,128)(2,1)} %select_select_fusion), calls=%async_computation.1 | async-start | bytes 131072 | tf_op jit(solution)/shard_map/all_to_all | solution.py:97
  54.4 0.6 slice_select_fusion.2
  55.7 0.6 fusion.24
  56.3 0.7 slice_select_fusion.1
  57.0 0.4 copy.115
  57.9 7.5 %fusion.1 = f32[2,128,512]{2,0,1:T(2,128)S(1)} fusion(bf16[1,255,512]{2,0,1:T(2,128)(2,1)S(1)} %copy.116, bf16[1,255,512]{2,0,1:T(2,128)(2,1)S(1)} %copy.115, bf16[128,1,512]{2,0,1:T(8,128)(2,1)S(1)} %bitcast.74), kind=kOutput, calls=%fused_computation.9 | convolution fusion | flops 34598912 | bytes 1177600 | tf_op jit(solution)/shard_map/conv_general_dilated | solution.py:27
  65.7 0.6 broadcast_in_dim.130
  66.3 5.5 %all-to-all-start.2 = ((f32[16,2,128,4]{2,3,1,0:T(4,128)}), f32[16,2,128,4]{2,3,1,0:T(4,128)S(1)}, u32[]{:S(2)}, u32[]{:S(2)}) async-start(f32[16,2,128,4]{2,3,1,0:T(4,128)} %broadcast_in_dim.130), calls=%async_computation.2 | async-start | bytes 131072 | tf_op jit(solution)/shard_map/all_to_all | solution.py:21
  71.8 8.1 %all-to-all-done.2 = f32[16,2,128,4]{2,3,1,0:T(4,128)S(1)} async-done(((f32[16,2,128,4]{2,3,1,0:T(4,128)}), f32[16,2,128,4]{2,3,1,0:T(4,128)S(1)}, u32[]{:S(2)}, u32[]{:S(2)}) %all-to-all-start.2) | async-done | bytes 65568 | tf_op jit(solution)/shard_map/all_to_all | solution.py:21
  80.1 1.0 %add_convert_fusion = bf16[2,128,512]{2,1,0:T(8,128)(2,1)} fusion(f32[2,512]{1,0:T(2,128)S(1)} %get-tuple-element.34, f32[2,128]{1,0:T(2,128)S(1)} %bitcast.78, f32[2,512]{1,0:T(2,128)S(1)} %get-tuple-element.35, f32[2,128]{1,0:T(2,128)S(1)} %bitcast.79, f32[2,512]{1,0:T(2,128)S(1)} %get-tuple-element.36, f32[2,128]{1,0:T(2,128)S(1)} %bitcast.80, ...), kind=kLoop, calls=%fused_computation.7 | loop fusion | flops 1703936 | bytes 1069056 | tf_op jit(solution)/shard_map/convert_element_type | solution.py:123
  (80 shorter events, 4.3 us)
Async XLA Ops:
  0.0 0.8 copy-start
  0.0 18.3 %copy-start.1 = (bf16[5,256,512]{2,1,0:T(8,128)(2,1)S(1)}, bf16[5,256,512]{2,1,0:T(8,128)(2,1)}, u32[]{:S(2)}) copy-start(bf16[5,256,512]{2,1,0:T(8,128)(2,1)} %param.7) | copy-start | bytes 3932164
  2.1 29.5 %all-to-all-start = ((bf16[4,4,8,512]{3,2,1,0:T(8,128)(2,1)}), bf16[4,4,8,512]{3,2,1,0:T(8,128)(2,1)S(1)}, u32[]{:S(2)}, u32[]{:S(2)}) async-start(bf16[4,4,8,512]{3,2,1,0:T(8,128)(2,1)} %broadcast_in_dim.118), calls=%async_computation | async-start | bytes 262144 | tf_op jit(solution)/shard_map/all_to_all | solution.py:21
  18.3 0.7 copy-start.6
  18.3 1.2 %copy-start.5 = (s32[4]{0:T(128)S(1)}, s32[4]{0:T(128)}, u32[]{:S(2)}) copy-start(s32[4]{0:T(128)} %param.13) | copy-start | bytes 52
  18.4 2.5 %copy-start.3 = (bf16[7,512]{1,0:T(8,128)(2,1)S(1)}, bf16[7,512]{1,0:T(8,128)(2,1)}, u32[]{:S(2)}) copy-start(bf16[7,512]{1,0:T(8,128)(2,1)} %param.8) | copy-start | bytes 21508
  18.4 2.6 %copy-start.7 = (pred[8,17]{0,1:T(8,128)(4,1)S(1)}, pred[8,17]{0,1:T(8,128)(4,1)}, u32[]{:S(2)}) copy-start(pred[8,17]{0,1:T(8,128)(4,1)} %constant.104) | copy-start | bytes 412
  21.1 1.1 %copy-start.2 = (bf16[128,512]{1,0:T(8,128)(2,1)S(1)}, bf16[128,512]{1,0:T(8,128)(2,1)}, u32[]{:S(2)}) copy-start(bf16[128,512]{1,0:T(8,128)(2,1)} %param.9) | copy-start | bytes 393220
  21.1 1.3 %copy-start.4 = (f32[64,4]{0,1:T(4,128)S(1)}, f32[64,4]{0,1:T(4,128)}, u32[]{:S(2)}) copy-start(f32[64,4]{0,1:T(4,128)} %param.11) | copy-start | bytes 3076
  31.7 17.0 %collective-permute-start = (bf16[165,512]{1,0:T(8,128)(2,1)S(1)}, bf16[165,512]{1,0:T(8,128)(2,1)S(1)}, u32[]{:S(2)}, u32[]{:S(2)}) collective-permute-start(bf16[165,512]{1,0:T(8,128)(2,1)S(1)} %pad_maximum_fusion), channel_id=1, source_target_pairs={{0,16},{16,32},{32,48},{48,64},{64,80},{80,96},{96,112},{112,128},... | collective-permute-start | bytes 506888 | tf_op jit(solution)/shard_map/ppermute | solution.py:15
  49.5 15.9 %all-to-all-start.1 = ((bf16[4,2,8,512]{3,2,1,0:T(8,128)(2,1)}), bf16[4,2,8,512]{3,2,1,0:T(8,128)(2,1)S(1)}, u32[]{:S(2)}, u32[]{:S(2)}) async-start(bf16[4,2,8,512]{3,2,1,0:T(8,128)(2,1)} %select_select_fusion), calls=%async_computation.1 | async-start | bytes 131072 | tf_op jit(solution)/shard_map/all_to_all | solution.py:97
  66.3 13.6 %all-to-all-start.2 = ((f32[16,2,128,4]{2,3,1,0:T(4,128)}), f32[16,2,128,4]{2,3,1,0:T(4,128)S(1)}, u32[]{:S(2)}, u32[]{:S(2)}) async-start(f32[16,2,128,4]{2,3,1,0:T(4,128)} %broadcast_in_dim.130), calls=%async_computation.2 | async-start | bytes 131072 | tf_op jit(solution)/shard_map/all_to_all | solution.py:21

commit v10 on v5

--- a/solution.py
+++ b/solution.py
@@ -49,9 +49,10 @@
 
     held = edit_table.shape[0]
     owner_slot = seq_tenant - me * held
-    owned = (owner_slot >= 0) & (owner_slot < held)
-    local_rows = jnp.take(edit_table, jnp.clip(owner_slot, 0, held - 1), axis=0)
-    local_rows = jnp.where(owned[:, None, None], local_rows, jnp.zeros_like(local_rows))
+    picker = (owner_slot[:, None] == jnp.arange(held, dtype=jnp.int32)[None, :]).astype(edit_table.dtype)
+    local_rows = jnp.einsum(
+        "sh,hrc->src", picker, edit_table, preferred_element_type=jnp.float32
+    ).astype(edit_table.dtype)
     partial_rows = a2a_sum(local_rows, "y")
 
     first_gate = streams[0].astype(jnp.float32)

time: 74.2 us -> 73.7 us (level)
    and x1, other arithmetic: 0.77 us -> 0.01 us  [on_device(): jnp.take(edit_bias, seq_tenant, axis=0)]
    select_n x2, other arithmetic: 0.08 us -> 0.84 us  [on_device(): jnp.take(edit_bias, seq_tenant, axis=0)]
where the time goes in v10:
time: 73.7 us; the launch traced here: 73.3 us
  starting transfers between devices  31 us (42%)
  waiting for transfers between devices  20.1 us (27%)
  matrix products  8.23 us (11%)
  other arithmetic  7.54 us (10%)
  local copies, waits for them, and re-layouts  5.96 us (8%)
    all_to_all x1, starting transfers between devices, on_device(): lax.all_to_all(outgoing, 'zh', 0, 0, tiled=False)  14.7 us
    all_to_all x2, starting transfers between devices, a2a_sum(): return jnp.sum(lax.all_to_all(copies, axis, 0, 0, tiled=False), axis=0)  14.3 us
    ppermute x1, waiting for transfers between devices, shifted(): lax.ppermute(block, SEQ, [(i, (i + distance) % size) for i in range(size)])  9.79 us
    all_to_all x2, waiting for transfers between devices, a2a_sum(): return jnp.sum(lax.all_to_all(copies, axis, 0, 0, tiled=False), axis=0)  8.11 us
    conv_general_dilated x3, matrix products, depth_conv(): lax.conv_general_dilated(window, kernel, (1,), 'VALID', dimension_numbers...  7.81 us
    all_to_all x1, waiting for transfers between devices, on_device(): lax.all_to_all(outgoing, 'zh', 0, 0, tiled=False)  2.2 us
    ppermute x1, starting transfers between devices, shifted(): lax.ppermute(block, SEQ, [(i, (i + distance) % size) for i in range(size)])  1.92 us
  transfers between devices with their start and end apart: 4, of which 3 were waited for; matrix products, arithmetic and copies ran while one was open for 23% of the time, Pallas kernels for 0%

profile of v10, /device:TPU:8, one launch (start us, length us, event | category | flops | bytes accessed | tf_op | source)
XLA Modules:
  0.0 73.3 jit_solution(5057319047998899032)
XLA Ops:
  0.0 0.8 %compare_select_fusion.1 = (s32[4]{0:T(128)S(1)}, s32[4]{0:T(128)S(1)}) fusion(s32[4]{0:T(128)} %param.13, s32[]{:T(128)S(6)} %mul.118), kind=kLoop, calls=%fused_computation.74 | loop fusion | flops 16 | bytes 52 | tf_op jit(solution)/shard_map/jit(_take)/jit(_where)/select_n | solution.py:117
  1.0 0.7 broadcast_in_dim.91
  1.7 9.1 %all-to-all-start = ((bf16[4,4,8,512]{3,2,1,0:T(8,128)(2,1)}), bf16[4,4,8,512]{3,2,1,0:T(8,128)(2,1)S(1)}, u32[]{:S(2)}, u32[]{:S(2)}) async-start(bf16[4,4,8,512]{3,2,1,0:T(8,128)(2,1)} %broadcast_in_dim.91), calls=%async_computation | async-start | bytes 262144 | tf_op jit(solution)/shard_map/all_to_all | solution.py:21
  10.8 1.1 %multiply_convert_fusion = bf16[1,256,512]{2,1,0:T(8,128)(2,1)S(1)} fusion(bf16[5,256,512]{2,1,0:T(8,128)(2,1)} %param.7), kind=kLoop, calls=%fused_computation.8 | loop fusion | flops 524288 | bytes 786432 | tf_op jit(solution)/shard_map/convert_element_type | solution.py:61
  12.1 0.4 copy-done.6
  13.1 0.6 fusion.50
  13.7 0.6 fusion.31
  16.2 0.6 gather_fusion
  16.8 0.6 gather_fusion.1
  17.5 1.9 %collective-permute-start = (bf16[165,512]{1,0:T(8,128)(2,1)S(1)}, bf16[165,512]{1,0:T(8,128)(2,1)S(1)}, u32[]{:S(2)}, u32[]{:S(2)}) collective-permute-start(bf16[165,512]{1,0:T(8,128)(2,1)S(1)} %pad_maximum_fusion), channel_id=1, source_target_pairs={{0,16},{16,32},{32,48},{48,64},{64,80},{80,96},{96,112},{112,128},... | collective-permute-start | bytes 506888 | tf_op jit(solution)/shard_map/ppermute | solution.py:15
  19.5 9.8 %collective-permute-done = bf16[165,512]{1,0:T(8,128)(2,1)S(1)} collective-permute-done((bf16[165,512]{1,0:T(8,128)(2,1)S(1)}, bf16[165,512]{1,0:T(8,128)(2,1)S(1)}, u32[]{:S(2)}, u32[]{:S(2)}) %collective-permute-start) | collective-permute-done | bytes 168992 | tf_op jit(solution)/shard_map/ppermute | solution.py:15
  29.3 0.7 %select_select_fusion = bf16[4,2,8,512]{3,2,1,0:T(8,128)(2,1)} fusion(pred[4,2]{1,0:T(4,128)(4,1)S(1)} %copy.136, pred[4,2]{1,0:T(4,128)(4,1)S(1)} %copy.135, pred[4,2]{1,0:T(4,128)(4,1)S(1)} %copy.134, pred[4,2]{1,0:T(4,128)(4,1)S(1)} %copy.133, bf16[8,512]{1,0:T(8,128)(2,1)S(1)} %get-tuple-element.11, bf16[8,512]{1,0:T(8,128)(2,1)S(1)} %get-tuple-element.12, ...), kind=kLoop, calls=%fused_computation.50 | loop fusion | flops 131072 | bytes 98336 | tf_op jit(solution)/shard_map/jit(_where)/select_n | solution.py:96
  30.0 14.7 %all-to-all-start.1 = ((bf16[4,2,8,512]{3,2,1,0:T(8,128)(2,1)}), bf16[4,2,8,512]{3,2,1,0:T(8,128)(2,1)S(1)}, u32[]{:S(2)}, u32[]{:S(2)}) async-start(bf16[4,2,8,512]{3,2,1,0:T(8,128)(2,1)} %select_select_fusion), calls=%async_computation.1 | async-start | bytes 131072 | tf_op jit(solution)/shard_map/all_to_all | solution.py:97
  44.7 0.6 slice_select_fusion.2
  46.0 0.6 fusion.24
  46.6 0.7 slice_select_fusion.1
  47.4 0.4 copy.129
  47.8 0.4 copy.130
  48.2 7.5 %fusion.1 = f32[2,128,512]{2,0,1:T(2,128)S(1)} fusion(bf16[1,255,512]{2,0,1:T(2,128)(2,1)S(1)} %copy.130, bf16[1,255,512]{2,0,1:T(2,128)(2,1)S(1)} %copy.129, bf16[128,1,512]{2,0,1:T(8,128)(2,1)S(1)} %bitcast.77), kind=kOutput, calls=%fused_computation.9 | convolution fusion | flops 34598912 | bytes 1177600 | tf_op jit(solution)/shard_map/conv_general_dilated | solution.py:27
  55.7 2.2 %all-to-all-done.1 = bf16[4,2,8,512]{3,2,1,0:T(8,128)(2,1)S(1)} async-done(((bf16[4,2,8,512]{3,2,1,0:T(8,128)(2,1)}), bf16[4,2,8,512]{3,2,1,0:T(8,128)(2,1)S(1)}, u32[]{:S(2)}, u32[]{:S(2)}) %all-to-all-start.1) | async-done | bytes 65568 | tf_op jit(solution)/shard_map/all_to_all | solution.py:97
  58.2 0.6 broadcast_in_dim.103
  58.8 5.2 %all-to-all-start.2 = ((f32[16,2,128,4]{2,3,1,0:T(4,128)}), f32[16,2,128,4]{2,3,1,0:T(4,128)S(1)}, u32[]{:S(2)}, u32[]{:S(2)}) async-start(f32[16,2,128,4]{2,3,1,0:T(4,128)} %broadcast_in_dim.103), calls=%async_computation.2 | async-start | bytes 131072 | tf_op jit(solution)/shard_map/all_to_all | solution.py:21
  64.1 8.1 %all-to-all-done.2 = f32[16,2,128,4]{2,3,1,0:T(4,128)S(1)} async-done(((f32[16,2,128,4]{2,3,1,0:T(4,128)}), f32[16,2,128,4]{2,3,1,0:T(4,128)S(1)}, u32[]{:S(2)}, u32[]{:S(2)}) %all-to-all-start.2) | async-done | bytes 65568 | tf_op jit(solution)/shard_map/all_to_all | solution.py:21
  72.3 1.0 %add_convert_fusion = bf16[2,128,512]{2,1,0:T(8,128)(2,1)} fusion(f32[2,512]{1,0:T(2,128)S(1)} %get-tuple-element.30, f32[2,128]{1,0:T(2,128)S(1)} %bitcast.81, f32[2,512]{1,0:T(2,128)S(1)} %get-tuple-element.31, f32[2,128]{1,0:T(2,128)S(1)} %bitcast.82, f32[2,512]{1,0:T(2,128)S(1)} %get-tuple-element.32, f32[2,128]{1,0:T(2,128)S(1)} %bitcast.83, ...), kind=kLoop, calls=%fused_computation.7 | loop fusion | flops 1703936 | bytes 1069056 | tf_op jit(solution)/shard_map/convert_element_type | solution.py:123
  (79 shorter events, 4.0 us)
Async XLA Ops:
  0.0 0.8 %copy-start = (bf16[2,8,512]{2,1,0:T(8,128)(2,1)S(1)}, bf16[2,8,512]{2,1,0:T(8,128)(2,1)}, u32[]{:S(2)}) copy-start(bf16[2,8,512]{2,1,0:T(8,128)(2,1)} %param.10) | copy-start | bytes 49156
  0.0 11.9 %copy-start.1 = (bf16[5,256,512]{2,1,0:T(8,128)(2,1)S(1)}, bf16[5,256,512]{2,1,0:T(8,128)(2,1)}, u32[]{:S(2)}) copy-start(bf16[5,256,512]{2,1,0:T(8,128)(2,1)} %param.7) | copy-start | bytes 3932164
  1.7 15.7 %all-to-all-start = ((bf16[4,4,8,512]{3,2,1,0:T(8,128)(2,1)}), bf16[4,4,8,512]{3,2,1,0:T(8,128)(2,1)S(1)}, u32[]{:S(2)}, u32[]{:S(2)}) async-start(bf16[4,4,8,512]{3,2,1,0:T(8,128)(2,1)} %broadcast_in_dim.91), calls=%async_computation | async-start | bytes 262144 | tf_op jit(solution)/shard_map/all_to_all | solution.py:21
  11.9 0.7 copy-start.6
  11.9 1.2 %copy-start.5 = (s32[4]{0:T(128)S(1)}, s32[4]{0:T(128)}, u32[]{:S(2)}) copy-start(s32[4]{0:T(128)} %param.13) | copy-start | bytes 52
  12.0 2.5 %copy-start.3 = (bf16[7,512]{1,0:T(8,128)(2,1)S(1)}, bf16[7,512]{1,0:T(8,128)(2,1)}, u32[]{:S(2)}) copy-start(bf16[7,512]{1,0:T(8,128)(2,1)} %param.8) | copy-start | bytes 21508
  12.0 2.6 %copy-start.7 = (pred[8,17]{0,1:T(8,128)(4,1)S(1)}, pred[8,17]{0,1:T(8,128)(4,1)}, u32[]{:S(2)}) copy-start(pred[8,17]{0,1:T(8,128)(4,1)} %constant.87) | copy-start | bytes 412
  14.8 1.0 %copy-start.2 = (bf16[128,512]{1,0:T(8,128)(2,1)S(1)}, bf16[128,512]{1,0:T(8,128)(2,1)}, u32[]{:S(2)}) copy-start(bf16[128,512]{1,0:T(8,128)(2,1)} %param.9) | copy-start | bytes 393220
  14.8 1.2 %copy-start.4 = (f32[64,4]{0,1:T(4,128)S(1)}, f32[64,4]{0,1:T(4,128)}, u32[]{:S(2)}) copy-start(f32[64,4]{0,1:T(4,128)} %param.11) | copy-start | bytes 3076
  17.5 11.8 %collective-permute-start = (bf16[165,512]{1,0:T(8,128)(2,1)S(1)}, bf16[165,512]{1,0:T(8,128)(2,1)S(1)}, u32[]{:S(2)}, u32[]{:S(2)}) collective-permute-start(bf16[165,512]{1,0:T(8,128)(2,1)S(1)} %pad_maximum_fusion), channel_id=1, source_target_pairs={{0,16},{16,32},{32,48},{48,64},{64,80},{80,96},{96,112},{112,128},... | collective-permute-start | bytes 506888 | tf_op jit(solution)/shard_map/ppermute | solution.py:15
  30.0 27.9 %all-to-all-start.1 = ((bf16[4,2,8,512]{3,2,1,0:T(8,128)(2,1)}), bf16[4,2,8,512]{3,2,1,0:T(8,128)(2,1)S(1)}, u32[]{:S(2)}, u32[]{:S(2)}) async-start(bf16[4,2,8,512]{3,2,1,0:T(8,128)(2,1)} %select_select_fusion), calls=%async_computation.1 | async-start | bytes 131072 | tf_op jit(solution)/shard_map/all_to_all | solution.py:97
  58.8 13.4 %all-to-all-start.2 = ((f32[16,2,128,4]{2,3,1,0:T(4,128)}), f32[16,2,128,4]{2,3,1,0:T(4,128)S(1)}, u32[]{:S(2)}, u32[]{:S(2)}) async-start(f32[16,2,128,4]{2,3,1,0:T(4,128)} %broadcast_in_dim.103), calls=%async_computation.2 | async-start | bytes 131072 | tf_op jit(solution)/shard_map/all_to_all | solution.py:21

commit v11 on v10

--- a/solution.py
+++ b/solution.py
@@ -50,10 +50,11 @@
     held = edit_table.shape[0]
     owner_slot = seq_tenant - me * held
     picker = (owner_slot[:, None] == jnp.arange(held, dtype=jnp.int32)[None, :]).astype(edit_table.dtype)
-    local_rows = jnp.einsum(
-        "sh,hrc->src", picker, edit_table, preferred_element_type=jnp.float32
+    copies = jnp.broadcast_to(picker[None], (lax.axis_size("y"),) + picker.shape)
+    local_copies = jnp.einsum(
+        "nsh,hrc->nsrc", copies, edit_table, preferred_element_type=jnp.float32
     ).astype(edit_table.dtype)
-    partial_rows = a2a_sum(local_rows, "y")
+    partial_rows = jnp.sum(lax.all_to_all(local_copies, "y", 0, 0, tiled=False), axis=0)
 
     first_gate = streams[0].astype(jnp.float32)
     second_gate = streams[3].astype(jnp.float32)

time: 73.7 us -> 79.4 us (1.077)
  waiting for transfers between devices: 20.1 us -> 23.6 us
  matrix products: 8.23 us -> 9.65 us
  other arithmetic: 7.54 us -> 8.75 us
    all_to_all x2 -> x1, starting transfers between devices: 14.3 us -> 5.23 us  [a2a_sum(): return jnp.sum(lax.all_to_all(copies, axis, 0, 0, tiled=False), axis=0)]
    all_to_all x0 -> x1, starting transfers between devices: none -> 9.09 us  [on_device(): lax.all_to_all(local_copies, 'y', 0, 0, tiled=False)]
    all_to_all x1, waiting for transfers between devices: 2.2 us -> 5.71 us  [on_device(): lax.all_to_all(outgoing, 'zh', 0, 0, tiled=False)]
    dot_general x1, matrix products: 0.21 us -> 1.65 us  [on_device(): jnp.einsum('nsh,hrc->nsrc', copies, edit_table, preferred_element_type=jn...]
    slice x1, other arithmetic: 0.1 us -> 1.22 us  [on_device(): second_gate = streams[3].astype(jnp.float32)]
    all_to_all x2 -> x1, waiting for transfers between devices: 8.11 us -> 8.05 us  [a2a_sum(): return jnp.sum(lax.all_to_all(copies, axis, 0, 0, tiled=False), axis=0)]
  transfers between devices with their start and end apart: 4 -> 4, of which waited for: 3 -> 3; matrix products, arithmetic and copies ran while one was open for 23% -> 19% of each run, Pallas kernels for 0% -> 0%
where the time goes in v11:
time: 79.4 us; the launch traced here: 78.9 us
  starting transfers between devices  31 us (39%)
  waiting for transfers between devices  23.6 us (30%)
  matrix products  9.65 us (12%)
  other arithmetic  8.75 us (11%)
  local copies, waits for them, and re-layouts  5.47 us (7%)
    all_to_all x1, starting transfers between devices, on_device(): lax.all_to_all(outgoing, 'zh', 0, 0, tiled=False)  14.7 us
    ppermute x1, waiting for transfers between devices, shifted(): lax.ppermute(block, SEQ, [(i, (i + distance) % size) for i in range(size)])  9.79 us
    all_to_all x1, starting transfers between devices, on_device(): lax.all_to_all(local_copies, 'y', 0, 0, tiled=False)  9.09 us
    all_to_all x1, waiting for transfers between devices, a2a_sum(): return jnp.sum(lax.all_to_all(copies, axis, 0, 0, tiled=False), axis=0)  8.05 us
    conv_general_dilated x3, matrix products, depth_conv(): lax.conv_general_dilated(window, kernel, (1,), 'VALID', dimension_numbers...  7.8 us
    all_to_all x1, waiting for transfers between devices, on_device(): lax.all_to_all(outgoing, 'zh', 0, 0, tiled=False)  5.71 us
    all_to_all x1, starting transfers between devices, a2a_sum(): return jnp.sum(lax.all_to_all(copies, axis, 0, 0, tiled=False), axis=0)  5.23 us
    ppermute x1, starting transfers between devices, shifted(): lax.ppermute(block, SEQ, [(i, (i + distance) % size) for i in range(size)])  1.92 us
  transfers between devices with their start and end apart: 4, of which 3 were waited for; matrix products, arithmetic and copies ran while one was open for 19% of the time, Pallas kernels for 0%

profile of v11, /device:TPU:8, one launch (start us, length us, event | category | flops | bytes accessed | tf_op | source)
XLA Modules:
  0.0 78.9 jit_solution(12299881910909768261)
XLA Ops:
  0.0 0.7 compare_select_fusion.1
  0.7 1.6 %convolution_convert_fusion = bf16[4,4,8,512]{3,1,2,0:T(4,128)(2,1)} fusion(bf16[2,8,512]{2,1,0:T(8,128)(2,1)} %param.10, bf16[4,2]{0,1:T(2,128)(2,1)S(1)} %compare_convert_fusion.1), kind=kOutput, calls=%fused_computation.4 | convolution fusion | flops 327680 | bytes 147472 | tf_op jit(solution)/shard_map/nsh,hrc->nsrc/dot_general | solution.py:54
  2.3 9.1 %all-to-all-start = ((bf16[4,4,8,512]{3,1,2,0:T(4,128)(2,1)}), bf16[4,4,8,512]{3,1,2,0:T(4,128)(2,1)S(1)}, u32[]{:S(2)}, u32[]{:S(2)}) async-start(bf16[4,4,8,512]{3,1,2,0:T(4,128)(2,1)} %convolution_convert_fusion), calls=%async_computation | async-start | bytes 262144 | tf_op jit(solution)/shard_map/all_to_all | solution.py:57
  11.4 1.1 %multiply_convert_fusion = bf16[1,256,512]{2,1,0:T(8,128)(2,1)S(1)} fusion(bf16[5,256,512]{2,1,0:T(8,128)(2,1)} %param.7), kind=kLoop, calls=%fused_computation.8 | loop fusion | flops 524288 | bytes 786432 | tf_op jit(solution)/shard_map/convert_element_type | solution.py:62
  12.5 1.2 %fusion.45 = (bf16[1,256,512]{2,1,0:T(8,128)(2,1)S(1)}, f32[1,256,512]{2,1,0:T(8,128)S(1)}, f32[1,256,512]{2,1,0:T(8,128)S(1)}) fusion(bf16[5,256,512]{2,1,0:T(8,128)(2,1)} %param.7), kind=kLoop, calls=%fused_computation.107 | loop fusion | flops 262144 | bytes 2097152 | tf_op jit(solution)/shard_map/slice | solution.py:60
  14.5 0.6 fusion.49
  15.1 0.6 fusion.31
  16.6 0.5 copy-done
  18.1 0.6 gather_fusion
  18.7 0.6 gather_fusion.1
  19.4 1.9 %collective-permute-start = (bf16[165,512]{1,0:T(8,128)(2,1)S(1)}, bf16[165,512]{1,0:T(8,128)(2,1)S(1)}, u32[]{:S(2)}, u32[]{:S(2)}) collective-permute-start(bf16[165,512]{1,0:T(8,128)(2,1)S(1)} %pad_maximum_fusion), channel_id=1, source_target_pairs={{0,16},{16,32},{32,48},{48,64},{64,80},{80,96},{96,112},{112,128},... | collective-permute-start | bytes 506888 | tf_op jit(solution)/shard_map/ppermute | solution.py:15
  21.4 9.8 %collective-permute-done = bf16[165,512]{1,0:T(8,128)(2,1)S(1)} collective-permute-done((bf16[165,512]{1,0:T(8,128)(2,1)S(1)}, bf16[165,512]{1,0:T(8,128)(2,1)S(1)}, u32[]{:S(2)}, u32[]{:S(2)}) %collective-permute-start) | collective-permute-done | bytes 168992 | tf_op jit(solution)/shard_map/ppermute | solution.py:15
  31.2 0.6 slice_select_fusion.2
  32.6 0.6 fusion.24
  33.2 0.7 slice_select_fusion.1
  34.4 0.4 copy.147
  34.9 0.7 select_select_fusion
  35.7 14.7 %all-to-all-start.1 = ((bf16[4,2,8,512]{3,2,1,0:T(8,128)(2,1)}), bf16[4,2,8,512]{3,2,1,0:T(8,128)(2,1)S(1)}, u32[]{:S(2)}, u32[]{:S(2)}) async-start(bf16[4,2,8,512]{3,2,1,0:T(8,128)(2,1)} %select_select_fusion), calls=%async_computation.1 | async-start | bytes 131072 | tf_op jit(solution)/shard_map/all_to_all | solution.py:98
  50.4 7.5 %fusion.1 = f32[2,128,512]{2,0,1:T(2,128)S(1)} fusion(bf16[1,255,512]{2,0,1:T(2,128)(2,1)S(1)} %copy.147, bf16[1,255,512]{2,0,1:T(2,128)(2,1)S(1)} %copy.146, bf16[128,1,512]{2,0,1:T(8,128)(2,1)S(1)} %bitcast.83), kind=kOutput, calls=%fused_computation.9 | convolution fusion | flops 34598912 | bytes 1177600 | tf_op jit(solution)/shard_map/conv_general_dilated | solution.py:27
  57.9 5.7 %all-to-all-done.1 = bf16[4,2,8,512]{3,2,1,0:T(8,128)(2,1)S(1)} async-done(((bf16[4,2,8,512]{3,2,1,0:T(8,128)(2,1)}), bf16[4,2,8,512]{3,2,1,0:T(8,128)(2,1)S(1)}, u32[]{:S(2)}, u32[]{:S(2)}) %all-to-all-start.1) | async-done | bytes 65568 | tf_op jit(solution)/shard_map/all_to_all | solution.py:98
  63.8 0.6 broadcast_in_dim.103
  64.5 5.2 %all-to-all-start.2 = ((f32[16,2,128,4]{2,3,1,0:T(4,128)}), f32[16,2,128,4]{2,3,1,0:T(4,128)S(1)}, u32[]{:S(2)}, u32[]{:S(2)}) async-start(f32[16,2,128,4]{2,3,1,0:T(4,128)} %broadcast_in_dim.103), calls=%async_computation.2 | async-start | bytes 131072 | tf_op jit(solution)/shard_map/all_to_all | solution.py:21
  69.8 8.1 %all-to-all-done.2 = f32[16,2,128,4]{2,3,1,0:T(4,128)S(1)} async-done(((f32[16,2,128,4]{2,3,1,0:T(4,128)}), f32[16,2,128,4]{2,3,1,0:T(4,128)S(1)}, u32[]{:S(2)}, u32[]{:S(2)}) %all-to-all-start.2) | async-done | bytes 65568 | tf_op jit(solution)/shard_map/all_to_all | solution.py:21
  77.9 1.0 %add_convert_fusion = bf16[2,128,512]{2,1,0:T(8,128)(2,1)} fusion(f32[2,512]{1,0:T(2,128)S(1)} %bitcast.85, f32[2,128]{1,0:T(2,128)S(1)} %bitcast.92, f32[2,512]{1,0:T(2,128)S(1)} %bitcast.86, f32[2,128]{1,0:T(2,128)S(1)} %bitcast.93, f32[2,512]{1,0:T(2,128)S(1)} %bitcast.87, f32[2,128]{1,0:T(2,128)S(1)} %bitcast.94, f32[2,512]{1,0:T(2,128)S(1)} %bitcast.88, ...), kind=kLoop, calls=%fused_computation.7 | loop fusion | flops 1703936 | bytes 1069056 | tf_op jit(solution)/shard_map/convert_element_type | solution.py:124
  (80 shorter events, 4.2 us)
Async XLA Ops:
  2.3 17.0 %all-to-all-start = ((bf16[4,4,8,512]{3,1,2,0:T(4,128)(2,1)}), bf16[4,4,8,512]{3,1,2,0:T(4,128)(2,1)S(1)}, u32[]{:S(2)}, u32[]{:S(2)}) async-start(bf16[4,4,8,512]{3,1,2,0:T(4,128)(2,1)} %convolution_convert_fusion), calls=%async_computation | async-start | bytes 262144 | tf_op jit(solution)/shard_map/all_to_all | solution.py:57
  12.5 1.3 %copy-start.4 = (s32[4]{0:T(128)S(1)}, s32[4]{0:T(128)}, u32[]{:S(2)}) copy-start(s32[4]{0:T(128)} %param.12) | copy-start | bytes 52
  12.5 1.9 %copy-start.3 = (s32[4]{0:T(128)S(1)}, s32[4]{0:T(128)}, u32[]{:S(2)}) copy-start(s32[4]{0:T(128)} %param.13) | copy-start | bytes 52
  13.8 2.2 %copy-start.1 = (bf16[7,512]{1,0:T(8,128)(2,1)S(1)}, bf16[7,512]{1,0:T(8,128)(2,1)}, u32[]{:S(2)}) copy-start(bf16[7,512]{1,0:T(8,128)(2,1)} %param.8) | copy-start | bytes 21508
  13.8 2.3 %copy-start.5 = (pred[8,17]{0,1:T(8,128)(4,1)S(1)}, pred[8,17]{0,1:T(8,128)(4,1)}, u32[]{:S(2)}) copy-start(pred[8,17]{0,1:T(8,128)(4,1)} %constant.87) | copy-start | bytes 412
  16.2 0.9 %copy-start = (bf16[128,512]{1,0:T(8,128)(2,1)S(1)}, bf16[128,512]{1,0:T(8,128)(2,1)}, u32[]{:S(2)}) copy-start(bf16[128,512]{1,0:T(8,128)(2,1)} %param.9) | copy-start | bytes 393220
  16.3 1.7 %copy-start.2 = (f32[64,4]{0,1:T(4,128)S(1)}, f32[64,4]{0,1:T(4,128)}, u32[]{:S(2)}) copy-start(f32[64,4]{0,1:T(4,128)} %param.11) | copy-start | bytes 3076
  19.4 11.8 %collective-permute-start = (bf16[165,512]{1,0:T(8,128)(2,1)S(1)}, bf16[165,512]{1,0:T(8,128)(2,1)S(1)}, u32[]{:S(2)}, u32[]{:S(2)}) collective-permute-start(bf16[165,512]{1,0:T(8,128)(2,1)S(1)} %pad_maximum_fusion), channel_id=1, source_target_pairs={{0,16},{16,32},{32,48},{48,64},{64,80},{80,96},{96,112},{112,128},... | collective-permute-start | bytes 506888 | tf_op jit(solution)/shard_map/ppermute | solution.py:15
  35.7 27.9 %all-to-all-start.1 = ((bf16[4,2,8,512]{3,2,1,0:T(8,128)(2,1)}), bf16[4,2,8,512]{3,2,1,0:T(8,128)(2,1)S(1)}, u32[]{:S(2)}, u32[]{:S(2)}) async-start(bf16[4,2,8,512]{3,2,1,0:T(8,128)(2,1)} %select_select_fusion), calls=%async_computation.1 | async-start | bytes 131072 | tf_op jit(solution)/shard_map/all_to_all | solution.py:98
  64.5 13.4 %all-to-all-start.2 = ((f32[16,2,128,4]{2,3,1,0:T(4,128)}), f32[16,2,128,4]{2,3,1,0:T(4,128)S(1)}, u32[]{:S(2)}, u32[]{:S(2)}) async-start(f32[16,2,128,4]{2,3,1,0:T(4,128)} %broadcast_in_dim.103), calls=%async_computation.2 | async-start | bytes 131072 | tf_op jit(solution)/shard_map/all_to_all | solution.py:21

commit v12 on v10

--- a/solution.py
+++ b/solution.py
@@ -113,7 +113,10 @@
         "tnc,trc->tnr", hidden, tile_rows, preferred_element_type=jnp.float32
     )
     partial = projected[..., rank:] - projected[..., :rank]
-    summed = a2a_sum(partial, "chan")
+    chan_size = lax.axis_size("chan")
+    copies = jnp.broadcast_to(partial.astype(jnp.bfloat16)[None], (chan_size,) + partial.shape)
+    received = lax.all_to_all(copies, "chan", 0, 0, tiled=False)
+    summed = jnp.sum(received.astype(jnp.float32), axis=0)
     bias_tile = jnp.take(jnp.take(edit_bias, seq_tenant, axis=0), seq_of, axis=0)
     coefficient = summed + bias_tile[:, None, :]
     rows_r = tile_rows[:, :rank, :].astype(jnp.float32)

time: 73.7 us -> 73.6 us (level)
    all_to_all x2 -> x1, waiting for transfers between devices: 8.11 us -> 0.01 us  [a2a_sum(): return jnp.sum(lax.all_to_all(copies, axis, 0, 0, tiled=False), axis=0)]
    all_to_all x0 -> x1, waiting for transfers between devices: none -> 7.98 us  [on_device(): received = lax.all_to_all(copies, 'chan', 0, 0, tiled=False)]
    all_to_all x0 -> x1, starting transfers between devices: none -> 5.23 us  [on_device(): received = lax.all_to_all(copies, 'chan', 0, 0, tiled=False)]
    all_to_all x2 -> x1, starting transfers between devices: 14.3 us -> 9.09 us  [a2a_sum(): return jnp.sum(lax.all_to_all(copies, axis, 0, 0, tiled=False), axis=0)]
where the time goes in v12:
time: 73.6 us; the launch traced here: 73.1 us
  starting transfers between devices  31 us (42%)
  waiting for transfers between devices  20 us (27%)
  matrix products  8.23 us (11%)
  other arithmetic  7.54 us (10%)
  local copies, waits for them, and re-layouts  5.94 us (8%)
    all_to_all x1, starting transfers between devices, on_device(): lax.all_to_all(outgoing, 'zh', 0, 0, tiled=False)  14.7 us
    ppermute x1, waiting for transfers between devices, shifted(): lax.ppermute(block, SEQ, [(i, (i + distance) % size) for i in range(size)])  9.79 us
    all_to_all x1, starting transfers between devices, a2a_sum(): return jnp.sum(lax.all_to_all(copies, axis, 0, 0, tiled=False), axis=0)  9.09 us
    all_to_all x1, waiting for transfers between devices, on_device(): received = lax.all_to_all(copies, 'chan', 0, 0, tiled=False)  7.98 us
    conv_general_dilated x3, matrix products, depth_conv(): lax.conv_general_dilated(window, kernel, (1,), 'VALID', dimension_numbers...  7.81 us
    all_to_all x1, starting transfers between devices, on_device(): received = lax.all_to_all(copies, 'chan', 0, 0, tiled=False)  5.23 us
    all_to_all x1, waiting for transfers between devices, on_device(): lax.all_to_all(outgoing, 'zh', 0, 0, tiled=False)  2.2 us
    ppermute x1, starting transfers between devices, shifted(): lax.ppermute(block, SEQ, [(i, (i + distance) % size) for i in range(size)])  1.92 us
  transfers between devices with their start and end apart: 4, of which 3 were waited for; matrix products, arithmetic and copies ran while one was open for 23% of the time, Pallas kernels for 0%

profile of v12, /device:TPU:8, one launch (start us, length us, event | category | flops | bytes accessed | tf_op | source)
XLA Modules:
  0.0 73.1 jit_solution(14301987484691482844)
XLA Ops:
  0.0 0.8 %compare_select_fusion.1 = (s32[4]{0:T(128)S(1)}, s32[4]{0:T(128)S(1)}) fusion(s32[4]{0:T(128)} %param.13, s32[]{:T(128)S(6)} %mul.118), kind=kLoop, calls=%fused_computation.76 | loop fusion | flops 16 | bytes 52 | tf_op jit(solution)/shard_map/jit(_take)/jit(_where)/select_n | solution.py:120
  1.0 0.7 broadcast_in_dim.91
  1.7 9.1 %all-to-all-start = ((bf16[4,4,8,512]{3,2,1,0:T(8,128)(2,1)}), bf16[4,4,8,512]{3,2,1,0:T(8,128)(2,1)S(1)}, u32[]{:S(2)}, u32[]{:S(2)}) async-start(bf16[4,4,8,512]{3,2,1,0:T(8,128)(2,1)} %broadcast_in_dim.91), calls=%async_computation | async-start | bytes 262144 | tf_op jit(solution)/shard_map/all_to_all | solution.py:21
  10.8 1.1 %multiply_convert_fusion = bf16[1,256,512]{2,1,0:T(8,128)(2,1)S(1)} fusion(bf16[5,256,512]{2,1,0:T(8,128)(2,1)} %param.7), kind=kLoop, calls=%fused_computation.8 | loop fusion | flops 524288 | bytes 786432 | tf_op jit(solution)/shard_map/convert_element_type | solution.py:61
  12.1 0.4 copy-done.6
  13.1 0.6 fusion.51
  13.7 0.6 fusion.31
  16.2 0.6 gather_fusion
  16.8 0.6 gather_fusion.1
  17.5 1.9 %collective-permute-start = (bf16[165,512]{1,0:T(8,128)(2,1)S(1)}, bf16[165,512]{1,0:T(8,128)(2,1)S(1)}, u32[]{:S(2)}, u32[]{:S(2)}) collective-permute-start(bf16[165,512]{1,0:T(8,128)(2,1)S(1)} %pad_maximum_fusion), channel_id=1, source_target_pairs={{0,16},{16,32},{32,48},{48,64},{64,80},{80,96},{96,112},{112,128},... | collective-permute-start | bytes 506888 | tf_op jit(solution)/shard_map/ppermute | solution.py:15
  19.5 9.8 %collective-permute-done = bf16[165,512]{1,0:T(8,128)(2,1)S(1)} collective-permute-done((bf16[165,512]{1,0:T(8,128)(2,1)S(1)}, bf16[165,512]{1,0:T(8,128)(2,1)S(1)}, u32[]{:S(2)}, u32[]{:S(2)}) %collective-permute-start) | collective-permute-done | bytes 168992 | tf_op jit(solution)/shard_map/ppermute | solution.py:15
  29.3 0.7 %select_select_fusion = bf16[4,2,8,512]{3,2,1,0:T(8,128)(2,1)} fusion(pred[4,2]{1,0:T(4,128)(4,1)S(1)} %copy.136, pred[4,2]{1,0:T(4,128)(4,1)S(1)} %copy.135, pred[4,2]{1,0:T(4,128)(4,1)S(1)} %copy.134, pred[4,2]{1,0:T(4,128)(4,1)S(1)} %copy.133, bf16[8,512]{1,0:T(8,128)(2,1)S(1)} %get-tuple-element.11, bf16[8,512]{1,0:T(8,128)(2,1)S(1)} %get-tuple-element.12, ...), kind=kLoop, calls=%fused_computation.51 | loop fusion | flops 131072 | bytes 98336 | tf_op jit(solution)/shard_map/jit(_where)/select_n | solution.py:96
  30.0 14.7 %all-to-all-start.1 = ((bf16[4,2,8,512]{3,2,1,0:T(8,128)(2,1)}), bf16[4,2,8,512]{3,2,1,0:T(8,128)(2,1)S(1)}, u32[]{:S(2)}, u32[]{:S(2)}) async-start(bf16[4,2,8,512]{3,2,1,0:T(8,128)(2,1)} %select_select_fusion), calls=%async_computation.1 | async-start | bytes 131072 | tf_op jit(solution)/shard_map/all_to_all | solution.py:97
  44.7 0.6 slice_select_fusion.2
  46.0 0.6 fusion.24
  46.6 0.7 slice_select_fusion.1
  47.4 0.4 copy.129
  47.8 0.4 copy.130
  48.2 7.5 %fusion.1 = f32[2,128,512]{2,0,1:T(2,128)S(1)} fusion(bf16[1,255,512]{2,0,1:T(2,128)(2,1)S(1)} %copy.130, bf16[1,255,512]{2,0,1:T(2,128)(2,1)S(1)} %copy.129, bf16[128,1,512]{2,0,1:T(8,128)(2,1)S(1)} %bitcast.77), kind=kOutput, calls=%fused_computation.9 | convolution fusion | flops 34598912 | bytes 1177600 | tf_op jit(solution)/shard_map/conv_general_dilated | solution.py:27
  55.7 2.2 %all-to-all-done.1 = bf16[4,2,8,512]{3,2,1,0:T(8,128)(2,1)S(1)} async-done(((bf16[4,2,8,512]{3,2,1,0:T(8,128)(2,1)}), bf16[4,2,8,512]{3,2,1,0:T(8,128)(2,1)S(1)}, u32[]{:S(2)}, u32[]{:S(2)}) %all-to-all-start.1) | async-done | bytes 65568 | tf_op jit(solution)/shard_map/all_to_all | solution.py:97
  58.2 0.6 broadcast_in_dim.103
  58.8 5.2 %all-to-all-start.2 = ((bf16[16,2,128,4]{2,3,1,0:T(4,128)(2,1)}), bf16[16,2,128,4]{2,3,1,0:T(4,128)(2,1)S(1)}, u32[]{:S(2)}, u32[]{:S(2)}) async-start(bf16[16,2,128,4]{2,3,1,0:T(4,128)(2,1)} %broadcast_in_dim.103), calls=%async_computation.2 | async-start | bytes 65536 | tf_op jit(solution)/shard_map/all_to_all | solution.py:118
  64.1 8.0 %all-to-all-done.2 = bf16[16,2,128,4]{2,3,1,0:T(4,128)(2,1)S(1)} async-done(((bf16[16,2,128,4]{2,3,1,0:T(4,128)(2,1)}), bf16[16,2,128,4]{2,3,1,0:T(4,128)(2,1)S(1)}, u32[]{:S(2)}, u32[]{:S(2)}) %all-to-all-start.2) | async-done | bytes 32800 | tf_op jit(solution)/shard_map/all_to_all | solution.py:118
  72.2 1.0 %add_convert_fusion = bf16[2,128,512]{2,1,0:T(8,128)(2,1)} fusion(f32[2,512]{1,0:T(2,128)S(1)} %get-tuple-element.30, f32[2,128]{1,0:T(2,128)S(1)} %bitcast.81, f32[2,512]{1,0:T(2,128)S(1)} %get-tuple-element.31, f32[2,128]{1,0:T(2,128)S(1)} %bitcast.82, f32[2,512]{1,0:T(2,128)S(1)} %get-tuple-element.32, f32[2,128]{1,0:T(2,128)S(1)} %bitcast.83, ...), kind=kLoop, calls=%fused_computation.7 | loop fusion | flops 1703936 | bytes 1069056 | tf_op jit(solution)/shard_map/convert_element_type | solution.py:126
  (79 shorter events, 4.0 us)
Async XLA Ops:
  0.0 0.8 %copy-start = (bf16[2,8,512]{2,1,0:T(8,128)(2,1)S(1)}, bf16[2,8,512]{2,1,0:T(8,128)(2,1)}, u32[]{:S(2)}) copy-start(bf16[2,8,512]{2,1,0:T(8,128)(2,1)} %param.10) | copy-start | bytes 49156
  0.0 11.9 %copy-start.1 = (bf16[5,256,512]{2,1,0:T(8,128)(2,1)S(1)}, bf16[5,256,512]{2,1,0:T(8,128)(2,1)}, u32[]{:S(2)}) copy-start(bf16[5,256,512]{2,1,0:T(8,128)(2,1)} %param.7) | copy-start | bytes 3932164
  1.7 15.7 %all-to-all-start = ((bf16[4,4,8,512]{3,2,1,0:T(8,128)(2,1)}), bf16[4,4,8,512]{3,2,1,0:T(8,128)(2,1)S(1)}, u32[]{:S(2)}, u32[]{:S(2)}) async-start(bf16[4,4,8,512]{3,2,1,0:T(8,128)(2,1)} %broadcast_in_dim.91), calls=%async_computation | async-start | bytes 262144 | tf_op jit(solution)/shard_map/all_to_all | solution.py:21
  11.9 0.7 copy-start.6
  11.9 1.2 %copy-start.5 = (s32[4]{0:T(128)S(1)}, s32[4]{0:T(128)}, u32[]{:S(2)}) copy-start(s32[4]{0:T(128)} %param.13) | copy-start | bytes 52
  12.0 2.5 %copy-start.3 = (bf16[7,512]{1,0:T(8,128)(2,1)S(1)}, bf16[7,512]{1,0:T(8,128)(2,1)}, u32[]{:S(2)}) copy-start(bf16[7,512]{1,0:T(8,128)(2,1)} %param.8) | copy-start | bytes 21508
  12.0 2.6 %copy-start.7 = (pred[8,17]{0,1:T(8,128)(4,1)S(1)}, pred[8,17]{0,1:T(8,128)(4,1)}, u32[]{:S(2)}) copy-start(pred[8,17]{0,1:T(8,128)(4,1)} %constant.87) | copy-start | bytes 412
  14.8 1.0 %copy-start.2 = (bf16[128,512]{1,0:T(8,128)(2,1)S(1)}, bf16[128,512]{1,0:T(8,128)(2,1)}, u32[]{:S(2)}) copy-start(bf16[128,512]{1,0:T(8,128)(2,1)} %param.9) | copy-start | bytes 393220
  14.8 1.2 %copy-start.4 = (f32[64,4]{0,1:T(4,128)S(1)}, f32[64,4]{0,1:T(4,128)}, u32[]{:S(2)}) copy-start(f32[64,4]{0,1:T(4,128)} %param.11) | copy-start | bytes 3076
  17.5 11.8 %collective-permute-start = (bf16[165,512]{1,0:T(8,128)(2,1)S(1)}, bf16[165,512]{1,0:T(8,128)(2,1)S(1)}, u32[]{:S(2)}, u32[]{:S(2)}) collective-permute-start(bf16[165,512]{1,0:T(8,128)(2,1)S(1)} %pad_maximum_fusion), channel_id=1, source_target_pairs={{0,16},{16,32},{32,48},{48,64},{64,80},{80,96},{96,112},{112,128},... | collective-permute-start | bytes 506888 | tf_op jit(solution)/shard_map/ppermute | solution.py:15
  30.0 27.9 %all-to-all-start.1 = ((bf16[4,2,8,512]{3,2,1,0:T(8,128)(2,1)}), bf16[4,2,8,512]{3,2,1,0:T(8,128)(2,1)S(1)}, u32[]{:S(2)}, u32[]{:S(2)}) async-start(bf16[4,2,8,512]{3,2,1,0:T(8,128)(2,1)} %select_select_fusion), calls=%async_computation.1 | async-start | bytes 131072 | tf_op jit(solution)/shard_map/all_to_all | solution.py:97
  58.8 13.2 %all-to-all-start.2 = ((bf16[16,2,128,4]{2,3,1,0:T(4,128)(2,1)}), bf16[16,2,128,4]{2,3,1,0:T(4,128)(2,1)S(1)}, u32[]{:S(2)}, u32[]{:S(2)}) async-start(bf16[16,2,128,4]{2,3,1,0:T(4,128)(2,1)} %broadcast_in_dim.103), calls=%async_computation.2 | async-start | bytes 65536 | tf_op jit(solution)/shard_map/all_to_all | solution.py:118

commit v13 on v10

--- a/solution.py
+++ b/solution.py
@@ -109,11 +109,13 @@
 
     rows_per = edit_table.shape[1]
     rank = rows_per // 2
+    chan_size = lax.axis_size("chan")
+    row_copies = jnp.broadcast_to(tile_rows[None], (chan_size,) + tile_rows.shape)
     projected = jnp.einsum(
-        "tnc,trc->tnr", hidden, tile_rows, preferred_element_type=jnp.float32
+        "tnc,ktrc->ktnr", hidden, row_copies, preferred_element_type=jnp.float32
     )
     partial = projected[..., rank:] - projected[..., :rank]
-    summed = a2a_sum(partial, "chan")
+    summed = jnp.sum(lax.all_to_all(partial, "chan", 0, 0, tiled=False), axis=0)
     bias_tile = jnp.take(jnp.take(edit_bias, seq_tenant, axis=0), seq_of, axis=0)
     coefficient = summed + bias_tile[:, None, :]
     rows_r = tile_rows[:, :rank, :].astype(jnp.float32)

time: 73.7 us -> 77.8 us (1.056)
  waiting for transfers between devices: 20.1 us -> 23.6 us
    all_to_all x2 -> x1, waiting for transfers between devices: 8.11 us -> 0.01 us  [a2a_sum(): return jnp.sum(lax.all_to_all(copies, axis, 0, 0, tiled=False), axis=0)]
    all_to_all x0 -> x1, waiting for transfers between devices: none -> 8.09 us  [on_device(): summed = jnp.sum(lax.all_to_all(partial, 'chan', 0, 0, tiled=False), axis=0)]
    all_to_all x2 -> x1, starting transfers between devices: 14.3 us -> 9.09 us  [a2a_sum(): return jnp.sum(lax.all_to_all(copies, axis, 0, 0, tiled=False), axis=0)]
    all_to_all x0 -> x1, starting transfers between devices: none -> 5.23 us  [on_device(): summed = jnp.sum(lax.all_to_all(partial, 'chan', 0, 0, tiled=False), axis=0)]
    all_to_all x1, waiting for transfers between devices: 2.2 us -> 5.71 us  [on_device(): lax.all_to_all(outgoing, 'zh', 0, 0, tiled=False)]
  transfers between devices with their start and end apart: 4 -> 4, of which waited for: 3 -> 3; matrix products, arithmetic and copies ran while one was open for 23% -> 17% of each run, Pallas kernels for 0% -> 0%
where the time goes in v13:
time: 77.8 us; the launch traced here: 77.3 us
  starting transfers between devices  31 us (40%)
  waiting for transfers between devices  23.6 us (30%)
  matrix products  8.26 us (11%)
  other arithmetic  7.56 us (10%)
  local copies, waits for them, and re-layouts  6.47 us (8%)
    all_to_all x1, starting transfers between devices, on_device(): lax.all_to_all(outgoing, 'zh', 0, 0, tiled=False)  14.7 us
    ppermute x1, waiting for transfers between devices, shifted(): lax.ppermute(block, SEQ, [(i, (i + distance) % size) for i in range(size)])  9.79 us
    all_to_all x1, starting transfers between devices, a2a_sum(): return jnp.sum(lax.all_to_all(copies, axis, 0, 0, tiled=False), axis=0)  9.09 us
    all_to_all x1, waiting for transfers between devices, on_device(): summed = jnp.sum(lax.all_to_all(partial, 'chan', 0, 0, tiled=False), axis=0)  8.09 us
    conv_general_dilated x3, matrix products, depth_conv(): lax.conv_general_dilated(window, kernel, (1,), 'VALID', dimension_numbers...  7.8 us
    all_to_all x1, waiting for transfers between devices, on_device(): lax.all_to_all(outgoing, 'zh', 0, 0, tiled=False)  5.71 us
    all_to_all x1, starting transfers between devices, on_device(): summed = jnp.sum(lax.all_to_all(partial, 'chan', 0, 0, tiled=False), axis=0)  5.23 us
    ppermute x1, starting transfers between devices, shifted(): lax.ppermute(block, SEQ, [(i, (i + distance) % size) for i in range(size)])  1.92 us
  transfers between devices with their start and end apart: 4, of which 3 were waited for; matrix products, arithmetic and copies ran while one was open for 17% of the time, Pallas kernels for 0%

profile of v13, /device:TPU:8, one launch (start us, length us, event | category | flops | bytes accessed | tf_op | source)
XLA Modules:
  0.0 77.3 jit_solution(8381924447278720275)
XLA Ops:
  0.0 0.8 compare_select_fusion.1
  1.0 0.7 broadcast_in_dim.91
  1.7 9.1 %all-to-all-start = ((bf16[4,4,8,512]{3,2,1,0:T(8,128)(2,1)}), bf16[4,4,8,512]{3,2,1,0:T(8,128)(2,1)S(1)}, u32[]{:S(2)}, u32[]{:S(2)}) async-start(bf16[4,4,8,512]{3,2,1,0:T(8,128)(2,1)} %broadcast_in_dim.91), calls=%async_computation | async-start | bytes 262144 | tf_op jit(solution)/shard_map/all_to_all | solution.py:21
  10.8 1.1 %multiply_convert_fusion = bf16[1,256,512]{2,1,0:T(8,128)(2,1)S(1)} fusion(bf16[5,256,512]{2,1,0:T(8,128)(2,1)} %param.7), kind=kLoop, calls=%fused_computation.9 | loop fusion | flops 524288 | bytes 786432 | tf_op jit(solution)/shard_map/convert_element_type | solution.py:61
  12.1 0.4 copy-done.6
  13.1 0.6 fusion.51
  13.7 0.6 fusion.33
  15.2 0.5 copy-done.2
  16.7 0.6 gather_fusion
  17.3 0.6 gather_fusion.1
  18.0 1.9 %collective-permute-start = (bf16[165,512]{1,0:T(8,128)(2,1)S(1)}, bf16[165,512]{1,0:T(8,128)(2,1)S(1)}, u32[]{:S(2)}, u32[]{:S(2)}) collective-permute-start(bf16[165,512]{1,0:T(8,128)(2,1)S(1)} %pad_maximum_fusion), channel_id=1, source_target_pairs={{0,16},{16,32},{32,48},{48,64},{64,80},{80,96},{96,112},{112,128},... | collective-permute-start | bytes 506888 | tf_op jit(solution)/shard_map/ppermute | solution.py:15
  20.0 9.8 %collective-permute-done = bf16[165,512]{1,0:T(8,128)(2,1)S(1)} collective-permute-done((bf16[165,512]{1,0:T(8,128)(2,1)S(1)}, bf16[165,512]{1,0:T(8,128)(2,1)S(1)}, u32[]{:S(2)}, u32[]{:S(2)}) %collective-permute-start) | collective-permute-done | bytes 168992 | tf_op jit(solution)/shard_map/ppermute | solution.py:15
  29.8 0.6 slice_select_fusion.2
  31.1 0.6 fusion.25
  31.7 0.7 slice_select_fusion.1
  32.4 0.4 copy.116
  33.3 0.7 select_select_fusion
  34.0 14.7 %all-to-all-start.1 = ((bf16[4,2,8,512]{3,2,1,0:T(8,128)(2,1)}), bf16[4,2,8,512]{3,2,1,0:T(8,128)(2,1)S(1)}, u32[]{:S(2)}, u32[]{:S(2)}) async-start(bf16[4,2,8,512]{3,2,1,0:T(8,128)(2,1)} %select_select_fusion), calls=%async_computation.1 | async-start | bytes 131072 | tf_op jit(solution)/shard_map/all_to_all | solution.py:97
  48.7 7.5 %fusion.1 = f32[2,128,512]{2,0,1:T(2,128)S(1)} fusion(bf16[1,255,512]{2,0,1:T(2,128)(2,1)S(1)} %copy.117, bf16[1,255,512]{2,0,1:T(2,128)(2,1)S(1)} %copy.116, bf16[128,1,512]{2,0,1:T(8,128)(2,1)S(1)} %bitcast.83), kind=kOutput, calls=%fused_computation.10 | convolution fusion | flops 34598912 | bytes 1177600 | tf_op jit(solution)/shard_map/conv_general_dilated | solution.py:27
  56.2 5.7 %all-to-all-done.1 = bf16[4,2,8,512]{3,2,1,0:T(8,128)(2,1)S(1)} async-done(((bf16[4,2,8,512]{3,2,1,0:T(8,128)(2,1)}), bf16[4,2,8,512]{3,2,1,0:T(8,128)(2,1)S(1)}, u32[]{:S(2)}, u32[]{:S(2)}) %all-to-all-start.1) | async-done | bytes 65568 | tf_op jit(solution)/shard_map/all_to_all | solution.py:97
  62.2 0.6 copy.124
  62.9 5.2 %all-to-all-start.2 = ((f32[16,2,128,4]{2,3,1,0:T(4,128)}), f32[16,2,128,4]{2,3,1,0:T(4,128)S(1)}, u32[]{:S(2)}, u32[]{:S(2)}) async-start(f32[16,2,128,4]{2,3,1,0:T(4,128)} %copy.124), calls=%async_computation.2 | async-start | bytes 131072 | tf_op jit(solution)/shard_map/all_to_all | solution.py:118
  68.2 8.1 %all-to-all-done.2 = f32[16,2,128,4]{2,3,1,0:T(4,128)S(1)} async-done(((f32[16,2,128,4]{2,3,1,0:T(4,128)}), f32[16,2,128,4]{2,3,1,0:T(4,128)S(1)}, u32[]{:S(2)}, u32[]{:S(2)}) %all-to-all-start.2) | async-done | bytes 65568 | tf_op jit(solution)/shard_map/all_to_all | solution.py:118
  76.4 1.0 %add_convert_fusion = bf16[2,128,512]{2,1,0:T(8,128)(2,1)} fusion(f32[2,512]{1,0:T(2,128)S(1)} %get-tuple-element.30, f32[2,128]{1,0:T(2,128)S(1)} %bitcast.87, f32[2,512]{1,0:T(2,128)S(1)} %get-tuple-element.31, f32[2,128]{1,0:T(2,128)S(1)} %bitcast.88, f32[2,512]{1,0:T(2,128)S(1)} %get-tuple-element.32, f32[2,128]{1,0:T(2,128)S(1)} %bitcast.89, ...), kind=kLoop, calls=%fused_computation.8 | loop fusion | flops 1703936 | bytes 1069056 | tf_op jit(solution)/shard_map/convert_element_type | solution.py:125
  (79 shorter events, 4.5 us)
Async XLA Ops:
  0.0 0.8 copy-start
  0.0 11.9 %copy-start.1 = (bf16[5,256,512]{2,1,0:T(8,128)(2,1)S(1)}, bf16[5,256,512]{2,1,0:T(8,128)(2,1)}, u32[]{:S(2)}) copy-start(bf16[5,256,512]{2,1,0:T(8,128)(2,1)} %param.7) | copy-start | bytes 3932164
  1.7 16.2 %all-to-all-start = ((bf16[4,4,8,512]{3,2,1,0:T(8,128)(2,1)}), bf16[4,4,8,512]{3,2,1,0:T(8,128)(2,1)S(1)}, u32[]{:S(2)}, u32[]{:S(2)}) async-start(bf16[4,4,8,512]{3,2,1,0:T(8,128)(2,1)} %broadcast_in_dim.91), calls=%async_computation | async-start | bytes 262144 | tf_op jit(solution)/shard_map/all_to_all | solution.py:21
  11.9 0.7 copy-start.6
  11.9 1.2 %copy-start.5 = (s32[4]{0:T(128)S(1)}, s32[4]{0:T(128)}, u32[]{:S(2)}) copy-start(s32[4]{0:T(128)} %param.13) | copy-start | bytes 52
  12.0 2.5 %copy-start.3 = (bf16[7,512]{1,0:T(8,128)(2,1)S(1)}, bf16[7,512]{1,0:T(8,128)(2,1)}, u32[]{:S(2)}) copy-start(bf16[7,512]{1,0:T(8,128)(2,1)} %param.8) | copy-start | bytes 21508
  12.0 2.6 %copy-start.7 = (pred[8,17]{0,1:T(8,128)(4,1)S(1)}, pred[8,17]{0,1:T(8,128)(4,1)}, u32[]{:S(2)}) copy-start(pred[8,17]{0,1:T(8,128)(4,1)} %constant.87) | copy-start | bytes 412
  14.8 0.9 %copy-start.2 = (bf16[128,512]{1,0:T(8,128)(2,1)S(1)}, bf16[128,512]{1,0:T(8,128)(2,1)}, u32[]{:S(2)}) copy-start(bf16[128,512]{1,0:T(8,128)(2,1)} %param.9) | copy-start | bytes 393220
  14.8 1.7 %copy-start.4 = (f32[64,4]{0,1:T(4,128)S(1)}, f32[64,4]{0,1:T(4,128)}, u32[]{:S(2)}) copy-start(f32[64,4]{0,1:T(4,128)} %param.11) | copy-start | bytes 3076
  18.0 11.8 %collective-permute-start = (bf16[165,512]{1,0:T(8,128)(2,1)S(1)}, bf16[165,512]{1,0:T(8,128)(2,1)S(1)}, u32[]{:S(2)}, u32[]{:S(2)}) collective-permute-start(bf16[165,512]{1,0:T(8,128)(2,1)S(1)} %pad_maximum_fusion), channel_id=1, source_target_pairs={{0,16},{16,32},{32,48},{48,64},{64,80},{80,96},{96,112},{112,128},... | collective-permute-start | bytes 506888 | tf_op jit(solution)/shard_map/ppermute | solution.py:15
  34.0 27.9 %all-to-all-start.1 = ((bf16[4,2,8,512]{3,2,1,0:T(8,128)(2,1)}), bf16[4,2,8,512]{3,2,1,0:T(8,128)(2,1)S(1)}, u32[]{:S(2)}, u32[]{:S(2)}) async-start(bf16[4,2,8,512]{3,2,1,0:T(8,128)(2,1)} %select_select_fusion), calls=%async_computation.1 | async-start | bytes 131072 | tf_op jit(solution)/shard_map/all_to_all | solution.py:97
  62.9 13.4 %all-to-all-start.2 = ((f32[16,2,128,4]{2,3,1,0:T(4,128)}), f32[16,2,128,4]{2,3,1,0:T(4,128)S(1)}, u32[]{:S(2)}, u32[]{:S(2)}) async-start(f32[16,2,128,4]{2,3,1,0:T(4,128)} %copy.124), calls=%async_computation.2 | async-start | bytes 131072 | tf_op jit(solution)/shard_map/all_to_all | solution.py:118
